TPU v7x, 512 devices: a whole 4x4x16 slice. The times are simulated.
512 devices in a mesh: aux: 16 (over z), pair: 32 (over y, x, core).
Axes of the slice: x: 4, y: 4, z: 16, core: 2. Of those that a mesh axis runs over, the one named last changes fastest.
Arguments:
- b_tensor: bfloat16 [2560, 262144], P('aux', 'pair'), may hold values from -0.0625 to 0.0625
- eps_occ: float32 [256], replicated, may hold values from -1 to -0.3
- eps_vir: float32 [1024], replicated, may hold values from 0.05 to 3
- trial: bfloat16 [32, 262144], P(None, 'pair'), may hold values from -6 to 6
Outputs:
- trial_next: float32 [32, 262144], P(None, 'pair')
- residual: bfloat16 [32, 262144], P(None, 'pair')
- subspace: float32 [32, 32], replicated
All inputs are finite; a program needn't handle non-finite values.
Results may differ from a plain program's by a relative error of at most 0.028.
Values may be sent and summed in bfloat16 or wider, within the bound.
No kernel may reach another device: no remote copies, remote signals or barrier semaphores. Data moves between devices by JAX's collectives and lax.ppermute only.
A program may use at most 64 MiB of HBM per device.

v0:
```python
import jax
import jax.numpy as jnp
from jax import lax
from jax.sharding import PartitionSpec as P

ITERS = 2


HIGHEST_PRECISION = lax.Precision.HIGHEST


def correlation_of(first_rows, second_rows):
    return lax.dot_general(
        first_rows,
        second_rows,
        (((1,), (1,)), ((), ())),
        precision=HIGHEST_PRECISION,
        preferred_element_type=jnp.float32,
    )


def product(first_mat, second_mat):
    return jnp.dot(
        first_mat, second_mat, precision=HIGHEST_PRECISION, preferred_element_type=jnp.float32
    )


def global_sum(matrices):
    return lax.psum(matrices, "pair")


def orthonormal(trial_now, gram_now):
    lower_tri = jnp.linalg.cholesky(gram_now)
    inverse = lax.linalg.triangular_solve(
        lower_tri, jnp.eye(gram_now.shape[0], dtype=jnp.float32), left_side=True, lower=True
    )
    return product(inverse, trial_now)


def coupling_of(b_tensor, basis_now):
    basis_low = basis_now.astype(jnp.bfloat16)
    partial_proj = lax.dot_general(
        b_tensor, basis_low, (((1,), (1,)), ((), ())), preferred_element_type=jnp.float32
    )
    projected_low = lax.psum(partial_proj, "pair").astype(jnp.bfloat16)
    partial_value = lax.dot_general(
        projected_low, b_tensor, (((0,), (0,)), ((), ())), preferred_element_type=jnp.float32
    )
    return lax.psum(partial_value.astype(jnp.bfloat16), "aux").astype(jnp.float32)


def on_device(b_tensor, eps_occ, eps_vir, trial):
    block_cols = b_tensor.shape[1]
    npair_all = eps_occ.shape[0] * eps_vir.shape[0]
    everything = (eps_vir[None, :] - eps_occ[:, None]).reshape(npair_all)
    diagonal = lax.dynamic_slice_in_dim(everything, lax.axis_index("pair") * block_cols, block_cols)
    trial_now = trial.astype(jnp.float32)
    diag_row = diagonal[None, :]
    for iteration in range(ITERS):
        gram_now = global_sum(correlation_of(trial_now, trial_now) / npair_all)
        basis_now = orthonormal(trial_now, gram_now)
        image_now = coupling_of(b_tensor, basis_now) + diag_row * basis_now
        subspace = global_sum(correlation_of(image_now, basis_now) / npair_all)
        residual = image_now - product(subspace, basis_now)
        trial_now = basis_now - residual / diag_row
    return (trial_now, residual.astype(jnp.bfloat16), subspace)


def solution(mesh):
    in_specs = (P("aux", "pair"), P(), P(), P(None, "pair"))
    out_specs = (P(None, "pair"), P(None, "pair"), P())
    return jax.shard_map(
        on_device, mesh=mesh, in_specs=in_specs, out_specs=out_specs, check_vma=False
    )
```

profile of v0, /device:TPU:32, one launch (start us, length us, event | category | flops | bytes accessed | tf_op | source)
XLA Modules:
  0.0 1066.8 jit_solution(1206010079620472459)
XLA Ops:
  7.2 1.6 convolution_multiply_fusion.3
  8.8 128.4 %psum.56 = f32[32,32]{0,1:T(8,128)S(1)} all-reduce(f32[32,32]{0,1:T(8,128)S(1)} %convolution_multiply_fusion.3), channel_id=1, replica_groups=mesh['aux'=16,'pair'=32] {'pair'}, use_global_device_ids=true, to_apply=%region_0.0 | all-reduce | flops 1024 | bytes 8192 | tf_op jit(solution)/shard_map/psum | solution.py:29
  137.3 2.9 cholesky.44
  141.6 2.4 custom-call.6
  144.2 1.6 fusion.23
  145.9 1.0 copy-done.1
  147.8 123.9 %psum.57 = bf16[160,32]{0,1:T(8,128)(2,1)S(1)} all-reduce(f32[160,32]{0,1:T(8,128)S(1)} %convolution_bitcast_fusion.1), channel_id=1, replica_groups=mesh['aux'=16,'pair'=32] {'pair'}, use_global_device_ids=true, to_apply=%region_3.6 | all-reduce | flops 5120 | bytes 30720 | tf_op jit(solution)/shard_map/psum | solution.py:45
  271.7 1.3 convolution_convert_fusion.1
  273.3 1.2 copy.16
  275.2 133.4 %all-reduce.3.cloned.1.call-done = bf16[32,8192]{1,0:T(8,128)(2,1)} async-done(((bf16[32,8192]{1,0:T(8,128)(2,1)}), bf16[32,8192]{1,0:T(8,128)(2,1)}) %all-reduce.3.cloned.1.call-update) | async-done | bytes 524304 | tf_op jit(solution)/shard_map/psum | solution.py:49
  408.6 2.9 convolution_multiply_fusion.2
  411.5 123.8 %psum.59 = f32[32,32]{0,1:T(8,128)S(1)} all-reduce(f32[32,32]{0,1:T(8,128)S(1)} %convolution_multiply_fusion.2), channel_id=1, replica_groups=mesh['aux'=16,'pair'=32] {'pair'}, use_global_device_ids=true, to_apply=%region_5.8 | all-reduce | flops 1024 | bytes 8192 | tf_op jit(solution)/shard_map/psum | solution.py:29
  535.3 2.8 fusion.1
  540.0 123.8 %psum.60 = f32[32,32]{0,1:T(8,128)S(1)} all-reduce(f32[32,32]{0,1:T(8,128)S(1)} %convolution_multiply_fusion.1), channel_id=1, replica_groups=mesh['aux'=16,'pair'=32] {'pair'}, use_global_device_ids=true, to_apply=%region_6.9 | all-reduce | flops 1024 | bytes 8192 | tf_op jit(solution)/shard_map/psum | solution.py:29
  663.9 2.9 cholesky.55
  668.1 2.4 custom-call.7
  670.8 2.2 fusion.24
  673.0 1.0 copy-done.2
  675.0 123.8 %psum.61 = bf16[160,32]{0,1:T(8,128)(2,1)S(1)} all-reduce(f32[160,32]{0,1:T(8,128)S(1)} %convolution_bitcast_fusion), channel_id=1, replica_groups=mesh['aux'=16,'pair'=32] {'pair'}, use_global_device_ids=true, to_apply=%region_7.10 | all-reduce | flops 5120 | bytes 30720 | tf_op jit(solution)/shard_map/psum | solution.py:45
  798.7 1.3 convolution_convert_fusion
  800.1 128.7 %all-reduce.5.cloned.1.call-done = bf16[32,8192]{1,0:T(8,128)(2,1)} async-done(((bf16[32,8192]{1,0:T(8,128)(2,1)}), bf16[32,8192]{1,0:T(8,128)(2,1)}) %all-reduce.5.cloned.1.call-update) | async-done | bytes 524304 | tf_op jit(solution)/shard_map/psum | solution.py:49
  928.9 2.8 convolution_multiply_fusion
  931.7 123.8 %psum.63 = f32[32,32]{0,1:T(8,128)S(1)} all-reduce(f32[32,32]{0,1:T(8,128)S(1)} %convolution_multiply_fusion), channel_id=1, replica_groups=mesh['aux'=16,'pair'=32] {'pair'}, use_global_device_ids=true, to_apply=%region_9.12 | all-reduce | flops 1024 | bytes 8192 | tf_op jit(solution)/shard_map/psum | solution.py:29
  1056.1 3.9 fusion.22
  (36 shorter events, 8.8 us)
Async XLA Ops:
  7.2 139.7 %copy-start = (bf16[160,8192]{1,0:T(8,128)(2,1)S(1)}, bf16[160,8192]{1,0:T(8,128)(2,1)}, u32[]{:S(2)}) copy-start(bf16[160,8192]{1,0:T(8,128)(2,1)} %param.7) | copy-start | bytes 7864324
  7.2 401.5 %all-reduce.3.cloned.1.call-start = ((), (), s32[]{:S(2)}) async-start(), calls=%async_computation | async-start | bytes 1048576 | tf_op jit(solution)/shard_map/psum | solution.py:49
  145.9 1.0 copy-start.1
  147.8 125.4 %copy-start.6 = (f32[1024]{0:T(1024)S(1)}, f32[1024]{0:T(1024)}, u32[]{:S(2)}) copy-start(f32[1024]{0:T(1024)} %param.9) | copy-start | bytes 12292
  147.8 125.3 %copy-start.7 = (f32[256]{0:T(256)S(1)}, f32[256]{0:T(256)}, u32[]{:S(2)}) copy-start(f32[256]{0:T(256)} %param.8) | copy-start | bytes 3076
  273.1 655.8 %all-reduce.5.cloned.1.call-start = ((), (), s32[]{:S(2)}) async-start(), calls=%async_computation.1 | async-start | bytes 1048576 | tf_op jit(solution)/shard_map/psum | solution.py:49
  408.6 126.7 %copy-start.4 = (bf16[32,8192]{1,0:T(8,128)(2,1)S(1)}, bf16[32,8192]{1,0:T(8,128)(2,1)}, u32[]{:S(2)}) copy-start(bf16[32,8192]{1,0:T(8,128)(2,1)} %all-reduce.3.cloned.1.call-done) | copy-start | bytes 1572868
  538.1 1.0 copy-start.3
  673.0 1.0 copy-start.2
  928.9 127.3 %copy-start.5 = (bf16[32,8192]{1,0:T(8,128)(2,1)S(1)}, bf16[32,8192]{1,0:T(8,128)(2,1)}, u32[]{:S(2)}) copy-start(bf16[32,8192]{1,0:T(8,128)(2,1)} %all-reduce.5.cloned.1.call-done) | copy-start | bytes 1572868
Sparse Core Ops, SparseCore 0:
  273.2 135.3 all-reduce.2
  800.2 128.5 all-reduce.4
where the time goes:
time: 1070 us
  blocking collectives  747 us (70%)
  waiting for transfers between devices  262 us (24%)
  matrix products  23.8 us (2%)
  between operations  14.2 us (1%)
  other arithmetic  13.5 us (1%)
    psum x4, blocking collectives, global_sum(): return lax.psum(matrices, 'pair')  500 us
    psum x2, waiting for transfers between devices, coupling_of(): lax.psum(partial_value.astype(jnp.bfloat16), 'aux').astype(jnp.float32)  262 us
    psum x2, blocking collectives, coupling_of(): projected_low = lax.psum(partial_proj, 'pair').astype(jnp.bfloat16)  248 us
  transfers between devices with their start and end apart: 2, of which 2 were waited for; matrix products, arithmetic and copies ran while one was open for 0% of the time, Pallas kernels for 0%

commit v1 on v0

v1 whole, which is shorter than its diff:
```python
import jax
import jax.numpy as jnp
from jax import lax
from jax.sharding import PartitionSpec as P

ITERS = 2


HIGHEST_PRECISION = lax.Precision.HIGHEST


def correlation_of(first_rows, second_rows, precision=HIGHEST_PRECISION):
    return lax.dot_general(
        first_rows,
        second_rows,
        (((1,), (1,)), ((), ())),
        precision=precision,
        preferred_element_type=jnp.float32,
    )


def product(first_mat, second_mat):
    return jnp.dot(
        first_mat, second_mat, precision=HIGHEST_PRECISION, preferred_element_type=jnp.float32
    )


def pair_sum(matrices):
    return lax.all_gather(matrices, "pair").sum(0)


def aux_sum(terms):
    n_aux = lax.axis_size("aux")
    rows, cols = terms.shape
    pieces = terms.reshape(rows, n_aux, cols // n_aux)
    pieces = lax.all_to_all(pieces, "aux", 1, 1, tiled=True)
    mine = pieces.astype(jnp.float32).sum(1)
    return lax.all_gather(mine, "aux", axis=1, tiled=True)


def inverse_factor(gram_now):
    lower_tri = jnp.linalg.cholesky(gram_now)
    return lax.linalg.triangular_solve(
        lower_tri, jnp.eye(gram_now.shape[0], dtype=jnp.float32), left_side=True, lower=True
    )


def on_device(b_tensor, eps_occ, eps_vir, trial):
    block_cols = b_tensor.shape[1]
    npair_all = eps_occ.shape[0] * eps_vir.shape[0]
    k = trial.shape[0]
    everything = (eps_vir[None, :] - eps_occ[:, None]).reshape(npair_all)
    diagonal = lax.dynamic_slice_in_dim(everything, lax.axis_index("pair") * block_cols, block_cols)
    diag_row = diagonal[None, :]
    trial_now = trial
    for iteration in range(ITERS):
        if iteration == 0:
            gram_part = correlation_of(trial_now, trial_now, None)
            cross_part = correlation_of(b_tensor, trial_now, None)
        else:
            gram_part = correlation_of(trial_now, trial_now)
            cross_part = correlation_of(b_tensor.astype(jnp.float32), trial_now)
        summed = pair_sum(jnp.concatenate([gram_part / npair_all, cross_part], axis=0))
        inverse = inverse_factor(summed[:k])
        basis_now = product(inverse, trial_now.astype(jnp.float32))
        projected = lax.dot_general(
            summed[k:], inverse, (((1,), (1,)), ((), ())),
            precision=HIGHEST_PRECISION, preferred_element_type=jnp.float32,
        )
        projected_low = projected.astype(jnp.bfloat16)
        term = lax.dot_general(
            projected_low, b_tensor, (((0,), (0,)), ((), ())), preferred_element_type=jnp.float32
        ).astype(jnp.bfloat16)
        image_now = aux_sum(term) + diag_row * basis_now
        subspace = pair_sum(correlation_of(image_now, basis_now) / npair_all)
        residual = image_now - product(subspace, basis_now)
        trial_now = basis_now - residual / diag_row
    return (trial_now, residual.astype(jnp.bfloat16), subspace)


def solution(mesh):
    in_specs = (P("aux", "pair"), P(), P(), P(None, "pair"))
    out_specs = (P(None, "pair"), P(None, "pair"), P())
    return jax.shard_map(
        on_device, mesh=mesh, in_specs=in_specs, out_specs=out_specs, check_vma=False
    )
```

time: 1070 us -> 372 us (0.35)
  the two profiles are of different devices: /device:TPU:32 before, /device:TPU:1 now
where the time goes in v1:
time: 372 us; the launch traced here: 371 us
  blocking collectives  193 us (52%)
  waiting for transfers between devices  115 us (31%)
  matrix products  27.3 us (7%)
  other arithmetic  17.8 us (5%)
  between operations  14.3 us (4%)
    all_gather x4, blocking collectives, pair_sum(): return lax.all_gather(matrices, 'pair').sum(0)  128 us
    all_gather x2, waiting for transfers between devices, aux_sum(): return lax.all_gather(mine, 'aux', axis=1, tiled=True)  115 us
    all_to_all x2, blocking collectives, aux_sum(): pieces = lax.all_to_all(pieces, 'aux', 1, 1, tiled=True)  65.7 us
    dot_general x6, matrix products, correlation_of(): lax.dot_general(first_rows, second_rows, (((1,), (1,)), ((), ())), precis...  12.8 us
    dot_general x4, matrix products, product(): jnp.dot(first_mat, second_mat, precision=HIGHEST_PRECISION, preferred_ele...  12 us
  transfers between devices with their start and end apart: 2, of which 2 were waited for; matrix products, arithmetic and copies ran while one was open for 2% of the time, Pallas kernels for 0%

profile of v1, /device:TPU:1, one launch (start us, length us, event | category | flops | bytes accessed | tf_op | source)
XLA Modules:
  0.0 371.0 jit_solution(16617916019839826232)
XLA Ops:
  7.2 1.6 convolution_multiply_fusion.3
  9.2 2.0 fusion.19
  11.3 31.4 %all-gather.4 = f32[32,192,32]{1,2,0:T(8,128)} all-gather(f32[1,192,32]{1,2,0:T(8,128)S(1)} %maximum_bitcast_fusion), channel_id=2, replica_groups=mesh['aux'=16,'pair'=32] {'pair'}, dimensions={0}, use_global_device_ids=true | all-gather | bytes 811008 | tf_op jit(solution)/shard_map/all_gather | solution.py:29
  42.7 1.3 reduce_sum.54
  44.1 2.9 cholesky.44
  48.4 2.4 custom-call.6
  52.2 35.2 %all_to_all.10 = bf16[32,16,512]{2,0,1:T(8,128)(2,1)S(1)} all-to-all(bf16[32,16,512]{2,0,1:T(8,128)(2,1)S(1)} %bitcast.64), channel_id=1, replica_groups=mesh['aux'=16,'pair'=32] {'aux'}, dimensions={1} | all-to-all | bytes 1048576 | tf_op jit(solution)/shard_map/all_to_all | solution.py:36
  88.3 1.2 copy.28
  90.3 1.5 fusion.20
  91.8 57.8 %all-gather.9.cloned.1.call-done = f32[32,8192]{1,0:T(8,128)} async-done(((f32[32,512]{1,0:T(8,128)}), f32[32,8192]{1,0:T(8,128)}) %all-gather.9.cloned.1.call-update) | async-done | bytes 1048592 | tf_op jit(solution)/shard_map/all_gather | solution.py:38
  149.6 2.9 convolution_multiply_fusion.2
  152.6 34.8 %all-gather.1 = f32[1024,32]{1,0:T(8,128)S(1)} all-gather(f32[32,32]{1,0:T(8,128)S(1)} %copy.14), channel_id=3, replica_groups=mesh['aux'=16,'pair'=32] {'pair'}, dimensions={0}, use_global_device_ids=true | all-gather | bytes 135168 | tf_op jit(solution)/shard_map/all_gather | solution.py:29
  187.4 3.0 fusion.1
  190.5 2.4 convolution_bitcast_fusion
  194.0 26.7 %all-gather.5 = f32[32,192,32]{1,2,0:T(8,128)} all-gather(f32[1,192,32]{1,2,0:T(8,128)S(1)} %maximum_bitcast_fusion.1), channel_id=4, replica_groups=mesh['aux'=16,'pair'=32] {'pair'}, dimensions={0}, use_global_device_ids=true | all-gather | bytes 811008 | tf_op jit(solution)/shard_map/all_gather | solution.py:29
  220.7 1.3 reduce_sum.57
  222.1 2.9 cholesky.55
  226.3 2.4 custom-call.7
  230.1 30.5 %all_to_all.11 = bf16[32,16,512]{2,0,1:T(8,128)(2,1)S(1)} all-to-all(bf16[32,16,512]{2,0,1:T(8,128)(2,1)S(1)} %bitcast.66), channel_id=1, replica_groups=mesh['aux'=16,'pair'=32] {'aux'}, dimensions={1} | all-to-all | bytes 1048576 | tf_op jit(solution)/shard_map/all_to_all | solution.py:36
  261.3 3.2 fusion.21
  264.5 57.6 %all-gather.11.cloned.1.call-done = f32[32,8192]{1,0:T(8,128)} async-done(((f32[32,512]{1,0:T(8,128)}), f32[32,8192]{1,0:T(8,128)}) %all-gather.11.cloned.1.call-update) | async-done | bytes 1048592 | tf_op jit(solution)/shard_map/all_gather | solution.py:38
  322.1 2.9 convolution_multiply_fusion
  325.1 34.8 %all-gather.3 = f32[1024,32]{1,0:T(8,128)S(1)} all-gather(f32[32,32]{1,0:T(8,128)S(1)} %copy.19), channel_id=5, replica_groups=mesh['aux'=16,'pair'=32] {'pair'}, dimensions={0}, use_global_device_ids=true | all-gather | bytes 135168 | tf_op jit(solution)/shard_map/all_gather | solution.py:29
  360.0 4.2 %fusion.18 = (bf16[32,8192]{1,0:T(8,128)(2,1)}, f32[32,8192]{1,0:T(8,128)}) fusion(f32[32,8192]{1,0:T(8,128)} %fusion.21, f32[8192]{0:T(1024)S(1)} %dynamic_slice.3, f32[32,32]{1,0:T(8,128)S(1)} %reduce_sum.59, f32[32,8192]{1,0:T(8,128)} %all-gather.11.cloned.1.call-done), kind=kOutput, calls=%fused_computation.48 | convolution fusion | flops 102236160 | bytes 3706880 | tf_op jit(solution)/shard_map/dot_general | solution.py:23
  (47 shorter events, 9.6 us)
Async XLA Ops:
  7.2 2.1 copy-start
  7.2 142.5 %all-gather.9.cloned.1.call-start = ((), (), s32[]{:S(2)}) async-start(), calls=%async_computation.2 | async-start | bytes 1114112 | tf_op jit(solution)/shard_map/all_gather | solution.py:38
  51.4 36.7 %copy-start.4 = (f32[1024]{0:T(1024)S(1)}, f32[1024]{0:T(1024)}, u32[]{:S(2)}) copy-start(f32[1024]{0:T(1024)} %param.9) | copy-start | bytes 12292
  51.4 36.7 %copy-start.5 = (f32[256]{0:T(256)S(1)}, f32[256]{0:T(256)}, u32[]{:S(2)}) copy-start(f32[256]{0:T(256)} %param.8) | copy-start | bytes 3076
  52.2 38.1 %copy-start.2 = (bf16[32,8192]{1,0:T(8,128)(2,1)S(1)}, bf16[32,8192]{1,0:T(8,128)(2,1)}, u32[]{:S(2)}) copy-start(bf16[32,8192]{1,0:T(8,128)(2,1)} %param.10) | copy-start | bytes 1572868
  88.1 234.0 %all-gather.11.cloned.1.call-start = ((), (), s32[]{:S(2)}) async-start(), calls=%async_computation.3 | async-start | bytes 1114112 | tf_op jit(solution)/shard_map/all_gather | solution.py:38
  190.5 3.4 copy-start.1
  359.9 4.2 %copy-start.3 = (f32[32,32]{1,0:T(8,128)}, f32[32,32]{1,0:T(8,128)S(1)}, u32[]{:S(2)}) copy-start(f32[32,32]{1,0:T(8,128)S(1)} %reduce_sum.59) | copy-start | bytes 12292
Sparse Core Ops, SparseCore 0:
  88.2 61.3 all-gather.8
  261.4 60.6 all-gather.10

commit v2 on v1

--- a/solution.py
+++ b/solution.py
@@ -34,8 +34,8 @@
     rows, cols = terms.shape
     pieces = terms.reshape(rows, n_aux, cols // n_aux)
     pieces = lax.all_to_all(pieces, "aux", 1, 1, tiled=True)
-    mine = pieces.astype(jnp.float32).sum(1)
-    return lax.all_gather(mine, "aux", axis=1, tiled=True)
+    mine = pieces.astype(jnp.float32).sum(1).astype(jnp.bfloat16)
+    return lax.all_gather(mine, "aux", axis=1, tiled=True).astype(jnp.float32)
 
 
 def inverse_factor(gram_now):
@@ -54,25 +54,32 @@
     diag_row = diagonal[None, :]
     trial_now = trial
     for iteration in range(ITERS):
-        if iteration == 0:
-            gram_part = correlation_of(trial_now, trial_now, None)
-            cross_part = correlation_of(b_tensor, trial_now, None)
-        else:
-            gram_part = correlation_of(trial_now, trial_now)
-            cross_part = correlation_of(b_tensor.astype(jnp.float32), trial_now)
-        summed = pair_sum(jnp.concatenate([gram_part / npair_all, cross_part], axis=0))
+        precision = None if iteration == 0 else HIGHEST_PRECISION
+        wide_trial = trial_now.astype(jnp.float32)
+        gram_part = correlation_of(trial_now, trial_now, precision)
+        weighted_part = correlation_of(wide_trial * diag_row, wide_trial)
+        cross_part = correlation_of(b_tensor.astype(wide_trial.dtype) if precision else b_tensor,
+                                    trial_now, precision)
+        summed = pair_sum(jnp.concatenate(
+            [gram_part / npair_all, weighted_part / npair_all, cross_part], axis=0))
         inverse = inverse_factor(summed[:k])
-        basis_now = product(inverse, trial_now.astype(jnp.float32))
+        basis_now = product(inverse, wide_trial)
         projected = lax.dot_general(
-            summed[k:], inverse, (((1,), (1,)), ((), ())),
+            summed[2 * k:], inverse, (((1,), (1,)), ((), ())),
             precision=HIGHEST_PRECISION, preferred_element_type=jnp.float32,
         )
+        group_part = lax.dot_general(
+            projected, projected, (((0,), (0,)), ((), ())),
+            precision=HIGHEST_PRECISION, preferred_element_type=jnp.float32,
+        )
+        group_sum = lax.all_gather(group_part / npair_all, "aux").sum(0)
+        diag_part = product(product(inverse, summed[k:2 * k]), inverse.T)
+        subspace = group_sum + diag_part
         projected_low = projected.astype(jnp.bfloat16)
         term = lax.dot_general(
             projected_low, b_tensor, (((0,), (0,)), ((), ())), preferred_element_type=jnp.float32
         ).astype(jnp.bfloat16)
         image_now = aux_sum(term) + diag_row * basis_now
-        subspace = pair_sum(correlation_of(image_now, basis_now) / npair_all)
         residual = image_now - product(subspace, basis_now)
         trial_now = basis_now - residual / diag_row
     return (trial_now, residual.astype(jnp.bfloat16), subspace)

time: 372 us -> 285 us (0.77)
  the two profiles are of different devices: /device:TPU:1 before, /device:TPU:32 now
where the time goes in v2:
time: 285 us; the launch traced here: 284 us
  blocking collectives  212 us (74%)
  starting transfers between devices  25.8 us (9%)
  matrix products  23.1 us (8%)
  other arithmetic  17.5 us (6%)
  local copies, waits for them, and re-layouts  4.45 us (2%)
    all_gather x2, blocking collectives, on_device(): group_sum = lax.all_gather(group_part / npair_all, 'aux').sum(0)  96.6 us
    all_gather x2, blocking collectives, aux_sum(): return lax.all_gather(mine, 'aux', axis=1, tiled=True).astype(jnp.float32)  61.6 us
    all_gather x2, blocking collectives, pair_sum(): return lax.all_gather(matrices, 'pair').sum(0)  54.2 us
    all_to_all x2, starting transfers between devices, aux_sum(): pieces = lax.all_to_all(pieces, 'aux', 1, 1, tiled=True)  25.8 us
    dot_general x8, matrix products, product(): jnp.dot(first_mat, second_mat, precision=HIGHEST_PRECISION, preferred_ele...  12.1 us
    dot_general x6, matrix products, correlation_of(): lax.dot_general(first_rows, second_rows, (((1,), (1,)), ((), ())), precis...  8.78 us
    another operation x6, other arithmetic, inverse_factor(): lower_tri = jnp.linalg.cholesky(gram_now)  7.19 us
    another operation x4, other arithmetic, inverse_factor(): lax.linalg.triangular_solve(lower_tri, jnp.eye(gram_now.shape[0], dtype=j...  6.17 us
  transfers between devices with their start and end apart: 2, of which 0 were waited for; matrix products, arithmetic and copies ran while one was open for 2% of the time, Pallas kernels for 0%

profile of v2, /device:TPU:32, one launch (start us, length us, event | category | flops | bytes accessed | tf_op | source)
XLA Modules:
  0.0 284.3 jit_solution(4177780045437399140)
XLA Ops:
  0.7 1.6 convolution_multiply_fusion.4
  2.7 2.0 fusion.34
  4.9 1.2 copy.28
  7.6 27.5 %all-gather.4 = f32[32,224,32]{1,2,0:T(8,128)} all-gather(f32[1,224,32]{1,2,0:T(8,128)S(1)} %maximum_bitcast_fusion), channel_id=2, replica_groups=mesh['aux'=16,'pair'=32] {'pair'}, dimensions={0}, use_global_device_ids=true | all-gather | bytes 946176 | tf_op jit(solution)/shard_map/all_gather | solution.py:29
  35.1 1.3 reduce_sum.60
  36.5 2.9 %cholesky.44 = f32[32,32]{1,0:T(8,128)S(1)} custom-call(f32[32,32]{1,0:T(8,128)S(1)} %fusion.28), custom_call_target="Cholesky" | custom-call | tf_op jit(solution)/shard_map/jit(cholesky)/cholesky | solution.py:42
  40.8 2.4 custom-call.6
  45.1 15.2 %all-to-all-start = ((bf16[32,16,512]{2,0,1:T(8,128)(2,1)}), bf16[32,16,512]{2,0,1:T(8,128)(2,1)}, u32[]{:S(2)}, u32[]{:S(2)}) async-start(bf16[32,16,512]{2,0,1:T(8,128)(2,1)} %bitcast.71), calls=%async_computation | async-start | bytes 1048576 | tf_op jit(solution)/shard_map/all_to_all | solution.py:36
  60.5 48.3 %all-gather.1 = f32[512,32]{1,0:T(8,128)S(1)} all-gather(f32[32,32]{1,0:T(8,128)S(1)} %copy.14), channel_id=3, replica_groups=mesh['aux'=16,'pair'=32] {'aux'}, dimensions={0}, use_global_device_ids=true | all-gather | bytes 69632 | tf_op jit(solution)/shard_map/all_gather | solution.py:75
  109.3 1.5 fusion.35
  110.8 1.1 reduce_sum.61
  112.0 30.8 %all_gather.32 = bf16[32,8192]{1,0:T(8,128)(2,1)S(1)} all-gather(bf16[32,512]{1,0:T(8,128)(2,1)S(1)} %reduce_sum.61), channel_id=1, replica_groups=mesh['aux'=16,'pair'=32] {'aux'}, dimensions={1}, use_global_device_ids=true | all-gather | bytes 557056 | tf_op jit(solution)/shard_map/all_gather | solution.py:38
  142.8 2.8 fusion.1
  145.6 1.0 fusion.4
  147.6 2.4 convolution_bitcast_fusion
  150.1 26.7 %all-gather.5 = f32[32,224,32]{1,2,0:T(8,128)} all-gather(f32[1,224,32]{1,2,0:T(8,128)S(1)} %maximum_bitcast_fusion.1), channel_id=4, replica_groups=mesh['aux'=16,'pair'=32] {'pair'}, dimensions={0}, use_global_device_ids=true | all-gather | bytes 946176 | tf_op jit(solution)/shard_map/all_gather | solution.py:29
  176.8 1.3 reduce_sum.63
  178.2 2.9 %cholesky.55 = f32[32,32]{1,0:T(8,128)S(1)} custom-call(f32[32,32]{1,0:T(8,128)S(1)} %fusion.26), custom_call_target="Cholesky" | custom-call | tf_op jit(solution)/shard_map/jit(cholesky)/cholesky | solution.py:42
  182.5 2.4 custom-call.7
  186.8 10.6 %all-to-all-start.1 = ((bf16[32,16,512]{2,0,1:T(8,128)(2,1)}), bf16[32,16,512]{2,0,1:T(8,128)(2,1)S(1)}, u32[]{:S(2)}, u32[]{:S(2)}) async-start(bf16[32,16,512]{2,0,1:T(8,128)(2,1)} %bitcast.72), calls=%async_computation.1 | async-start | bytes 1048576 | tf_op jit(solution)/shard_map/all_to_all | solution.py:36
  197.6 48.3 %all-gather.3 = f32[512,32]{1,0:T(8,128)S(1)} all-gather(f32[32,32]{1,0:T(8,128)S(1)} %copy.19), channel_id=5, replica_groups=mesh['aux'=16,'pair'=32] {'aux'}, dimensions={0}, use_global_device_ids=true | all-gather | bytes 69632 | tf_op jit(solution)/shard_map/all_gather | solution.py:75
  246.4 3.2 %fusion.36 = f32[32,8192]{1,0:T(8,128)} fusion(f32[32,32]{1,0:T(8,128)S(1)} %fusion.15, f32[32,8192]{1,0:T(8,128)} %copy-done.1), kind=kOutput, calls=%fused_computation.61 | convolution fusion | flops 100663296 | bytes 2101248 | tf_op jit(solution)/shard_map/dot_general | solution.py:23
  249.7 30.8 %all_gather.37 = bf16[32,8192]{1,0:T(8,128)(2,1)S(1)} all-gather(bf16[32,512]{1,0:T(8,128)(2,1)S(1)} %reduce_sum.64), channel_id=1, replica_groups=mesh['aux'=16,'pair'=32] {'aux'}, dimensions={1}, use_global_device_ids=true | all-gather | bytes 557056 | tf_op jit(solution)/shard_map/all_gather | solution.py:38
  280.4 3.8 %fusion.33 = (bf16[32,8192]{1,0:T(8,128)(2,1)}, f32[32,8192]{1,0:T(8,128)}) fusion(f32[32,8192]{1,0:T(8,128)} %fusion.36, f32[8192]{0:T(1024)S(1)} %dynamic_slice.3, f32[32,32]{1,0:T(8,128)S(1)} %convolution_add_fusion, bf16[32,8192]{1,0:T(8,128)(2,1)S(1)} %all_gather.37), kind=kOutput, calls=%fused_computation.58 | convolution fusion | flops 102498304 | bytes 3182592 | tf_op jit(solution)/shard_map/dot_general | solution.py:23
  (52 shorter events, 11.1 us)
Async XLA Ops:
  0.6 2.1 copy-start
  0.6 4.1 %copy-start.4 = (f32[1024]{0:T(1024)S(1)}, f32[1024]{0:T(1024)}, u32[]{:S(2)}) copy-start(f32[1024]{0:T(1024)} %param.9) | copy-start | bytes 12292
  0.7 4.1 %copy-start.5 = (f32[256]{0:T(256)S(1)}, f32[256]{0:T(256)}, u32[]{:S(2)}) copy-start(f32[256]{0:T(256)} %param.8) | copy-start | bytes 3076
  2.7 4.1 %copy-start.2 = (bf16[32,8192]{1,0:T(8,128)(2,1)S(1)}, bf16[32,8192]{1,0:T(8,128)(2,1)}, u32[]{:S(2)}) copy-start(bf16[32,8192]{1,0:T(8,128)(2,1)} %param.10) | copy-start | bytes 1572868
  45.1 65.8 %all-to-all-start = ((bf16[32,16,512]{2,0,1:T(8,128)(2,1)}), bf16[32,16,512]{2,0,1:T(8,128)(2,1)}, u32[]{:S(2)}, u32[]{:S(2)}) async-start(bf16[32,16,512]{2,0,1:T(8,128)(2,1)} %bitcast.71), calls=%async_computation | async-start | bytes 1048576 | tf_op jit(solution)/shard_map/all_to_all | solution.py:36
  145.6 4.5 %copy-start.1 = (f32[32,8192]{1,0:T(8,128)}, f32[32,8192]{1,0:T(8,128)S(1)}, u32[]{:S(2)}) copy-start(f32[32,8192]{1,0:T(8,128)S(1)} %fusion.1) | copy-start | bytes 3145732
  186.8 62.8 %all-to-all-start.1 = ((bf16[32,16,512]{2,0,1:T(8,128)(2,1)}), bf16[32,16,512]{2,0,1:T(8,128)(2,1)S(1)}, u32[]{:S(2)}, u32[]{:S(2)}) async-start(bf16[32,16,512]{2,0,1:T(8,128)(2,1)} %bitcast.72), calls=%async_computation.1 | async-start | bytes 1048576 | tf_op jit(solution)/shard_map/all_to_all | solution.py:36
  246.4 37.9 %copy-start.3 = (f32[32,32]{1,0:T(8,128)}, f32[32,32]{1,0:T(8,128)S(1)}, u32[]{:S(2)}) copy-start(f32[32,32]{1,0:T(8,128)S(1)} %convolution_add_fusion) | copy-start | bytes 12292

commit v3 on v2

--- a/solution.py
+++ b/solution.py
@@ -29,13 +29,22 @@
     return lax.all_gather(matrices, "pair").sum(0)
 
 
-def aux_sum(terms):
+def aux_sum(terms, small):
     n_aux = lax.axis_size("aux")
     rows, cols = terms.shape
-    pieces = terms.reshape(rows, n_aux, cols // n_aux)
+    high = small.astype(jnp.bfloat16)
+    low = (small - high.astype(jnp.float32)).astype(jnp.bfloat16)
+    extra = jnp.concatenate([high, low], axis=1)
+    pieces = jnp.concatenate([
+        terms.reshape(rows, n_aux, cols // n_aux),
+        jnp.broadcast_to(extra[:, None, :], (rows, n_aux, extra.shape[1])),
+    ], axis=2)
     pieces = lax.all_to_all(pieces, "aux", 1, 1, tiled=True)
-    mine = pieces.astype(jnp.float32).sum(1).astype(jnp.bfloat16)
-    return lax.all_gather(mine, "aux", axis=1, tiled=True).astype(jnp.float32)
+    mine = pieces[:, :, : cols // n_aux].astype(jnp.float32).sum(1).astype(jnp.bfloat16)
+    parts = pieces[:, :, cols // n_aux:].astype(jnp.float32)
+    width = small.shape[1]
+    small_sum = (parts[:, :, :width] + parts[:, :, width:]).sum(1)
+    return lax.all_gather(mine, "aux", axis=1, tiled=True).astype(jnp.float32), small_sum
 
 
 def inverse_factor(gram_now):
@@ -72,14 +81,14 @@
             projected, projected, (((0,), (0,)), ((), ())),
             precision=HIGHEST_PRECISION, preferred_element_type=jnp.float32,
         )
-        group_sum = lax.all_gather(group_part / npair_all, "aux").sum(0)
         diag_part = product(product(inverse, summed[k:2 * k]), inverse.T)
-        subspace = group_sum + diag_part
         projected_low = projected.astype(jnp.bfloat16)
         term = lax.dot_general(
             projected_low, b_tensor, (((0,), (0,)), ((), ())), preferred_element_type=jnp.float32
         ).astype(jnp.bfloat16)
-        image_now = aux_sum(term) + diag_row * basis_now
+        coupling, group_sum = aux_sum(term, group_part / npair_all)
+        subspace = group_sum + diag_part
+        image_now = coupling + diag_row * basis_now
         residual = image_now - product(subspace, basis_now)
         trial_now = basis_now - residual / diag_row
     return (trial_now, residual.astype(jnp.bfloat16), subspace)

time: 285 us -> 255 us (0.89)
  the two profiles are of different devices: /device:TPU:32 before, /device:TPU:2 now
where the time goes in v3:
time: 255 us; the launch traced here: 254 us
  blocking collectives  123 us (48%)
  waiting for transfers between devices  64.3 us (25%)
  matrix products  23.9 us (9%)
  other arithmetic  20.6 us (8%)
  starting transfers between devices  17.2 us (7%)
  local copies, waits for them, and re-layouts  3.87 us (2%)
    all_gather x2, blocking collectives, aux_sum(): lax.all_gather(mine, 'aux', axis=1, tiled=True).astype(jnp.float32)  67.2 us
    all_to_all x2, waiting for transfers between devices, aux_sum(): pieces = lax.all_to_all(pieces, 'aux', 1, 1, tiled=True)  64.3 us
    all_gather x2, blocking collectives, pair_sum(): return lax.all_gather(matrices, 'pair').sum(0)  55.7 us
    all_to_all x2, starting transfers between devices, aux_sum(): pieces = lax.all_to_all(pieces, 'aux', 1, 1, tiled=True)  17.2 us
    dot_general x8, matrix products, product(): jnp.dot(first_mat, second_mat, precision=HIGHEST_PRECISION, preferred_ele...  12 us
    dot_general x6, matrix products, correlation_of(): lax.dot_general(first_rows, second_rows, (((1,), (1,)), ((), ())), precis...  8.78 us
    another operation x6, other arithmetic, inverse_factor(): lower_tri = jnp.linalg.cholesky(gram_now)  7.19 us
    another operation x4, other arithmetic, inverse_factor(): lax.linalg.triangular_solve(lower_tri, jnp.eye(gram_now.shape[0], dtype=j...  6.17 us
  transfers between devices with their start and end apart: 2, of which 2 were waited for; matrix products, arithmetic and copies ran while one was open for 2% of the time, Pallas kernels for 0%

profile of v3, /device:TPU:2, one launch (start us, length us, event | category | flops | bytes accessed | tf_op | source)
XLA Modules:
  0.0 253.7 jit_solution(2226761210409575499)
XLA Ops:
  0.7 1.6 convolution_multiply_fusion.4
  2.7 2.0 fusion.36
  4.9 1.2 copy.25
  7.6 30.0 %all-gather.2 = f32[32,224,32]{1,2,0:T(8,128)} all-gather(f32[1,224,32]{1,2,0:T(8,128)S(1)} %maximum_bitcast_fusion), channel_id=2, replica_groups=mesh['aux'=16,'pair'=32] {'pair'}, dimensions={0}, use_global_device_ids=true | all-gather | bytes 946176 | tf_op jit(solution)/shard_map/all_gather | solution.py:29
  37.7 1.3 reduce_sum.60
  39.1 2.9 %cholesky.44 = f32[32,32]{1,0:T(8,128)S(1)} custom-call(f32[32,32]{1,0:T(8,128)S(1)} %fusion.30), custom_call_target="Cholesky" | custom-call | tf_op jit(solution)/shard_map/jit(cholesky)/cholesky | solution.py:51
  43.3 2.4 custom-call.6
  46.4 1.3 convolution_convert_fusion.1
  49.9 12.4 %all-to-all-start = ((bf16[32,16,576]{2,0,1:T(8,128)(2,1)}), bf16[32,16,576]{2,0,1:T(8,128)(2,1)}, u32[]{:S(2)}, u32[]{:S(2)}) async-start(bf16[32,16,576]{2,0,1:T(8,128)(2,1)} %pad_maximum_fusion), calls=%async_computation | async-start | bytes 1310720 | tf_op jit(solution)/shard_map/all_to_all | solution.py:42
  62.5 1.5 fusion.37
  64.1 33.0 %all-to-all-done = bf16[32,16,576]{2,0,1:T(8,128)(2,1)} async-done(((bf16[32,16,576]{2,0,1:T(8,128)(2,1)}), bf16[32,16,576]{2,0,1:T(8,128)(2,1)}, u32[]{:S(2)}, u32[]{:S(2)}) %all-to-all-start) | async-done | bytes 589856 | tf_op jit(solution)/shard_map/all_to_all | solution.py:42
  98.2 1.1 slice_reduce_fusion.1
  99.3 33.6 %all_gather.20 = bf16[32,8192]{1,0:T(8,128)(2,1)S(1)} all-gather(bf16[32,512]{1,0:T(8,128)(2,1)S(1)} %slice_reduce_fusion.1), channel_id=1, replica_groups=mesh['aux'=16,'pair'=32] {'aux'}, dimensions={1}, use_global_device_ids=true | all-gather | bytes 557056 | tf_op jit(solution)/shard_map/all_gather | solution.py:47
  133.0 2.7 %fusion.1 = f32[32,8192]{1,0:T(8,128)S(1)} fusion(f32[32,8192]{1,0:T(8,128)} %fusion.37, f32[32,32]{1,0:T(8,128)S(1)} %convolution_add_fusion.1, bf16[32,8192]{1,0:T(8,128)(2,1)S(1)} %all_gather.20, f32[8192]{0:T(1024)S(1)} %dynamic_slice.3), kind=kOutput, calls=%fused_computation.3 | convolution fusion | flops 102236160 | bytes 2658304 | tf_op jit(solution)/shard_map/dot_general | solution.py:23
  137.8 2.4 convolution_bitcast_fusion
  140.3 25.7 %all-gather.3 = f32[32,224,32]{1,2,0:T(8,128)} all-gather(f32[1,224,32]{1,2,0:T(8,128)S(1)} %maximum_bitcast_fusion.1), channel_id=3, replica_groups=mesh['aux'=16,'pair'=32] {'pair'}, dimensions={0}, use_global_device_ids=true | all-gather | bytes 946176 | tf_op jit(solution)/shard_map/all_gather | solution.py:29
  166.0 1.3 reduce_sum.63
  167.4 2.9 %cholesky.55 = f32[32,32]{1,0:T(8,128)S(1)} custom-call(f32[32,32]{1,0:T(8,128)S(1)} %fusion.28), custom_call_target="Cholesky" | custom-call | tf_op jit(solution)/shard_map/jit(cholesky)/cholesky | solution.py:51
  171.7 2.4 custom-call.7
  176.4 4.8 %all-to-all-start.1 = ((bf16[32,16,576]{2,0,1:T(8,128)(2,1)}), bf16[32,16,576]{2,0,1:T(8,128)(2,1)S(1)}, u32[]{:S(2)}, u32[]{:S(2)}) async-start(bf16[32,16,576]{2,0,1:T(8,128)(2,1)} %pad_maximum_fusion.1), calls=%async_computation.1 | async-start | bytes 1310720 | tf_op jit(solution)/shard_map/all_to_all | solution.py:42
  181.4 3.2 %fusion.38 = f32[32,8192]{1,0:T(8,128)} fusion(f32[32,32]{1,0:T(8,128)S(1)} %fusion.17, f32[32,8192]{1,0:T(8,128)} %copy-done.1), kind=kOutput, calls=%fused_computation.75 | convolution fusion | flops 100663296 | bytes 2101248 | tf_op jit(solution)/shard_map/dot_general | solution.py:23
  184.6 31.3 %all-to-all-done.1 = bf16[32,16,576]{2,0,1:T(8,128)(2,1)S(1)} async-done(((bf16[32,16,576]{2,0,1:T(8,128)(2,1)}), bf16[32,16,576]{2,0,1:T(8,128)(2,1)S(1)}, u32[]{:S(2)}, u32[]{:S(2)}) %all-to-all-start.1) | async-done | bytes 589856 | tf_op jit(solution)/shard_map/all_to_all | solution.py:42
  216.1 33.6 %all_gather.23 = bf16[32,8192]{1,0:T(8,128)(2,1)S(1)} all-gather(bf16[32,512]{1,0:T(8,128)(2,1)S(1)} %slice_reduce_fusion), channel_id=1, replica_groups=mesh['aux'=16,'pair'=32] {'aux'}, dimensions={1}, use_global_device_ids=true | all-gather | bytes 557056 | tf_op jit(solution)/shard_map/all_gather | solution.py:47
  249.9 3.8 %fusion.35 = (bf16[32,8192]{1,0:T(8,128)(2,1)}, f32[32,8192]{1,0:T(8,128)}) fusion(f32[32,8192]{1,0:T(8,128)} %fusion.38, f32[8192]{0:T(1024)S(1)} %dynamic_slice.3, f32[32,32]{1,0:T(8,128)S(1)} %convolution_add_fusion, bf16[32,8192]{1,0:T(8,128)(2,1)S(1)} %all_gather.23), kind=kOutput, calls=%fused_computation.72 | convolution fusion | flops 102498304 | bytes 3182592 | tf_op jit(solution)/shard_map/dot_general | solution.py:23
  (57 shorter events, 14.0 us)
Async XLA Ops:
  0.6 2.1 copy-start
  0.6 4.1 %copy-start.4 = (f32[1024]{0:T(1024)S(1)}, f32[1024]{0:T(1024)}, u32[]{:S(2)}) copy-start(f32[1024]{0:T(1024)} %param.9) | copy-start | bytes 12292
  0.7 4.1 %copy-start.5 = (f32[256]{0:T(256)S(1)}, f32[256]{0:T(256)}, u32[]{:S(2)}) copy-start(f32[256]{0:T(256)} %param.8) | copy-start | bytes 3076
  2.7 4.1 %copy-start.2 = (bf16[32,8192]{1,0:T(8,128)(2,1)S(1)}, bf16[32,8192]{1,0:T(8,128)(2,1)}, u32[]{:S(2)}) copy-start(bf16[32,8192]{1,0:T(8,128)(2,1)} %param.10) | copy-start | bytes 1572868
  49.9 47.2 %all-to-all-start = ((bf16[32,16,576]{2,0,1:T(8,128)(2,1)}), bf16[32,16,576]{2,0,1:T(8,128)(2,1)}, u32[]{:S(2)}, u32[]{:S(2)}) async-start(bf16[32,16,576]{2,0,1:T(8,128)(2,1)} %pad_maximum_fusion), calls=%async_computation | async-start | bytes 1310720 | tf_op jit(solution)/shard_map/all_to_all | solution.py:42
  135.8 4.5 %copy-start.1 = (f32[32,8192]{1,0:T(8,128)}, f32[32,8192]{1,0:T(8,128)S(1)}, u32[]{:S(2)}) copy-start(f32[32,8192]{1,0:T(8,128)S(1)} %fusion.1) | copy-start | bytes 3145732
  176.4 39.5 %all-to-all-start.1 = ((bf16[32,16,576]{2,0,1:T(8,128)(2,1)}), bf16[32,16,576]{2,0,1:T(8,128)(2,1)S(1)}, u32[]{:S(2)}, u32[]{:S(2)}) async-start(bf16[32,16,576]{2,0,1:T(8,128)(2,1)} %pad_maximum_fusion.1), calls=%async_computation.1 | async-start | bytes 1310720 | tf_op jit(solution)/shard_map/all_to_all | solution.py:42
  249.9 3.8 %copy-start.3 = (f32[32,32]{1,0:T(8,128)}, f32[32,32]{1,0:T(8,128)S(1)}, u32[]{:S(2)}) copy-start(f32[32,32]{1,0:T(8,128)S(1)} %convolution_add_fusion) | copy-start | bytes 12292

commit v4 on v3

--- a/solution.py
+++ b/solution.py
@@ -58,8 +58,15 @@
     block_cols = b_tensor.shape[1]
     npair_all = eps_occ.shape[0] * eps_vir.shape[0]
     k = trial.shape[0]
-    everything = (eps_vir[None, :] - eps_occ[:, None]).reshape(npair_all)
-    diagonal = lax.dynamic_slice_in_dim(everything, lax.axis_index("pair") * block_cols, block_cols)
+    nvir = eps_vir.shape[0]
+    if block_cols % nvir == 0:
+        occ_rows = block_cols // nvir
+        occ_block = lax.dynamic_slice_in_dim(eps_occ, lax.axis_index("pair") * occ_rows, occ_rows)
+        diagonal = (eps_vir[None, :] - occ_block[:, None]).reshape(block_cols)
+    else:
+        everything = (eps_vir[None, :] - eps_occ[:, None]).reshape(npair_all)
+        diagonal = lax.dynamic_slice_in_dim(
+            everything, lax.axis_index("pair") * block_cols, block_cols)
     diag_row = diagonal[None, :]
     trial_now = trial
     for iteration in range(ITERS):
@@ -67,8 +74,13 @@
         wide_trial = trial_now.astype(jnp.float32)
         gram_part = correlation_of(trial_now, trial_now, precision)
         weighted_part = correlation_of(wide_trial * diag_row, wide_trial)
-        cross_part = correlation_of(b_tensor.astype(wide_trial.dtype) if precision else b_tensor,
-                                    trial_now, precision)
+        if precision is None:
+            cross_part = correlation_of(b_tensor, trial_now, None)
+        else:
+            high = trial_now.astype(jnp.bfloat16)
+            low = (trial_now - high.astype(jnp.float32)).astype(jnp.bfloat16)
+            cross_part = (correlation_of(b_tensor, high, None)
+                          + correlation_of(b_tensor, low, None))
         summed = pair_sum(jnp.concatenate(
             [gram_part / npair_all, weighted_part / npair_all, cross_part], axis=0))
         inverse = inverse_factor(summed[:k])

time: 255 us -> 254 us (level)
    dot_general x6 -> x7, matrix products: 8.78 us -> 9.4 us  [correlation_of(): lax.dot_general(first_rows, second_rows, (((1,), (1,)), ((), ())), precis...]
where the time goes in v4:
time: 254 us; the launch traced here: 253 us
  blocking collectives  123 us (48%)
  waiting for transfers between devices  64.3 us (25%)
  matrix products  24.5 us (10%)
  other arithmetic  21.2 us (8%)
  starting transfers between devices  17.2 us (7%)
    all_gather x2, blocking collectives, aux_sum(): lax.all_gather(mine, 'aux', axis=1, tiled=True).astype(jnp.float32)  67.2 us
    all_to_all x2, waiting for transfers between devices, aux_sum(): pieces = lax.all_to_all(pieces, 'aux', 1, 1, tiled=True)  64.3 us
    all_gather x2, blocking collectives, pair_sum(): return lax.all_gather(matrices, 'pair').sum(0)  55.7 us
    all_to_all x2, starting transfers between devices, aux_sum(): pieces = lax.all_to_all(pieces, 'aux', 1, 1, tiled=True)  17.2 us
    dot_general x8, matrix products, product(): jnp.dot(first_mat, second_mat, precision=HIGHEST_PRECISION, preferred_ele...  12 us
    dot_general x7, matrix products, correlation_of(): lax.dot_general(first_rows, second_rows, (((1,), (1,)), ((), ())), precis...  9.4 us
    another operation x6, other arithmetic, inverse_factor(): lower_tri = jnp.linalg.cholesky(gram_now)  7.19 us
    another operation x4, other arithmetic, inverse_factor(): lax.linalg.triangular_solve(lower_tri, jnp.eye(gram_now.shape[0], dtype=j...  6.17 us
  transfers between devices with their start and end apart: 2, of which 2 were waited for; matrix products, arithmetic and copies ran while one was open for 2% of the time, Pallas kernels for 0%

profile of v4, /device:TPU:2, one launch (start us, length us, event | category | flops | bytes accessed | tf_op | source)
XLA Modules:
  0.0 253.4 jit_solution(10060372977707924873)
XLA Ops:
  0.6 1.6 convolution_multiply_fusion.4
  3.8 1.9 convolution_multiply_fusion
  5.8 2.0 fusion.40
  7.8 30.0 %all-gather.2 = f32[32,224,32]{1,2,0:T(8,128)} all-gather(f32[1,224,32]{1,2,0:T(8,128)S(1)} %maximum_bitcast_fusion), channel_id=2, replica_groups=mesh['aux'=16,'pair'=32] {'pair'}, dimensions={0}, use_global_device_ids=true | all-gather | bytes 946176 | tf_op jit(solution)/shard_map/all_gather | solution.py:29
  37.9 1.3 reduce_sum.60
  39.2 2.9 %cholesky.44 = f32[32,32]{1,0:T(8,128)S(1)} custom-call(f32[32,32]{1,0:T(8,128)S(1)} %fusion.34), custom_call_target="Cholesky" | custom-call | tf_op jit(solution)/shard_map/jit(cholesky)/cholesky | solution.py:51
  43.5 2.4 custom-call.6
  46.6 1.3 convolution_convert_fusion.1
  48.0 1.2 copy.30
  50.1 12.4 %all-to-all-start = ((bf16[32,16,576]{2,0,1:T(8,128)(2,1)}), bf16[32,16,576]{2,0,1:T(8,128)(2,1)}, u32[]{:S(2)}, u32[]{:S(2)}) async-start(bf16[32,16,576]{2,0,1:T(8,128)(2,1)} %pad_maximum_fusion), calls=%async_computation | async-start | bytes 1310720 | tf_op jit(solution)/shard_map/all_to_all | solution.py:42
  62.8 1.5 fusion.41
  64.3 33.0 %all-to-all-done = bf16[32,16,576]{2,0,1:T(8,128)(2,1)} async-done(((bf16[32,16,576]{2,0,1:T(8,128)(2,1)}), bf16[32,16,576]{2,0,1:T(8,128)(2,1)}, u32[]{:S(2)}, u32[]{:S(2)}) %all-to-all-start) | async-done | bytes 589856 | tf_op jit(solution)/shard_map/all_to_all | solution.py:42
  98.4 1.1 slice_reduce_fusion.1
  99.5 33.6 %all_gather.20 = bf16[32,8192]{1,0:T(8,128)(2,1)S(1)} all-gather(bf16[32,512]{1,0:T(8,128)(2,1)S(1)} %slice_reduce_fusion.1), channel_id=1, replica_groups=mesh['aux'=16,'pair'=32] {'aux'}, dimensions={1}, use_global_device_ids=true | all-gather | bytes 557056 | tf_op jit(solution)/shard_map/all_gather | solution.py:47
  133.3 2.7 %fusion.1 = f32[32,8192]{1,0:T(8,128)S(1)} fusion(f32[32,8192]{1,0:T(8,128)} %fusion.41, f32[32,32]{1,0:T(8,128)S(1)} %convolution_add_fusion.2, bf16[32,8192]{1,0:T(8,128)(2,1)S(1)} %all_gather.20, f32[8192]{0:T(1024)S(1)} %bitcast.74), kind=kOutput, calls=%fused_computation.3 | convolution fusion | flops 102236160 | bytes 2658304 | tf_op jit(solution)/shard_map/dot_general | solution.py:23
  140.1 25.7 %all-gather.3 = f32[32,224,32]{1,2,0:T(8,128)} all-gather(f32[1,224,32]{1,2,0:T(8,128)S(1)} %maximum_bitcast_fusion.1), channel_id=3, replica_groups=mesh['aux'=16,'pair'=32] {'pair'}, dimensions={0}, use_global_device_ids=true | all-gather | bytes 946176 | tf_op jit(solution)/shard_map/all_gather | solution.py:29
  165.7 1.3 reduce_sum.63
  167.1 2.9 %cholesky.55 = f32[32,32]{1,0:T(8,128)S(1)} custom-call(f32[32,32]{1,0:T(8,128)S(1)} %fusion.32), custom_call_target="Cholesky" | custom-call | tf_op jit(solution)/shard_map/jit(cholesky)/cholesky | solution.py:51
  171.4 2.4 custom-call.7
  176.1 4.8 %all-to-all-start.1 = ((bf16[32,16,576]{2,0,1:T(8,128)(2,1)}), bf16[32,16,576]{2,0,1:T(8,128)(2,1)S(1)}, u32[]{:S(2)}, u32[]{:S(2)}) async-start(bf16[32,16,576]{2,0,1:T(8,128)(2,1)} %pad_maximum_fusion.1), calls=%async_computation.1 | async-start | bytes 1310720 | tf_op jit(solution)/shard_map/all_to_all | solution.py:42
  181.1 3.2 %fusion.42 = f32[32,8192]{1,0:T(8,128)} fusion(f32[32,32]{1,0:T(8,128)S(1)} %fusion.21, f32[32,8192]{1,0:T(8,128)} %copy-done.1), kind=kOutput, calls=%fused_computation.81 | convolution fusion | flops 100663296 | bytes 2101248 | tf_op jit(solution)/shard_map/dot_general | solution.py:23
  184.3 31.3 %all-to-all-done.1 = bf16[32,16,576]{2,0,1:T(8,128)(2,1)S(1)} async-done(((bf16[32,16,576]{2,0,1:T(8,128)(2,1)}), bf16[32,16,576]{2,0,1:T(8,128)(2,1)S(1)}, u32[]{:S(2)}, u32[]{:S(2)}) %all-to-all-start.1) | async-done | bytes 589856 | tf_op jit(solution)/shard_map/all_to_all | solution.py:42
  215.9 33.6 %all_gather.23 = bf16[32,8192]{1,0:T(8,128)(2,1)S(1)} all-gather(bf16[32,512]{1,0:T(8,128)(2,1)S(1)} %slice_reduce_fusion), channel_id=1, replica_groups=mesh['aux'=16,'pair'=32] {'aux'}, dimensions={1}, use_global_device_ids=true | all-gather | bytes 557056 | tf_op jit(solution)/shard_map/all_gather | solution.py:47
  249.6 3.8 %fusion.39 = (bf16[32,8192]{1,0:T(8,128)(2,1)}, f32[32,8192]{1,0:T(8,128)}) fusion(f32[32,8192]{1,0:T(8,128)} %fusion.42, f32[8192]{0:T(1024)S(1)} %bitcast.76, f32[32,32]{1,0:T(8,128)S(1)} %convolution_add_fusion.1, bf16[32,8192]{1,0:T(8,128)(2,1)S(1)} %all_gather.23), kind=kOutput, calls=%fused_computation.78 | convolution fusion | flops 102498304 | bytes 3182592 | tf_op jit(solution)/shard_map/dot_general | solution.py:23
  (54 shorter events, 14.3 us)
Async XLA Ops:
  0.6 5.1 %copy-start = (bf16[160,8192]{1,0:T(8,128)(2,1)S(1)}, bf16[160,8192]{1,0:T(8,128)(2,1)}, u32[]{:S(2)}) copy-start(bf16[160,8192]{1,0:T(8,128)(2,1)} %param.7) | copy-start | bytes 7864324
  47.9 14.9 %copy-start.2 = (bf16[32,8192]{1,0:T(8,128)(2,1)S(1)}, bf16[32,8192]{1,0:T(8,128)(2,1)}, u32[]{:S(2)}) copy-start(bf16[32,8192]{1,0:T(8,128)(2,1)} %param.10) | copy-start | bytes 1572868
  50.1 47.2 %all-to-all-start = ((bf16[32,16,576]{2,0,1:T(8,128)(2,1)}), bf16[32,16,576]{2,0,1:T(8,128)(2,1)}, u32[]{:S(2)}, u32[]{:S(2)}) async-start(bf16[32,16,576]{2,0,1:T(8,128)(2,1)} %pad_maximum_fusion), calls=%async_computation | async-start | bytes 1310720 | tf_op jit(solution)/shard_map/all_to_all | solution.py:42
  136.0 3.0 %copy-start.1 = (f32[32,8192]{1,0:T(8,128)}, f32[32,8192]{1,0:T(8,128)S(1)}, u32[]{:S(2)}) copy-start(f32[32,8192]{1,0:T(8,128)S(1)} %fusion.1) | copy-start | bytes 3145732
  176.1 39.5 %all-to-all-start.1 = ((bf16[32,16,576]{2,0,1:T(8,128)(2,1)}), bf16[32,16,576]{2,0,1:T(8,128)(2,1)S(1)}, u32[]{:S(2)}, u32[]{:S(2)}) async-start(bf16[32,16,576]{2,0,1:T(8,128)(2,1)} %pad_maximum_fusion.1), calls=%async_computation.1 | async-start | bytes 1310720 | tf_op jit(solution)/shard_map/all_to_all | solution.py:42
  249.6 3.8 %copy-start.3 = (f32[32,32]{1,0:T(8,128)}, f32[32,32]{1,0:T(8,128)S(1)}, u32[]{:S(2)}) copy-start(f32[32,32]{1,0:T(8,128)S(1)} %convolution_add_fusion.1) | copy-start | bytes 12292

commit v5 on v4

--- a/solution.py
+++ b/solution.py
@@ -2,6 +2,8 @@
 import jax.numpy as jnp
 from jax import lax
 from jax.sharding import PartitionSpec as P
+from jax.experimental import pallas as pl
+from jax.experimental.pallas import tpu as pltpu
 
 ITERS = 2
 
@@ -47,11 +49,36 @@
     return lax.all_gather(mine, "aux", axis=1, tiled=True).astype(jnp.float32), small_sum
 
 
+def _inverse_factor_kernel(gram_ref, inverse_ref):
+    work = gram_ref[...]
+    k = work.shape[0]
+    rows = lax.broadcasted_iota(jnp.int32, (k, k), 0)
+    lanes = lax.broadcasted_iota(jnp.int32, (k, k), 1)
+    row_ids = lax.broadcasted_iota(jnp.int32, (k, 1), 0)
+    lane_ids = lax.broadcasted_iota(jnp.int32, (1, k), 1)
+    inverse = (rows == lanes).astype(jnp.float32)
+    for j in range(k):
+        pick = rows == j
+        column = jnp.sum(jnp.where(lanes == j, work, 0.0), axis=1, keepdims=True)
+        work_row = jnp.sum(jnp.where(pick, work, 0.0), axis=0, keepdims=True)
+        inverse_row = jnp.sum(jnp.where(pick, inverse, 0.0), axis=0, keepdims=True)
+        pivot = jnp.sum(jnp.where(lane_ids == j, work_row, 0.0), axis=1, keepdims=True)
+        scale = 1.0 / jnp.sqrt(pivot)
+        work_row = work_row * scale
+        inverse_row = inverse_row * scale
+        factor = jnp.where(row_ids > j, column * scale, 0.0)
+        work = jnp.where(pick, work_row, work - factor * work_row)
+        inverse = jnp.where(pick, inverse_row, inverse - factor * inverse_row)
+    inverse_ref[...] = inverse
+
 def inverse_factor(gram_now):
-    lower_tri = jnp.linalg.cholesky(gram_now)
-    return lax.linalg.triangular_solve(
-        lower_tri, jnp.eye(gram_now.shape[0], dtype=jnp.float32), left_side=True, lower=True
-    )
+    k = gram_now.shape[0]
+    return pl.pallas_call(
+        _inverse_factor_kernel,
+        out_shape=jax.ShapeDtypeStruct((k, k), jnp.float32),
+        in_specs=[pl.BlockSpec(memory_space=pltpu.VMEM)],
+        out_specs=pl.BlockSpec(memory_space=pltpu.VMEM),
+    )(gram_now)
 
 
 def on_device(b_tensor, eps_occ, eps_vir, trial):

time: 254 us -> 253 us (level)
  other arithmetic: 21.2 us -> 7.81 us
  Pallas kernels: 0 us -> 9.79 us
    another operation x10 -> x0, other arithmetic: 13.4 us -> none  [the longest x6 7.19 us: inverse_factor(): lower_tri = jnp.linalg.cholesky(gram_now)]
    pallas_call x0 -> x2, Pallas kernels: none -> 9.79 us  [inverse_factor(): pl.pallas_call(_inverse_factor_kernel, out_shape=jax.ShapeDtypeStruct((k,...]
where the time goes in v5:
time: 253 us; the launch traced here: 252 us
  blocking collectives  123 us (49%)
  waiting for transfers between devices  64.3 us (25%)
  matrix products  25.5 us (10%)
  starting transfers between devices  17.2 us (7%)
  Pallas kernels  9.79 us (4%)
  other arithmetic  7.81 us (3%)
  local copies, waits for them, and re-layouts  3.61 us (1%)
    all_gather x2, blocking collectives, aux_sum(): lax.all_gather(mine, 'aux', axis=1, tiled=True).astype(jnp.float32)  67.2 us
    all_to_all x2, waiting for transfers between devices, aux_sum(): pieces = lax.all_to_all(pieces, 'aux', 1, 1, tiled=True)  64.3 us
    all_gather x2, blocking collectives, pair_sum(): return lax.all_gather(matrices, 'pair').sum(0)  55.7 us
    all_to_all x2, starting transfers between devices, aux_sum(): pieces = lax.all_to_all(pieces, 'aux', 1, 1, tiled=True)  17.2 us
    dot_general x8, matrix products, product(): jnp.dot(first_mat, second_mat, precision=HIGHEST_PRECISION, preferred_ele...  12 us
    pallas_call x2, Pallas kernels, inverse_factor(): pl.pallas_call(_inverse_factor_kernel, out_shape=jax.ShapeDtypeStruct((k,...  9.79 us
    dot_general x7, matrix products, correlation_of(): lax.dot_general(first_rows, second_rows, (((1,), (1,)), ((), ())), precis...  9.4 us
  transfers between devices with their start and end apart: 2, of which 2 were waited for; matrix products, arithmetic and copies ran while one was open for 2% of the time, Pallas kernels for 0%

profile of v5, /device:TPU:2, one launch (start us, length us, event | category | flops | bytes accessed | tf_op | source)
XLA Modules:
  0.0 252.0 jit_solution(7852303034229794878)
XLA Ops:
  0.6 1.6 convolution_multiply_fusion.4
  3.8 1.9 convolution_multiply_fusion
  5.8 2.0 fusion.28
  7.8 30.0 %all-gather.2 = f32[32,224,32]{1,2,0:T(8,128)} all-gather(f32[1,224,32]{1,2,0:T(8,128)S(1)} %maximum_bitcast_fusion), channel_id=2, replica_groups=mesh['aux'=16,'pair'=32] {'pair'}, dimensions={0}, use_global_device_ids=true | all-gather | bytes 946176 | tf_op jit(solution)/shard_map/all_gather | solution.py:31
  37.9 1.3 reduce_sum.60
  39.8 4.9 %shard_map.67 = f32[32,32]{1,0:T(8,128)} custom-call(f32[32,32]{1,0:T(8,128)} %copy.21.gram_ref), custom_call_target="tpu_custom_call" | custom-call | tf_op jit(solution)/shard_map/pallas_call | solution.py:76
  45.9 1.3 convolution_convert_fusion.1
  47.3 1.2 copy.30
  49.4 12.4 %all-to-all-start = ((bf16[32,16,576]{2,0,1:T(8,128)(2,1)}), bf16[32,16,576]{2,0,1:T(8,128)(2,1)}, u32[]{:S(2)}, u32[]{:S(2)}) async-start(bf16[32,16,576]{2,0,1:T(8,128)(2,1)} %pad_maximum_fusion), calls=%async_computation | async-start | bytes 1310720 | tf_op jit(solution)/shard_map/all_to_all | solution.py:44
  62.1 1.5 fusion.29
  63.6 33.0 %all-to-all-done = bf16[32,16,576]{2,0,1:T(8,128)(2,1)} async-done(((bf16[32,16,576]{2,0,1:T(8,128)(2,1)}), bf16[32,16,576]{2,0,1:T(8,128)(2,1)}, u32[]{:S(2)}, u32[]{:S(2)}) %all-to-all-start) | async-done | bytes 589856 | tf_op jit(solution)/shard_map/all_to_all | solution.py:44
  97.7 1.1 slice_reduce_fusion.1
  98.8 33.6 %all_gather.20 = bf16[32,8192]{1,0:T(8,128)(2,1)S(1)} all-gather(bf16[32,512]{1,0:T(8,128)(2,1)S(1)} %slice_reduce_fusion.1), channel_id=1, replica_groups=mesh['aux'=16,'pair'=32] {'aux'}, dimensions={1}, use_global_device_ids=true | all-gather | bytes 557056 | tf_op jit(solution)/shard_map/all_gather | solution.py:49
  132.6 2.7 %fusion.1 = f32[32,8192]{1,0:T(8,128)S(1)} fusion(f32[32,8192]{1,0:T(8,128)} %fusion.29, f32[32,32]{1,0:T(8,128)S(1)} %convolution_add_fusion.2, bf16[32,8192]{1,0:T(8,128)(2,1)S(1)} %all_gather.20, f32[8192]{0:T(1024)S(1)} %bitcast.56), kind=kOutput, calls=%fused_computation.3 | convolution fusion | flops 102236160 | bytes 2658304 | tf_op jit(solution)/shard_map/dot_general | solution.py:25
  135.3 1.0 fusion.5
  136.4 1.0 convolution_multiply_fusion.2
  139.3 25.7 %all-gather.3 = f32[32,224,32]{1,2,0:T(8,128)} all-gather(f32[1,224,32]{1,2,0:T(8,128)S(1)} %maximum_bitcast_fusion.1), channel_id=3, replica_groups=mesh['aux'=16,'pair'=32] {'pair'}, dimensions={0}, use_global_device_ids=true | all-gather | bytes 946176 | tf_op jit(solution)/shard_map/all_gather | solution.py:31
  165.0 1.3 reduce_sum.63
  167.0 4.9 %shard_map.68 = f32[32,32]{1,0:T(8,128)} custom-call(f32[32,32]{1,0:T(8,128)} %copy.22.gram_ref), custom_call_target="tpu_custom_call" | custom-call | tf_op jit(solution)/shard_map/pallas_call | solution.py:76
  174.7 4.8 %all-to-all-start.1 = ((bf16[32,16,576]{2,0,1:T(8,128)(2,1)}), bf16[32,16,576]{2,0,1:T(8,128)(2,1)S(1)}, u32[]{:S(2)}, u32[]{:S(2)}) async-start(bf16[32,16,576]{2,0,1:T(8,128)(2,1)} %pad_maximum_fusion.1), calls=%async_computation.1 | async-start | bytes 1310720 | tf_op jit(solution)/shard_map/all_to_all | solution.py:44
  179.7 3.2 %fusion.30 = f32[32,8192]{1,0:T(8,128)} fusion(f32[32,32]{1,0:T(8,128)S(1)} %copy-done.3, f32[32,8192]{1,0:T(8,128)} %copy-done.1), kind=kOutput, calls=%fused_computation.60 | convolution fusion | flops 100663296 | bytes 2101248 | tf_op jit(solution)/shard_map/dot_general | solution.py:25
  182.9 31.3 %all-to-all-done.1 = bf16[32,16,576]{2,0,1:T(8,128)(2,1)S(1)} async-done(((bf16[32,16,576]{2,0,1:T(8,128)(2,1)}), bf16[32,16,576]{2,0,1:T(8,128)(2,1)S(1)}, u32[]{:S(2)}, u32[]{:S(2)}) %all-to-all-start.1) | async-done | bytes 589856 | tf_op jit(solution)/shard_map/all_to_all | solution.py:44
  214.4 33.6 %all_gather.23 = bf16[32,8192]{1,0:T(8,128)(2,1)S(1)} all-gather(bf16[32,512]{1,0:T(8,128)(2,1)S(1)} %slice_reduce_fusion), channel_id=1, replica_groups=mesh['aux'=16,'pair'=32] {'aux'}, dimensions={1}, use_global_device_ids=true | all-gather | bytes 557056 | tf_op jit(solution)/shard_map/all_gather | solution.py:49
  248.2 3.8 %fusion.27 = (bf16[32,8192]{1,0:T(8,128)(2,1)}, f32[32,8192]{1,0:T(8,128)}) fusion(f32[32,8192]{1,0:T(8,128)} %fusion.30, f32[8192]{0:T(1024)S(1)} %bitcast.58, f32[32,32]{1,0:T(8,128)S(1)} %convolution_add_fusion.1, bf16[32,8192]{1,0:T(8,128)(2,1)S(1)} %all_gather.23), kind=kOutput, calls=%fused_computation.57 | convolution fusion | flops 102498304 | bytes 3182592 | tf_op jit(solution)/shard_map/dot_general | solution.py:25
  (46 shorter events, 11.9 us)
Async XLA Ops:
  0.6 5.1 %copy-start = (bf16[160,8192]{1,0:T(8,128)(2,1)S(1)}, bf16[160,8192]{1,0:T(8,128)(2,1)}, u32[]{:S(2)}) copy-start(bf16[160,8192]{1,0:T(8,128)(2,1)} %param.4) | copy-start | bytes 7864324
  47.2 14.7 %copy-start.4 = (f32[32,32]{1,0:T(8,128)S(1)}, f32[32,32]{1,0:T(8,128)}, u32[]{:S(2)}) copy-start(f32[32,32]{1,0:T(8,128)} %shard_map.67) | copy-start | bytes 12292
  47.2 14.9 %copy-start.2 = (bf16[32,8192]{1,0:T(8,128)(2,1)S(1)}, bf16[32,8192]{1,0:T(8,128)(2,1)}, u32[]{:S(2)}) copy-start(bf16[32,8192]{1,0:T(8,128)(2,1)} %param.7) | copy-start | bytes 1572868
  49.4 47.2 %all-to-all-start = ((bf16[32,16,576]{2,0,1:T(8,128)(2,1)}), bf16[32,16,576]{2,0,1:T(8,128)(2,1)}, u32[]{:S(2)}, u32[]{:S(2)}) async-start(bf16[32,16,576]{2,0,1:T(8,128)(2,1)} %pad_maximum_fusion), calls=%async_computation | async-start | bytes 1310720 | tf_op jit(solution)/shard_map/all_to_all | solution.py:44
  135.3 3.0 %copy-start.1 = (f32[32,8192]{1,0:T(8,128)}, f32[32,8192]{1,0:T(8,128)S(1)}, u32[]{:S(2)}) copy-start(f32[32,8192]{1,0:T(8,128)S(1)} %fusion.1) | copy-start | bytes 3145732
  173.6 5.9 %copy-start.3 = (f32[32,32]{1,0:T(8,128)S(1)}, f32[32,32]{1,0:T(8,128)}, u32[]{:S(2)}) copy-start(f32[32,32]{1,0:T(8,128)} %shard_map.68) | copy-start | bytes 12292
  174.7 39.5 %all-to-all-start.1 = ((bf16[32,16,576]{2,0,1:T(8,128)(2,1)}), bf16[32,16,576]{2,0,1:T(8,128)(2,1)S(1)}, u32[]{:S(2)}, u32[]{:S(2)}) async-start(bf16[32,16,576]{2,0,1:T(8,128)(2,1)} %pad_maximum_fusion.1), calls=%async_computation.1 | async-start | bytes 1310720 | tf_op jit(solution)/shard_map/all_to_all | solution.py:44
  248.2 3.8 %copy-start.5 = (f32[32,32]{1,0:T(8,128)}, f32[32,32]{1,0:T(8,128)S(1)}, u32[]{:S(2)}) copy-start(f32[32,32]{1,0:T(8,128)S(1)} %convolution_add_fusion.1) | copy-start | bytes 12292

commit v6 on v5

--- a/solution.py
+++ b/solution.py
@@ -97,17 +97,26 @@
     diag_row = diagonal[None, :]
     trial_now = trial
     for iteration in range(ITERS):
-        precision = None if iteration == 0 else HIGHEST_PRECISION
         wide_trial = trial_now.astype(jnp.float32)
-        gram_part = correlation_of(trial_now, trial_now, precision)
-        weighted_part = correlation_of(wide_trial * diag_row, wide_trial)
-        if precision is None:
+        weighted = wide_trial * diag_row
+        weighted_high = weighted.astype(jnp.bfloat16)
+        weighted_low = (weighted - weighted_high.astype(jnp.float32)).astype(jnp.bfloat16)
+        if iteration == 0:
+            both = correlation_of(
+                jnp.concatenate([trial_now, weighted_high, weighted_low], axis=0), trial_now, None)
+            gram_part = both[:k]
+            weighted_part = both[k:2 * k] + both[2 * k:]
             cross_part = correlation_of(b_tensor, trial_now, None)
         else:
             high = trial_now.astype(jnp.bfloat16)
             low = (trial_now - high.astype(jnp.float32)).astype(jnp.bfloat16)
-            cross_part = (correlation_of(b_tensor, high, None)
-                          + correlation_of(b_tensor, low, None))
+            split = jnp.concatenate([high, low], axis=0)
+            both = correlation_of(
+                jnp.concatenate([high, low, weighted_high, weighted_low], axis=0), split, None)
+            gram_part = both[:k, :k] + both[:k, k:] + both[k:2 * k, :k]
+            weighted_part = both[2 * k:3 * k, :k] + both[2 * k:3 * k, k:] + both[3 * k:, :k]
+            cross = correlation_of(b_tensor, split, None)
+            cross_part = cross[:, :k] + cross[:, k:]
         summed = pair_sum(jnp.concatenate(
             [gram_part / npair_all, weighted_part / npair_all, cross_part], axis=0))
         inverse = inverse_factor(summed[:k])

time: 253 us -> 249 us (0.984)
  matrix products: 25.5 us -> 21.9 us
    dot_general x7 -> x4, matrix products: 9.4 us -> 4.44 us  [correlation_of(): lax.dot_general(first_rows, second_rows, (((1,), (1,)), ((), ())), precis...]
where the time goes in v6:
time: 249 us
  blocking collectives  123 us (49%)
  waiting for transfers between devices  64.2 us (26%)
  matrix products  21.9 us (9%)
  starting transfers between devices  17.2 us (7%)
  Pallas kernels  9.79 us (4%)
  other arithmetic  8.16 us (3%)
  local copies, waits for them, and re-layouts  3.7 us (1%)
    all_gather x2, blocking collectives, aux_sum(): lax.all_gather(mine, 'aux', axis=1, tiled=True).astype(jnp.float32)  67.2 us
    all_to_all x2, waiting for transfers between devices, aux_sum(): pieces = lax.all_to_all(pieces, 'aux', 1, 1, tiled=True)  64.2 us
    all_gather x2, blocking collectives, pair_sum(): return lax.all_gather(matrices, 'pair').sum(0)  55.5 us
    all_to_all x2, starting transfers between devices, aux_sum(): pieces = lax.all_to_all(pieces, 'aux', 1, 1, tiled=True)  17.2 us
    dot_general x8, matrix products, product(): jnp.dot(first_mat, second_mat, precision=HIGHEST_PRECISION, preferred_ele...  13.4 us
    pallas_call x2, Pallas kernels, inverse_factor(): pl.pallas_call(_inverse_factor_kernel, out_shape=jax.ShapeDtypeStruct((k,...  9.79 us
  transfers between devices with their start and end apart: 2, of which 2 were waited for; matrix products, arithmetic and copies ran while one was open for 2% of the time, Pallas kernels for 0%

profile of v6, /device:TPU:2, one launch (start us, length us, event | category | flops | bytes accessed | tf_op | source)
XLA Modules:
  0.0 248.6 jit_solution(12760798850497138069)
XLA Ops:
  2.4 2.0 fusion.36
  5.4 30.0 %all-gather.2 = f32[32,224,32]{1,2,0:T(8,128)} all-gather(f32[1,224,32]{1,2,0:T(8,128)S(1)} %maximum_bitcast_fusion), channel_id=2, replica_groups=mesh['aux'=16,'pair'=32] {'pair'}, dimensions={0}, use_global_device_ids=true | all-gather | bytes 946176 | tf_op jit(solution)/shard_map/all_gather | solution.py:31
  35.4 1.3 reduce_sum.60
  37.4 4.9 %shard_map.67 = f32[32,32]{1,0:T(8,128)} custom-call(f32[32,32]{1,0:T(8,128)} %copy.21.gram_ref), custom_call_target="tpu_custom_call" | custom-call | tf_op jit(solution)/shard_map/pallas_call | solution.py:76
  42.3 0.9 fusion.21
  43.4 1.3 convolution_convert_fusion.1
  44.8 1.1 copy.30
  46.0 0.9 pad_maximum_fusion.3
  46.9 12.4 %all-to-all-start = ((bf16[32,16,576]{2,0,1:T(8,128)(2,1)}), bf16[32,16,576]{2,0,1:T(8,128)(2,1)}, u32[]{:S(2)}, u32[]{:S(2)}) async-start(bf16[32,16,576]{2,0,1:T(8,128)(2,1)} %pad_maximum_fusion.3), calls=%async_computation | async-start | bytes 1310720 | tf_op jit(solution)/shard_map/all_to_all | solution.py:44
  59.6 1.5 fusion.37
  61.1 33.0 %all-to-all-done = bf16[32,16,576]{2,0,1:T(8,128)(2,1)} async-done(((bf16[32,16,576]{2,0,1:T(8,128)(2,1)}), bf16[32,16,576]{2,0,1:T(8,128)(2,1)}, u32[]{:S(2)}, u32[]{:S(2)}) %all-to-all-start) | async-done | bytes 589856 | tf_op jit(solution)/shard_map/all_to_all | solution.py:44
  95.2 1.1 slice_reduce_fusion.1
  96.3 33.6 %all_gather.20 = bf16[32,8192]{1,0:T(8,128)(2,1)S(1)} all-gather(bf16[32,512]{1,0:T(8,128)(2,1)S(1)} %slice_reduce_fusion.1), channel_id=1, replica_groups=mesh['aux'=16,'pair'=32] {'aux'}, dimensions={1}, use_global_device_ids=true | all-gather | bytes 557056 | tf_op jit(solution)/shard_map/all_gather | solution.py:49
  130.1 3.9 %multiply_convert_fusion = (bf16[32,8192]{1,0:T(8,128)(2,1)S(1)}, bf16[32,8192]{1,0:T(8,128)(2,1)S(1)}, bf16[32,8192]{1,0:T(8,128)(2,1)S(1)}, bf16[32,8192]{1,0:T(8,128)(2,1)S(1)}, f32[32,8192]{1,0:T(8,128)}) fusion(f32[8192]{0:T(1024)S(1)} %bitcast.50, f32[32,8192]{1,0:T(8,128)} %fusion.37, f32[32,32]{1,0:T(8,128)S(1)} %convolution_add_fusion.1, ...), kind=kOutput, calls=%fused_computation.32 | convolution fusion | flops 104595456 | bytes 4755456 | tf_op jit(solution)/shard_map/dot_general | solution.py:25
  134.0 1.0 convolution_bitcast_fusion
  136.0 25.5 %all-gather.3 = f32[32,224,32]{1,2,0:T(8,128)} all-gather(f32[1,224,32]{1,2,0:T(8,128)S(1)} %maximum_bitcast_fusion.1), channel_id=3, replica_groups=mesh['aux'=16,'pair'=32] {'pair'}, dimensions={0}, use_global_device_ids=true | all-gather | bytes 946176 | tf_op jit(solution)/shard_map/all_gather | solution.py:31
  161.5 1.3 reduce_sum.63
  163.5 4.9 %shard_map.68 = f32[32,32]{1,0:T(8,128)} custom-call(f32[32,32]{1,0:T(8,128)} %copy.22.gram_ref), custom_call_target="tpu_custom_call" | custom-call | tf_op jit(solution)/shard_map/pallas_call | solution.py:76
  168.4 0.9 fusion.19
  171.2 4.8 %all-to-all-start.1 = ((bf16[32,16,576]{2,0,1:T(8,128)(2,1)}), bf16[32,16,576]{2,0,1:T(8,128)(2,1)S(1)}, u32[]{:S(2)}, u32[]{:S(2)}) async-start(bf16[32,16,576]{2,0,1:T(8,128)(2,1)} %pad_maximum_fusion.4), calls=%async_computation.1 | async-start | bytes 1310720 | tf_op jit(solution)/shard_map/all_to_all | solution.py:44
  176.2 3.3 %fusion.38 = f32[32,8192]{1,0:T(8,128)} fusion(f32[32,32]{1,0:T(8,128)S(1)} %copy-done.2, f32[32,8192]{1,0:T(8,128)} %get-tuple-element.21), kind=kOutput, calls=%fused_computation.79 | convolution fusion | flops 100663296 | bytes 2101248 | tf_op jit(solution)/shard_map/dot_general | solution.py:25
  179.5 31.2 %all-to-all-done.1 = bf16[32,16,576]{2,0,1:T(8,128)(2,1)S(1)} async-done(((bf16[32,16,576]{2,0,1:T(8,128)(2,1)}), bf16[32,16,576]{2,0,1:T(8,128)(2,1)S(1)}, u32[]{:S(2)}, u32[]{:S(2)}) %all-to-all-start.1) | async-done | bytes 589856 | tf_op jit(solution)/shard_map/all_to_all | solution.py:44
  210.9 33.6 %all_gather.23 = bf16[32,8192]{1,0:T(8,128)(2,1)S(1)} all-gather(bf16[32,512]{1,0:T(8,128)(2,1)S(1)} %slice_reduce_fusion), channel_id=1, replica_groups=mesh['aux'=16,'pair'=32] {'aux'}, dimensions={1}, use_global_device_ids=true | all-gather | bytes 557056 | tf_op jit(solution)/shard_map/all_gather | solution.py:49
  244.7 3.9 %fusion.35 = (bf16[32,8192]{1,0:T(8,128)(2,1)}, f32[32,8192]{1,0:T(8,128)}) fusion(f32[32,8192]{1,0:T(8,128)} %fusion.38, f32[8192]{0:T(1024)S(1)} %bitcast.51, f32[32,32]{1,0:T(8,128)S(1)} %convolution_add_fusion, bf16[32,8192]{1,0:T(8,128)(2,1)S(1)} %all_gather.23), kind=kOutput, calls=%fused_computation.76 | convolution fusion | flops 102498304 | bytes 3182592 | tf_op jit(solution)/shard_map/dot_general | solution.py:25
  (45 shorter events, 9.1 us)
Async XLA Ops:
  0.6 1.8 copy-start
  0.6 3.7 %copy-start.1 = (bf16[32,8192]{1,0:T(8,128)(2,1)S(1)}, bf16[32,8192]{1,0:T(8,128)(2,1)}, u32[]{:S(2)}) copy-start(bf16[32,8192]{1,0:T(8,128)(2,1)} %param.7) | copy-start | bytes 1572868
  44.7 14.6 %copy-start.3 = (f32[32,32]{1,0:T(8,128)S(1)}, f32[32,32]{1,0:T(8,128)}, u32[]{:S(2)}) copy-start(f32[32,32]{1,0:T(8,128)} %shard_map.67) | copy-start | bytes 12292
  46.9 47.2 %all-to-all-start = ((bf16[32,16,576]{2,0,1:T(8,128)(2,1)}), bf16[32,16,576]{2,0,1:T(8,128)(2,1)}, u32[]{:S(2)}, u32[]{:S(2)}) async-start(bf16[32,16,576]{2,0,1:T(8,128)(2,1)} %pad_maximum_fusion.3), calls=%async_computation | async-start | bytes 1310720 | tf_op jit(solution)/shard_map/all_to_all | solution.py:44
  170.0 5.9 %copy-start.2 = (f32[32,32]{1,0:T(8,128)S(1)}, f32[32,32]{1,0:T(8,128)}, u32[]{:S(2)}) copy-start(f32[32,32]{1,0:T(8,128)} %shard_map.68) | copy-start | bytes 12292
  171.2 39.5 %all-to-all-start.1 = ((bf16[32,16,576]{2,0,1:T(8,128)(2,1)}), bf16[32,16,576]{2,0,1:T(8,128)(2,1)S(1)}, u32[]{:S(2)}, u32[]{:S(2)}) async-start(bf16[32,16,576]{2,0,1:T(8,128)(2,1)} %pad_maximum_fusion.4), calls=%async_computation.1 | async-start | bytes 1310720 | tf_op jit(solution)/shard_map/all_to_all | solution.py:44
  244.7 4.0 %copy-start.4 = (f32[32,32]{1,0:T(8,128)}, f32[32,32]{1,0:T(8,128)S(1)}, u32[]{:S(2)}) copy-start(f32[32,32]{1,0:T(8,128)S(1)} %convolution_add_fusion) | copy-start | bytes 12292

commit v7 on v6

--- a/solution.py
+++ b/solution.py
@@ -31,22 +31,28 @@
     return lax.all_gather(matrices, "pair").sum(0)
 
 
-def aux_sum(terms, small):
+def aux_sum(terms):
     n_aux = lax.axis_size("aux")
     rows, cols = terms.shape
-    high = small.astype(jnp.bfloat16)
-    low = (small - high.astype(jnp.float32)).astype(jnp.bfloat16)
-    extra = jnp.concatenate([high, low], axis=1)
-    pieces = jnp.concatenate([
-        terms.reshape(rows, n_aux, cols // n_aux),
-        jnp.broadcast_to(extra[:, None, :], (rows, n_aux, extra.shape[1])),
-    ], axis=2)
+    pieces = terms.reshape(rows, n_aux, cols // n_aux)
     pieces = lax.all_to_all(pieces, "aux", 1, 1, tiled=True)
-    mine = pieces[:, :, : cols // n_aux].astype(jnp.float32).sum(1).astype(jnp.bfloat16)
-    parts = pieces[:, :, cols // n_aux:].astype(jnp.float32)
-    width = small.shape[1]
-    small_sum = (parts[:, :, :width] + parts[:, :, width:]).sum(1)
-    return lax.all_gather(mine, "aux", axis=1, tiled=True).astype(jnp.float32), small_sum
+    mine = pieces.astype(jnp.float32).sum(1).astype(jnp.bfloat16)
+    return lax.all_gather(mine, "aux", axis=1, tiled=True).astype(jnp.float32)
+
+
+def aux_gather_sum(small):
+    n_aux = lax.axis_size("aux")
+    if n_aux & (n_aux - 1):
+        return lax.all_gather(small, "aux").sum(0)
+    me = lax.axis_index("aux")
+    blocks = small[None]
+    step = 1
+    while step < n_aux:
+        other = lax.ppermute(blocks, "aux", [(i, i ^ step) for i in range(n_aux)])
+        blocks = jnp.where((me & step) != 0,
+                           jnp.concatenate([other, blocks]), jnp.concatenate([blocks, other]))
+        step *= 2
+    return blocks.sum(0)
 
 
 def _inverse_factor_kernel(gram_ref, inverse_ref):
@@ -134,9 +140,8 @@
         term = lax.dot_general(
             projected_low, b_tensor, (((0,), (0,)), ((), ())), preferred_element_type=jnp.float32
         ).astype(jnp.bfloat16)
-        coupling, group_sum = aux_sum(term, group_part / npair_all)
-        subspace = group_sum + diag_part
-        image_now = coupling + diag_row * basis_now
+        subspace = aux_gather_sum(group_part / npair_all) + diag_part
+        image_now = aux_sum(term) + diag_row * basis_now
         residual = image_now - product(subspace, basis_now)
         trial_now = basis_now - residual / diag_row
     return (trial_now, residual.astype(jnp.bfloat16), subspace)

time: 249 us -> 308 us (1.24)
  starting transfers between devices: 17.2 us -> 74.6 us
  waiting for transfers between devices: 64.2 us -> 68 us
    ppermute x0 -> x8, waiting for transfers between devices: none -> 68 us  [aux_gather_sum(): other = lax.ppermute(blocks, 'aux', [(i, i ^ step) for i in range(n_aux)])]
    all_to_all x2, waiting for transfers between devices: 64.2 us -> 0.01 us  [aux_sum(): pieces = lax.all_to_all(pieces, 'aux', 1, 1, tiled=True)]
    ppermute x0 -> x8, starting transfers between devices: none -> 53.7 us  [aux_gather_sum(): other = lax.ppermute(blocks, 'aux', [(i, i ^ step) for i in range(n_aux)])]
    all_to_all x2, starting transfers between devices: 17.2 us -> 20.9 us  [aux_sum(): pieces = lax.all_to_all(pieces, 'aux', 1, 1, tiled=True)]
  transfers between devices with their start and end apart: 2 -> 10, of which waited for: 2 -> 7; matrix products, arithmetic and copies ran while one was open for 2% -> 2% of each run, Pallas kernels for 0% -> 0%
where the time goes in v7:
time: 308 us; the launch traced here: 307 us
  blocking collectives  123 us (40%)
  starting transfers between devices  74.6 us (24%)
  waiting for transfers between devices  68 us (22%)
  matrix products  21 us (7%)
  Pallas kernels  9.79 us (3%)
  other arithmetic  5.26 us (2%)
  local copies, waits for them, and re-layouts  4.13 us (1%)
    ppermute x8, waiting for transfers between devices, aux_gather_sum(): other = lax.ppermute(blocks, 'aux', [(i, i ^ step) for i in range(n_aux)])  68 us
    all_gather x2, blocking collectives, aux_sum(): return lax.all_gather(mine, 'aux', axis=1, tiled=True).astype(jnp.float32)  67.6 us
    all_gather x2, blocking collectives, pair_sum(): return lax.all_gather(matrices, 'pair').sum(0)  55.5 us
    ppermute x8, starting transfers between devices, aux_gather_sum(): other = lax.ppermute(blocks, 'aux', [(i, i ^ step) for i in range(n_aux)])  53.7 us
    all_to_all x2, starting transfers between devices, aux_sum(): pieces = lax.all_to_all(pieces, 'aux', 1, 1, tiled=True)  20.9 us
    dot_general x8, matrix products, product(): jnp.dot(first_mat, second_mat, precision=HIGHEST_PRECISION, preferred_ele...  13.3 us
    pallas_call x2, Pallas kernels, inverse_factor(): pl.pallas_call(_inverse_factor_kernel, out_shape=jax.ShapeDtypeStruct((k,...  9.79 us
  transfers between devices with their start and end apart: 10, of which 7 were waited for; matrix products, arithmetic and copies ran while one was open for 2% of the time, Pallas kernels for 0%

profile of v7, /device:TPU:2, one launch (start us, length us, event | category | flops | bytes accessed | tf_op | source)
XLA Modules:
  0.0 306.8 jit_solution(15286601153267438934)
XLA Ops:
  5.4 30.0 %all-gather.2 = f32[32,224,32]{1,2,0:T(8,128)} all-gather(f32[1,224,32]{1,2,0:T(8,128)S(1)} %maximum_bitcast_fusion), channel_id=2, replica_groups=mesh['aux'=16,'pair'=32] {'pair'}, dimensions={0}, use_global_device_ids=true | all-gather | bytes 946176 | tf_op jit(solution)/shard_map/all_gather | solution.py:31
  37.4 4.9 %shard_map.67 = f32[32,32]{1,0:T(8,128)} custom-call(f32[32,32]{1,0:T(8,128)} %copy.18.gram_ref), custom_call_target="tpu_custom_call" | custom-call | tf_op jit(solution)/shard_map/pallas_call | solution.py:82
  44.7 12.4 %all-to-all-start = ((bf16[32,16,512]{2,0,1:T(8,128)(2,1)}), bf16[32,16,512]{2,0,1:T(8,128)(2,1)}, u32[]{:S(2)}, u32[]{:S(2)}) async-start(bf16[32,16,512]{2,0,1:T(8,128)(2,1)} %bitcast.51), calls=%async_computation | async-start | bytes 1048576 | tf_op jit(solution)/shard_map/all_to_all | solution.py:38
  57.3 3.8 %collective-permute-start = (f32[1,32,32]{1,2,0:T(8,128)S(1)}, f32[1,32,32]{1,2,0:T(8,128)S(1)}, u32[]{:S(2)}, u32[]{:S(2)}) collective-permute-start(f32[1,32,32]{1,2,0:T(8,128)S(1)} %fusion.17), channel_id=1, source_target_pairs={{0,32},{32,0},{64,96},{96,64},{128,160},{160,128},{192,224},{224,1... | collective-permute-start | bytes 12296 | tf_op jit(solution)/shard_map/ppermute | solution.py:51
  61.0 21.3 %collective-permute-done = f32[1,32,32]{1,2,0:T(8,128)S(1)} collective-permute-done((f32[1,32,32]{1,2,0:T(8,128)S(1)}, f32[1,32,32]{1,2,0:T(8,128)S(1)}, u32[]{:S(2)}, u32[]{:S(2)}) %collective-permute-start) | collective-permute-done | bytes 4128 | tf_op jit(solution)/shard_map/ppermute | solution.py:51
  82.4 3.4 %collective-permute-start.1 = (f32[2,32,32]{1,2,0:T(8,128)S(1)}, f32[2,32,32]{1,2,0:T(8,128)S(1)}, u32[]{:S(2)}, u32[]{:S(2)}) collective-permute-start(f32[2,32,32]{1,2,0:T(8,128)S(1)} %maximum_select_fusion.6), channel_id=1, source_target_pairs={{0,64},{32,96},{64,0},{96,32},{128,192},{160,224},{192,128},{224,1... | collective-permute-start | bytes 24584 | tf_op jit(solution)/shard_map/ppermute | solution.py:51
  85.8 3.3 %collective-permute-done.1 = f32[2,32,32]{1,2,0:T(8,128)S(1)} collective-permute-done((f32[2,32,32]{1,2,0:T(8,128)S(1)}, f32[2,32,32]{1,2,0:T(8,128)S(1)}, u32[]{:S(2)}, u32[]{:S(2)}) %collective-permute-start.1) | collective-permute-done | bytes 8224 | tf_op jit(solution)/shard_map/ppermute | solution.py:51
  89.1 7.8 %collective-permute-start.2 = (f32[4,32,32]{1,2,0:T(8,128)S(1)}, f32[4,32,32]{1,2,0:T(8,128)S(1)}, u32[]{:S(2)}, u32[]{:S(2)}) collective-permute-start(f32[4,32,32]{1,2,0:T(8,128)S(1)} %maximum_select_fusion.4), channel_id=1, source_target_pairs={{0,128},{32,160},{64,192},{96,224},{128,0},{160,32},{192,64},{224,... | collective-permute-start | bytes 49160 | tf_op jit(solution)/shard_map/ppermute | solution.py:51
  101.4 11.8 %collective-permute-start.3 = (f32[8,32,32]{1,2,0:T(8,128)S(1)}, f32[8,32,32]{1,2,0:T(8,128)S(1)}, u32[]{:S(2)}, u32[]{:S(2)}) collective-permute-start(f32[8,32,32]{1,2,0:T(8,128)S(1)} %maximum_select_fusion.2), channel_id=1, source_target_pairs={{0,256},{32,288},{64,320},{96,352},{128,384},{160,416},{192,448},{... | collective-permute-start | bytes 98312 | tf_op jit(solution)/shard_map/ppermute | solution.py:51
  113.4 7.6 %collective-permute-done.3 = f32[8,32,32]{1,2,0:T(8,128)S(1)} collective-permute-done((f32[8,32,32]{1,2,0:T(8,128)S(1)}, f32[8,32,32]{1,2,0:T(8,128)S(1)}, u32[]{:S(2)}, u32[]{:S(2)}) %collective-permute-start.3) | collective-permute-done | bytes 32800 | tf_op jit(solution)/shard_map/ppermute | solution.py:51
  122.3 33.0 %all_gather.20 = bf16[32,8192]{1,0:T(8,128)(2,1)S(1)} all-gather(bf16[32,512]{1,0:T(8,128)(2,1)S(1)} %reduce_sum.61), channel_id=1, replica_groups=mesh['aux'=16,'pair'=32] {'aux'}, dimensions={1}, use_global_device_ids=true | all-gather | bytes 557056 | tf_op jit(solution)/shard_map/all_gather | solution.py:40
  155.3 3.9 %multiply_convert_fusion = (bf16[32,8192]{1,0:T(8,128)(2,1)S(1)}, bf16[32,8192]{1,0:T(8,128)(2,1)S(1)}, bf16[32,8192]{1,0:T(8,128)(2,1)S(1)}, bf16[32,8192]{1,0:T(8,128)(2,1)S(1)}, f32[32,8192]{1,0:T(8,128)}) fusion(f32[8192]{0:T(1024)S(1)} %bitcast.54, f32[32,8192]{1,0:T(8,128)} %fusion.39, f32[32,32]{0,1:T(8,128)S(1)} %convolution_add_fusion, ...), kind=kOutput, calls=%fused_computation.33 | convolution fusion | flops 104595456 | bytes 4755456 | tf_op jit(solution)/shard_map/dot_general | solution.py:25
  161.2 25.5 %all-gather.3 = f32[32,224,32]{1,2,0:T(8,128)} all-gather(f32[1,224,32]{1,2,0:T(8,128)S(1)} %maximum_bitcast_fusion.1), channel_id=3, replica_groups=mesh['aux'=16,'pair'=32] {'pair'}, dimensions={0}, use_global_device_ids=true | all-gather | bytes 946176 | tf_op jit(solution)/shard_map/all_gather | solution.py:31
  188.7 4.9 %shard_map.68 = f32[32,32]{1,0:T(8,128)} custom-call(f32[32,32]{1,0:T(8,128)} %copy.19.gram_ref), custom_call_target="tpu_custom_call" | custom-call | tf_op jit(solution)/shard_map/pallas_call | solution.py:82
  196.0 8.5 %all-to-all-start.1 = ((bf16[32,16,512]{2,0,1:T(8,128)(2,1)}), bf16[32,16,512]{2,0,1:T(8,128)(2,1)S(1)}, u32[]{:S(2)}, u32[]{:S(2)}) async-start(bf16[32,16,512]{2,0,1:T(8,128)(2,1)} %bitcast.52), calls=%async_computation.1 | async-start | bytes 1048576 | tf_op jit(solution)/shard_map/all_to_all | solution.py:38
  204.6 3.8 %collective-permute-start.4 = (f32[1,32,32]{1,2,0:T(8,128)S(1)}, f32[1,32,32]{1,2,0:T(8,128)S(1)}, u32[]{:S(2)}, u32[]{:S(2)}) collective-permute-start(f32[1,32,32]{1,2,0:T(8,128)S(1)} %fusion.16), channel_id=1, source_target_pairs={{0,32},{32,0},{64,96},{96,64},{128,160},{160,128},{192,224},{224,1... | collective-permute-start | bytes 12296 | tf_op jit(solution)/shard_map/ppermute | solution.py:51
  208.5 21.3 %collective-permute-done.4 = f32[1,32,32]{1,2,0:T(8,128)S(1)} collective-permute-done((f32[1,32,32]{1,2,0:T(8,128)S(1)}, f32[1,32,32]{1,2,0:T(8,128)S(1)}, u32[]{:S(2)}, u32[]{:S(2)}) %collective-permute-start.4) | collective-permute-done | bytes 4128 | tf_op jit(solution)/shard_map/ppermute | solution.py:51
  229.8 3.6 %collective-permute-start.5 = (f32[2,32,32]{1,2,0:T(8,128)S(1)}, f32[2,32,32]{1,2,0:T(8,128)S(1)}, u32[]{:S(2)}, u32[]{:S(2)}) collective-permute-start(f32[2,32,32]{1,2,0:T(8,128)S(1)} %maximum_select_fusion.7), channel_id=1, source_target_pairs={{0,64},{32,96},{64,0},{96,32},{128,192},{160,224},{192,128},{224,1... | collective-permute-start | bytes 24584 | tf_op jit(solution)/shard_map/ppermute | solution.py:51
  236.6 7.6 %collective-permute-start.6 = (f32[4,32,32]{1,2,0:T(8,128)S(1)}, f32[4,32,32]{1,2,0:T(8,128)S(1)}, u32[]{:S(2)}, u32[]{:S(2)}) collective-permute-start(f32[4,32,32]{1,2,0:T(8,128)S(1)} %maximum_select_fusion.5), channel_id=1, source_target_pairs={{0,128},{32,160},{64,192},{96,224},{128,0},{160,32},{192,64},{224,... | collective-permute-start | bytes 49160 | tf_op jit(solution)/shard_map/ppermute | solution.py:51
  244.5 5.0 %collective-permute-done.6 = f32[4,32,32]{1,2,0:T(8,128)S(1)} collective-permute-done((f32[4,32,32]{1,2,0:T(8,128)S(1)}, f32[4,32,32]{1,2,0:T(8,128)S(1)}, u32[]{:S(2)}, u32[]{:S(2)}) %collective-permute-start.6) | collective-permute-done | bytes 16416 | tf_op jit(solution)/shard_map/ppermute | solution.py:51
  249.4 11.9 %collective-permute-start.7 = (f32[8,32,32]{1,2,0:T(8,128)S(1)}, f32[8,32,32]{1,2,0:T(8,128)S(1)}, u32[]{:S(2)}, u32[]{:S(2)}) collective-permute-start(f32[8,32,32]{1,2,0:T(8,128)S(1)} %maximum_select_fusion.3), channel_id=1, source_target_pairs={{0,256},{32,288},{64,320},{96,352},{128,384},{160,416},{192,448},{... | collective-permute-start | bytes 98312 | tf_op jit(solution)/shard_map/ppermute | solution.py:51
  261.5 6.6 %collective-permute-done.7 = f32[8,32,32]{1,2,0:T(8,128)S(1)} collective-permute-done((f32[8,32,32]{1,2,0:T(8,128)S(1)}, f32[8,32,32]{1,2,0:T(8,128)S(1)}, u32[]{:S(2)}, u32[]{:S(2)}) %collective-permute-start.7) | collective-permute-done | bytes 32800 | tf_op jit(solution)/shard_map/ppermute | solution.py:51
  268.3 34.6 %all_gather.23 = bf16[32,8192]{1,0:T(8,128)(2,1)S(1)} all-gather(bf16[32,512]{1,0:T(8,128)(2,1)S(1)} %reduce_sum.64), channel_id=1, replica_groups=mesh['aux'=16,'pair'=32] {'aux'}, dimensions={1}, use_global_device_ids=true | all-gather | bytes 557056 | tf_op jit(solution)/shard_map/all_gather | solution.py:40
  302.9 3.9 %fusion.37 = (bf16[32,8192]{1,0:T(8,128)(2,1)}, f32[32,8192]{1,0:T(8,128)}) fusion(f32[32,8192]{1,0:T(8,128)} %fusion.40, f32[8192]{0:T(1024)S(1)} %bitcast.55, f32[32,32]{1,0:T(8,128)S(1)} %add.43, bf16[32,8192]{1,0:T(8,128)(2,1)S(1)} %all_gather.23), kind=kOutput, calls=%fused_computation.73 | convolution fusion | flops 102498304 | bytes 3182592 | tf_op jit(solution)/shard_map/dot_general | solution.py:25
  (59 shorter events, 25.5 us)
Async XLA Ops:
  0.6 1.8 copy-start
  0.6 3.7 %copy-start.1 = (bf16[32,8192]{1,0:T(8,128)(2,1)S(1)}, bf16[32,8192]{1,0:T(8,128)(2,1)}, u32[]{:S(2)}) copy-start(bf16[32,8192]{1,0:T(8,128)(2,1)} %param.7) | copy-start | bytes 1572868
  43.3 53.6 %copy-start.3 = (f32[32,32]{1,0:T(8,128)S(1)}, f32[32,32]{1,0:T(8,128)}, u32[]{:S(2)}) copy-start(f32[32,32]{1,0:T(8,128)} %shard_map.67) | copy-start | bytes 12292
  44.7 76.5 %all-to-all-start = ((bf16[32,16,512]{2,0,1:T(8,128)(2,1)}), bf16[32,16,512]{2,0,1:T(8,128)(2,1)}, u32[]{:S(2)}, u32[]{:S(2)}) async-start(bf16[32,16,512]{2,0,1:T(8,128)(2,1)} %bitcast.51), calls=%async_computation | async-start | bytes 1048576 | tf_op jit(solution)/shard_map/all_to_all | solution.py:38
  57.3 25.1 %collective-permute-start = (f32[1,32,32]{1,2,0:T(8,128)S(1)}, f32[1,32,32]{1,2,0:T(8,128)S(1)}, u32[]{:S(2)}, u32[]{:S(2)}) collective-permute-start(f32[1,32,32]{1,2,0:T(8,128)S(1)} %fusion.17), channel_id=1, source_target_pairs={{0,32},{32,0},{64,96},{96,64},{128,160},{160,128},{192,224},{224,1... | collective-permute-start | bytes 12296 | tf_op jit(solution)/shard_map/ppermute | solution.py:51
  82.4 6.7 %collective-permute-start.1 = (f32[2,32,32]{1,2,0:T(8,128)S(1)}, f32[2,32,32]{1,2,0:T(8,128)S(1)}, u32[]{:S(2)}, u32[]{:S(2)}) collective-permute-start(f32[2,32,32]{1,2,0:T(8,128)S(1)} %maximum_select_fusion.6), channel_id=1, source_target_pairs={{0,64},{32,96},{64,0},{96,32},{128,192},{160,224},{192,128},{224,1... | collective-permute-start | bytes 24584 | tf_op jit(solution)/shard_map/ppermute | solution.py:51
  89.1 12.3 %collective-permute-start.2 = (f32[4,32,32]{1,2,0:T(8,128)S(1)}, f32[4,32,32]{1,2,0:T(8,128)S(1)}, u32[]{:S(2)}, u32[]{:S(2)}) collective-permute-start(f32[4,32,32]{1,2,0:T(8,128)S(1)} %maximum_select_fusion.4), channel_id=1, source_target_pairs={{0,128},{32,160},{64,192},{96,224},{128,0},{160,32},{192,64},{224,... | collective-permute-start | bytes 49160 | tf_op jit(solution)/shard_map/ppermute | solution.py:51
  101.4 19.6 %collective-permute-start.3 = (f32[8,32,32]{1,2,0:T(8,128)S(1)}, f32[8,32,32]{1,2,0:T(8,128)S(1)}, u32[]{:S(2)}, u32[]{:S(2)}) collective-permute-start(f32[8,32,32]{1,2,0:T(8,128)S(1)} %maximum_select_fusion.2), channel_id=1, source_target_pairs={{0,256},{32,288},{64,320},{96,352},{128,384},{160,416},{192,448},{... | collective-permute-start | bytes 98312 | tf_op jit(solution)/shard_map/ppermute | solution.py:51
  194.6 38.8 %copy-start.2 = (f32[32,32]{1,0:T(8,128)S(1)}, f32[32,32]{1,0:T(8,128)}, u32[]{:S(2)}) copy-start(f32[32,32]{1,0:T(8,128)} %shard_map.68) | copy-start | bytes 12292
  196.0 72.2 %all-to-all-start.1 = ((bf16[32,16,512]{2,0,1:T(8,128)(2,1)}), bf16[32,16,512]{2,0,1:T(8,128)(2,1)S(1)}, u32[]{:S(2)}, u32[]{:S(2)}) async-start(bf16[32,16,512]{2,0,1:T(8,128)(2,1)} %bitcast.52), calls=%async_computation.1 | async-start | bytes 1048576 | tf_op jit(solution)/shard_map/all_to_all | solution.py:38
  204.6 25.1 %collective-permute-start.4 = (f32[1,32,32]{1,2,0:T(8,128)S(1)}, f32[1,32,32]{1,2,0:T(8,128)S(1)}, u32[]{:S(2)}, u32[]{:S(2)}) collective-permute-start(f32[1,32,32]{1,2,0:T(8,128)S(1)} %fusion.16), channel_id=1, source_target_pairs={{0,32},{32,0},{64,96},{96,64},{128,160},{160,128},{192,224},{224,1... | collective-permute-start | bytes 12296 | tf_op jit(solution)/shard_map/ppermute | solution.py:51
  229.8 6.8 %collective-permute-start.5 = (f32[2,32,32]{1,2,0:T(8,128)S(1)}, f32[2,32,32]{1,2,0:T(8,128)S(1)}, u32[]{:S(2)}, u32[]{:S(2)}) collective-permute-start(f32[2,32,32]{1,2,0:T(8,128)S(1)} %maximum_select_fusion.7), channel_id=1, source_target_pairs={{0,64},{32,96},{64,0},{96,32},{128,192},{160,224},{192,128},{224,1... | collective-permute-start | bytes 24584 | tf_op jit(solution)/shard_map/ppermute | solution.py:51
  236.6 12.8 %collective-permute-start.6 = (f32[4,32,32]{1,2,0:T(8,128)S(1)}, f32[4,32,32]{1,2,0:T(8,128)S(1)}, u32[]{:S(2)}, u32[]{:S(2)}) collective-permute-start(f32[4,32,32]{1,2,0:T(8,128)S(1)} %maximum_select_fusion.5), channel_id=1, source_target_pairs={{0,128},{32,160},{64,192},{96,224},{128,0},{160,32},{192,64},{224,... | collective-permute-start | bytes 49160 | tf_op jit(solution)/shard_map/ppermute | solution.py:51
  249.4 18.6 %collective-permute-start.7 = (f32[8,32,32]{1,2,0:T(8,128)S(1)}, f32[8,32,32]{1,2,0:T(8,128)S(1)}, u32[]{:S(2)}, u32[]{:S(2)}) collective-permute-start(f32[8,32,32]{1,2,0:T(8,128)S(1)} %maximum_select_fusion.3), channel_id=1, source_target_pairs={{0,256},{32,288},{64,320},{96,352},{128,384},{160,416},{192,448},{... | collective-permute-start | bytes 98312 | tf_op jit(solution)/shard_map/ppermute | solution.py:51
  268.2 38.6 %copy-start.4 = (f32[32,32]{1,0:T(8,128)}, f32[32,32]{1,0:T(8,128)S(1)}, u32[]{:S(2)}) copy-start(f32[32,32]{1,0:T(8,128)S(1)} %add.43) | copy-start | bytes 12292

commit v8 on v6

--- a/solution.py
+++ b/solution.py
@@ -34,18 +34,24 @@
 def aux_sum(terms, small):
     n_aux = lax.axis_size("aux")
     rows, cols = terms.shape
+    k = small.shape[0]
+    upper = lax.broadcasted_iota(jnp.int32, (k, k), 1) >= lax.broadcasted_iota(jnp.int32, (k, k), 0)
     high = small.astype(jnp.bfloat16)
     low = (small - high.astype(jnp.float32)).astype(jnp.bfloat16)
-    extra = jnp.concatenate([high, low], axis=1)
+    packed = jnp.where(upper, high, low.T)
+    extra = jnp.concatenate([packed, jnp.diagonal(low)[:, None]], axis=1)
     pieces = jnp.concatenate([
         terms.reshape(rows, n_aux, cols // n_aux),
-        jnp.broadcast_to(extra[:, None, :], (rows, n_aux, extra.shape[1])),
+        jnp.broadcast_to(extra[:, None, :], (rows, n_aux, k + 1)),
     ], axis=2)
     pieces = lax.all_to_all(pieces, "aux", 1, 1, tiled=True)
     mine = pieces[:, :, : cols // n_aux].astype(jnp.float32).sum(1).astype(jnp.bfloat16)
-    parts = pieces[:, :, cols // n_aux:].astype(jnp.float32)
-    width = small.shape[1]
-    small_sum = (parts[:, :, :width] + parts[:, :, width:]).sum(1)
+    got = pieces[:, :, cols // n_aux:].astype(jnp.float32).sum(1)
+    got_packed = got[:, :k]
+    got_high = jnp.where(upper, got_packed, got_packed.T)
+    got_low = jnp.where(upper, got_packed.T, got_packed)
+    got_low = jnp.where(upper & upper.T, jnp.diag(got[:, k]), got_low)
+    small_sum = got_high + got_low
     return lax.all_gather(mine, "aux", axis=1, tiled=True).astype(jnp.float32), small_sum
 
 

time: 249 us -> 252 us (1.012)
  local copies, waits for them, and re-layouts: 3.7 us -> 6.55 us
where the time goes in v8:
time: 252 us; the launch traced here: 251 us
  blocking collectives  123 us (49%)
  waiting for transfers between devices  64.2 us (25%)
  matrix products  22 us (9%)
  starting transfers between devices  17.2 us (7%)
  Pallas kernels  9.79 us (4%)
  other arithmetic  7.94 us (3%)
  local copies, waits for them, and re-layouts  6.55 us (3%)
    all_gather x2, blocking collectives, aux_sum(): lax.all_gather(mine, 'aux', axis=1, tiled=True).astype(jnp.float32)  67.2 us
    all_to_all x2, waiting for transfers between devices, aux_sum(): pieces = lax.all_to_all(pieces, 'aux', 1, 1, tiled=True)  64.2 us
    all_gather x2, blocking collectives, pair_sum(): return lax.all_gather(matrices, 'pair').sum(0)  55.5 us
    all_to_all x2, starting transfers between devices, aux_sum(): pieces = lax.all_to_all(pieces, 'aux', 1, 1, tiled=True)  17.2 us
    dot_general x8, matrix products, product(): jnp.dot(first_mat, second_mat, precision=HIGHEST_PRECISION, preferred_ele...  13.4 us
    pallas_call x2, Pallas kernels, inverse_factor(): pl.pallas_call(_inverse_factor_kernel, out_shape=jax.ShapeDtypeStruct((k,...  9.79 us
  transfers between devices with their start and end apart: 2, of which 2 were waited for; matrix products, arithmetic and copies ran while one was open for 2% of the time, Pallas kernels for 0%

profile of v8, /device:TPU:2, one launch (start us, length us, event | category | flops | bytes accessed | tf_op | source)
XLA Modules:
  0.0 251.3 jit_solution(997453674648268276)
XLA Ops:
  2.4 2.0 fusion.43
  5.4 30.0 %all-gather.2 = f32[32,224,32]{1,2,0:T(8,128)} all-gather(f32[1,224,32]{1,2,0:T(8,128)S(1)} %maximum_bitcast_fusion), channel_id=2, replica_groups=mesh['aux'=16,'pair'=32] {'pair'}, dimensions={0}, use_global_device_ids=true | all-gather | bytes 946176 | tf_op jit(solution)/shard_map/all_gather | solution.py:31
  35.4 1.3 reduce_sum.60
  37.4 4.9 %shard_map.67 = f32[32,32]{1,0:T(8,128)} custom-call(f32[32,32]{1,0:T(8,128)} %copy.69.gram_ref), custom_call_target="tpu_custom_call" | custom-call | tf_op jit(solution)/shard_map/pallas_call | solution.py:82
  42.3 0.9 fusion.19
  43.4 1.3 convolution_convert_fusion.1
  45.7 1.1 copy.79
  47.8 12.4 %all-to-all-start = ((bf16[32,16,545]{2,0,1:T(8,128)(2,1)}), bf16[32,16,545]{2,0,1:T(8,128)(2,1)}, u32[]{:S(2)}, u32[]{:S(2)}) async-start(bf16[32,16,545]{2,0,1:T(8,128)(2,1)} %pad_maximum_fusion.3), calls=%async_computation | async-start | bytes 1310720 | tf_op jit(solution)/shard_map/all_to_all | solution.py:47
  60.4 1.5 fusion.44
  62.0 33.0 %all-to-all-done = bf16[32,16,545]{2,0,1:T(8,128)(2,1)} async-done(((bf16[32,16,545]{2,0,1:T(8,128)(2,1)}), bf16[32,16,545]{2,0,1:T(8,128)(2,1)}, u32[]{:S(2)}, u32[]{:S(2)}) %all-to-all-start) | async-done | bytes 558112 | tf_op jit(solution)/shard_map/all_to_all | solution.py:47
  95.0 0.9 convert_reduce_fusion.1
  96.2 1.1 slice_reduce_fusion.1
  97.3 33.6 %all_gather.20 = bf16[32,8192]{1,0:T(8,128)(2,1)S(1)} all-gather(bf16[32,512]{1,0:T(8,128)(2,1)S(1)} %slice_reduce_fusion.1), channel_id=1, replica_groups=mesh['aux'=16,'pair'=32] {'aux'}, dimensions={1}, use_global_device_ids=true | all-gather | bytes 557056 | tf_op jit(solution)/shard_map/all_gather | solution.py:55
  131.1 4.0 %multiply_convert_fusion = (bf16[32,8192]{1,0:T(8,128)(2,1)S(1)}, bf16[32,8192]{1,0:T(8,128)(2,1)S(1)}, bf16[32,8192]{1,0:T(8,128)(2,1)S(1)}, bf16[32,8192]{1,0:T(8,128)(2,1)S(1)}, f32[32,8192]{1,0:T(8,128)}) fusion(f32[8192]{0:T(1024)S(1)} %bitcast.98, f32[32,8192]{1,0:T(8,128)} %fusion.44, f32[32,32]{0,1:T(8,128)S(1)} %convolution_add_fusion.1, ...), kind=kOutput, calls=%fused_computation.34 | convolution fusion | flops 104595456 | bytes 4755456 | tf_op jit(solution)/shard_map/dot_general | solution.py:25
  135.0 1.0 convolution_bitcast_fusion
  137.0 25.5 %all-gather.3 = f32[32,224,32]{1,2,0:T(8,128)} all-gather(f32[1,224,32]{1,2,0:T(8,128)S(1)} %maximum_bitcast_fusion.1), channel_id=3, replica_groups=mesh['aux'=16,'pair'=32] {'pair'}, dimensions={0}, use_global_device_ids=true | all-gather | bytes 946176 | tf_op jit(solution)/shard_map/all_gather | solution.py:31
  162.5 1.3 reduce_sum.63
  164.5 4.9 %shard_map.68 = f32[32,32]{1,0:T(8,128)} custom-call(f32[32,32]{1,0:T(8,128)} %copy.71.gram_ref), custom_call_target="tpu_custom_call" | custom-call | tf_op jit(solution)/shard_map/pallas_call | solution.py:82
  169.4 0.9 fusion.17
  173.1 4.8 %all-to-all-start.1 = ((bf16[32,16,545]{2,0,1:T(8,128)(2,1)}), bf16[32,16,545]{2,0,1:T(8,128)(2,1)S(1)}, u32[]{:S(2)}, u32[]{:S(2)}) async-start(bf16[32,16,545]{2,0,1:T(8,128)(2,1)} %pad_maximum_fusion.4), calls=%async_computation.1 | async-start | bytes 1310720 | tf_op jit(solution)/shard_map/all_to_all | solution.py:47
  178.1 3.3 %fusion.45 = f32[32,8192]{1,0:T(8,128)} fusion(f32[32,32]{1,0:T(8,128)S(1)} %copy-done.3, f32[32,8192]{1,0:T(8,128)} %get-tuple-element.32), kind=kOutput, calls=%fused_computation.100 | convolution fusion | flops 100663296 | bytes 2101248 | tf_op jit(solution)/shard_map/dot_general | solution.py:25
  181.3 31.2 %all-to-all-done.1 = bf16[32,16,545]{2,0,1:T(8,128)(2,1)S(1)} async-done(((bf16[32,16,545]{2,0,1:T(8,128)(2,1)}), bf16[32,16,545]{2,0,1:T(8,128)(2,1)S(1)}, u32[]{:S(2)}, u32[]{:S(2)}) %all-to-all-start.1) | async-done | bytes 558112 | tf_op jit(solution)/shard_map/all_to_all | solution.py:47
  213.7 33.6 %all_gather.23 = bf16[32,8192]{1,0:T(8,128)(2,1)S(1)} all-gather(bf16[32,512]{1,0:T(8,128)(2,1)S(1)} %slice_reduce_fusion), channel_id=1, replica_groups=mesh['aux'=16,'pair'=32] {'aux'}, dimensions={1}, use_global_device_ids=true | all-gather | bytes 557056 | tf_op jit(solution)/shard_map/all_gather | solution.py:55
  247.4 4.0 %fusion.42 = (bf16[32,8192]{1,0:T(8,128)(2,1)}, f32[32,8192]{1,0:T(8,128)}) fusion(f32[32,8192]{1,0:T(8,128)} %fusion.45, f32[8192]{0:T(1024)S(1)} %bitcast.99, f32[32,32]{0,1:T(8,128)S(1)} %convolution_add_fusion, bf16[32,8192]{1,0:T(8,128)(2,1)S(1)} %all_gather.23), kind=kOutput, calls=%fused_computation.97 | convolution fusion | flops 102498304 | bytes 3182592 | tf_op jit(solution)/shard_map/dot_general | solution.py:25
  (53 shorter events, 11.8 us)
Async XLA Ops:
  0.6 1.8 copy-start
  0.6 3.7 %copy-start.1 = (bf16[32,8192]{1,0:T(8,128)(2,1)S(1)}, bf16[32,8192]{1,0:T(8,128)(2,1)}, u32[]{:S(2)}) copy-start(bf16[32,8192]{1,0:T(8,128)(2,1)} %param.7) | copy-start | bytes 1572868
  44.8 15.4 %copy-start.2 = (f32[32,32]{1,0:T(8,128)S(1)}, f32[32,32]{1,0:T(8,128)}, u32[]{:S(2)}) copy-start(f32[32,32]{1,0:T(8,128)} %shard_map.67) | copy-start | bytes 12292
  47.8 47.2 %all-to-all-start = ((bf16[32,16,545]{2,0,1:T(8,128)(2,1)}), bf16[32,16,545]{2,0,1:T(8,128)(2,1)}, u32[]{:S(2)}, u32[]{:S(2)}) async-start(bf16[32,16,545]{2,0,1:T(8,128)(2,1)} %pad_maximum_fusion.3), calls=%async_computation | async-start | bytes 1310720 | tf_op jit(solution)/shard_map/all_to_all | solution.py:47
  171.1 6.8 %copy-start.3 = (f32[32,32]{1,0:T(8,128)S(1)}, f32[32,32]{1,0:T(8,128)}, u32[]{:S(2)}) copy-start(f32[32,32]{1,0:T(8,128)} %shard_map.68) | copy-start | bytes 12292
  173.1 39.5 %all-to-all-start.1 = ((bf16[32,16,545]{2,0,1:T(8,128)(2,1)}), bf16[32,16,545]{2,0,1:T(8,128)(2,1)S(1)}, u32[]{:S(2)}, u32[]{:S(2)}) async-start(bf16[32,16,545]{2,0,1:T(8,128)(2,1)} %pad_maximum_fusion.4), calls=%async_computation.1 | async-start | bytes 1310720 | tf_op jit(solution)/shard_map/all_to_all | solution.py:47

commit v9 on v6

--- a/solution.py
+++ b/solution.py
@@ -24,6 +24,18 @@
 def product(first_mat, second_mat):
     return jnp.dot(
         first_mat, second_mat, precision=HIGHEST_PRECISION, preferred_element_type=jnp.float32
+    )
+
+
+def split_product(first_mat, second_mat):
+    first_high = first_mat.astype(jnp.bfloat16)
+    first_low = (first_mat - first_high.astype(jnp.float32)).astype(jnp.bfloat16)
+    second_high = second_mat.astype(jnp.bfloat16)
+    second_low = (second_mat - second_high.astype(jnp.float32)).astype(jnp.bfloat16)
+    return jnp.dot(
+        jnp.concatenate([first_high, first_low, first_high], axis=1),
+        jnp.concatenate([second_high, second_high, second_low], axis=0),
+        preferred_element_type=jnp.float32,
     )
 
 
@@ -120,7 +132,7 @@
         summed = pair_sum(jnp.concatenate(
             [gram_part / npair_all, weighted_part / npair_all, cross_part], axis=0))
         inverse = inverse_factor(summed[:k])
-        basis_now = product(inverse, wide_trial)
+        basis_now = split_product(inverse, wide_trial)
         projected = lax.dot_general(
             summed[2 * k:], inverse, (((1,), (1,)), ((), ())),
             precision=HIGHEST_PRECISION, preferred_element_type=jnp.float32,
@@ -137,7 +149,7 @@
         coupling, group_sum = aux_sum(term, group_part / npair_all)
         subspace = group_sum + diag_part
         image_now = coupling + diag_row * basis_now
-        residual = image_now - product(subspace, basis_now)
+        residual = image_now - split_product(subspace, basis_now)
         trial_now = basis_now - residual / diag_row
     return (trial_now, residual.astype(jnp.bfloat16), subspace)
 

time: 249 us -> 245 us (0.984)
    dot_general x0 -> x4, matrix products: none -> 12.3 us  [split_product(): jnp.dot(jnp.concatenate([first_high, first_low, first_high], axis=1), jnp...]
    dot_general x8 -> x4, matrix products: 13.4 us -> 1.33 us  [product(): jnp.dot(first_mat, second_mat, precision=HIGHEST_PRECISION, preferred_ele...]
  transfers between devices with their start and end apart: 2 -> 2, of which waited for: 2 -> 2; matrix products, arithmetic and copies ran while one was open for 2% -> 3% of each run, Pallas kernels for 0% -> 0%
where the time goes in v9:
time: 245 us; the launch traced here: 244 us
  blocking collectives  123 us (50%)
  waiting for transfers between devices  62.7 us (26%)
  matrix products  21.3 us (9%)
  starting transfers between devices  17.2 us (7%)
  Pallas kernels  9.79 us (4%)
  other arithmetic  7.1 us (3%)
  local copies, waits for them, and re-layouts  2.66 us (1%)
    all_gather x2, blocking collectives, aux_sum(): lax.all_gather(mine, 'aux', axis=1, tiled=True).astype(jnp.float32)  67.2 us
    all_to_all x2, waiting for transfers between devices, aux_sum(): pieces = lax.all_to_all(pieces, 'aux', 1, 1, tiled=True)  62.7 us
    all_gather x2, blocking collectives, pair_sum(): return lax.all_gather(matrices, 'pair').sum(0)  55.5 us
    all_to_all x2, starting transfers between devices, aux_sum(): pieces = lax.all_to_all(pieces, 'aux', 1, 1, tiled=True)  17.2 us
    dot_general x4, matrix products, split_product(): jnp.dot(jnp.concatenate([first_high, first_low, first_high], axis=1), jnp...  12.3 us
    pallas_call x2, Pallas kernels, inverse_factor(): pl.pallas_call(_inverse_factor_kernel, out_shape=jax.ShapeDtypeStruct((k,...  9.79 us
  transfers between devices with their start and end apart: 2, of which 2 were waited for; matrix products, arithmetic and copies ran while one was open for 3% of the time, Pallas kernels for 0%

profile of v9, /device:TPU:2, one launch (start us, length us, event | category | flops | bytes accessed | tf_op | source)
XLA Modules:
  0.0 244.4 jit_solution(4391311180238542074)
XLA Ops:
  0.7 0.9 dynamic_slice.3
  2.4 2.0 fusion.83
  4.4 1.0 fusion.37
  6.3 30.0 %all-gather.2 = f32[32,224,32]{1,2,0:T(8,128)} all-gather(f32[1,224,32]{1,2,0:T(8,128)S(1)} %maximum_bitcast_fusion), channel_id=2, replica_groups=mesh['aux'=16,'pair'=32] {'pair'}, dimensions={0}, use_global_device_ids=true | all-gather | bytes 946176 | tf_op jit(solution)/shard_map/all_gather | solution.py:43
  36.3 1.3 reduce_sum.60
  38.3 4.9 %shard_map.67 = f32[32,32]{1,0:T(8,128)} custom-call(f32[32,32]{1,0:T(8,128)} %copy.21.gram_ref), custom_call_target="tpu_custom_call" | custom-call | tf_op jit(solution)/shard_map/pallas_call | solution.py:88
  43.2 0.9 fusion.44
  45.0 0.9 pad_maximum_fusion.5
  45.9 12.4 %all-to-all-start = ((bf16[32,16,576]{2,0,1:T(8,128)(2,1)}), bf16[32,16,576]{2,0,1:T(8,128)(2,1)S(1)}, u32[]{:S(2)}, u32[]{:S(2)}) async-start(bf16[32,16,576]{2,0,1:T(8,128)(2,1)} %pad_maximum_fusion.5), calls=%async_computation | async-start | bytes 1310720 | tf_op jit(solution)/shard_map/all_to_all | solution.py:56
  58.3 3.1 %subtract_convert_fusion.3 = (bf16[32,8192]{1,0:T(8,128)(2,1)}, bf16[32,8192]{1,0:T(8,128)(2,1)}, f32[32,8192]{1,0:T(8,128)}) fusion(bf16[32,8192]{1,0:T(8,128)(2,1)} %param.7, bf16[32,8192]{1,0:T(8,128)(2,1)} %get-tuple-element.21, bf16[32,32]{1,0:T(8,128)(2,1)S(1)} %get-tuple-element.31, bf16[32,32]{1,0:T(8,128)(2,1)S(1)} %get-tuple-element.30), kind=kOutput, calls=%fused_computation.56 | convolution fusion | flops 56117248 | bytes 3149824 | tf_op jit(solution)/shard_map/dot_general | solution.py:35
  61.7 31.3 %all-to-all-done = bf16[32,16,576]{2,0,1:T(8,128)(2,1)S(1)} async-done(((bf16[32,16,576]{2,0,1:T(8,128)(2,1)}), bf16[32,16,576]{2,0,1:T(8,128)(2,1)S(1)}, u32[]{:S(2)}, u32[]{:S(2)}) %all-to-all-start) | async-done | bytes 589856 | tf_op jit(solution)/shard_map/all_to_all | solution.py:56
  93.3 33.6 %all_gather.20 = bf16[32,8192]{1,0:T(8,128)(2,1)S(1)} all-gather(bf16[32,512]{1,0:T(8,128)(2,1)S(1)} %slice_reduce_fusion.1), channel_id=1, replica_groups=mesh['aux'=16,'pair'=32] {'aux'}, dimensions={1}, use_global_device_ids=true | all-gather | bytes 557056 | tf_op jit(solution)/shard_map/all_gather | solution.py:61
  127.0 2.5 %multiply_convert_fusion = (bf16[32,8192]{1,0:T(8,128)(2,1)S(1)}, bf16[32,8192]{1,0:T(8,128)(2,1)S(1)}, bf16[32,8192]{1,0:T(8,128)(2,1)S(1)}, bf16[32,8192]{1,0:T(8,128)(2,1)S(1)}) fusion(f32[8192]{0:T(1024)S(1)} %bitcast.42, f32[32,8192]{1,0:T(8,128)} %get-tuple-element.34, bf16[32,8192]{1,0:T(8,128)(2,1)} %get-tuple-element.11, ...), kind=kOutput, calls=%fused_computation.57 | convolution fusion | flops 59000832 | bytes 4755456 | tf_op jit(solution)/shard_map/dot_general | solution.py:35
  129.5 1.0 convolution_bitcast_fusion
  131.6 25.5 %all-gather.3 = f32[32,224,32]{1,2,0:T(8,128)} all-gather(f32[1,224,32]{1,2,0:T(8,128)S(1)} %maximum_bitcast_fusion.1), channel_id=3, replica_groups=mesh['aux'=16,'pair'=32] {'pair'}, dimensions={0}, use_global_device_ids=true | all-gather | bytes 946176 | tf_op jit(solution)/shard_map/all_gather | solution.py:43
  157.1 1.3 reduce_sum.63
  159.1 4.9 %shard_map.68 = f32[32,32]{1,0:T(8,128)} custom-call(f32[32,32]{1,0:T(8,128)} %copy.22.gram_ref), custom_call_target="tpu_custom_call" | custom-call | tf_op jit(solution)/shard_map/pallas_call | solution.py:88
  164.0 0.9 fusion.42
  165.8 0.9 pad_maximum_fusion.6
  166.8 4.8 %all-to-all-start.1 = ((bf16[32,16,576]{2,0,1:T(8,128)(2,1)}), bf16[32,16,576]{2,0,1:T(8,128)(2,1)S(1)}, u32[]{:S(2)}, u32[]{:S(2)}) async-start(bf16[32,16,576]{2,0,1:T(8,128)(2,1)} %pad_maximum_fusion.6), calls=%async_computation.1 | async-start | bytes 1310720 | tf_op jit(solution)/shard_map/all_to_all | solution.py:56
  171.6 3.1 %subtract_convert_fusion = (bf16[32,8192]{1,0:T(8,128)(2,1)}, bf16[32,8192]{1,0:T(8,128)(2,1)}, f32[32,8192]{1,0:T(8,128)}) fusion(bf16[32,8192]{1,0:T(8,128)(2,1)} %copy-done.4, bf16[32,8192]{1,0:T(8,128)(2,1)} %copy-done.5, bf16[32,32]{1,0:T(8,128)(2,1)S(1)} %get-tuple-element.27, bf16[32,32]{1,0:T(8,128)(2,1)S(1)} %get-tuple-element.26), kind=kOutput, calls=%fused_computation.53 | convolution fusion | flops 56117248 | bytes 3149824 | tf_op jit(solution)/shard_map/dot_general | solution.py:35
  174.9 31.3 %all-to-all-done.1 = bf16[32,16,576]{2,0,1:T(8,128)(2,1)S(1)} async-done(((bf16[32,16,576]{2,0,1:T(8,128)(2,1)}), bf16[32,16,576]{2,0,1:T(8,128)(2,1)S(1)}, u32[]{:S(2)}, u32[]{:S(2)}) %all-to-all-start.1) | async-done | bytes 589856 | tf_op jit(solution)/shard_map/all_to_all | solution.py:56
  206.5 33.6 %all_gather.23 = bf16[32,8192]{1,0:T(8,128)(2,1)S(1)} all-gather(bf16[32,512]{1,0:T(8,128)(2,1)S(1)} %slice_reduce_fusion), channel_id=1, replica_groups=mesh['aux'=16,'pair'=32] {'aux'}, dimensions={1}, use_global_device_ids=true | all-gather | bytes 557056 | tf_op jit(solution)/shard_map/all_gather | solution.py:61
  240.9 3.5 %fusion.82 = (bf16[32,8192]{1,0:T(8,128)(2,1)}, f32[32,8192]{1,0:T(8,128)}) fusion(f32[32,8192]{1,0:T(8,128)} %get-tuple-element.36, f32[8192]{0:T(1024)S(1)} %bitcast.43, bf16[32,8192]{1,0:T(8,128)(2,1)} %get-tuple-element.5, bf16[32,8192]{1,0:T(8,128)(2,1)} %get-tuple-element.6, bf16[32,32]{1,0:T(8,128)(2,1)S(1)} %get-tuple-element.25, ...), kind=kOutput, calls=%fused_computation.129 | convolution fusion | flops 56903680 | bytes 4231168 | tf_op jit(solution)/shard_map/dot_general | solution.py:35
  (49 shorter events, 7.6 us)
Async XLA Ops:
  0.6 1.8 copy-start
  0.6 3.7 %copy-start.1 = (bf16[32,8192]{1,0:T(8,128)(2,1)S(1)}, bf16[32,8192]{1,0:T(8,128)(2,1)}, u32[]{:S(2)}) copy-start(bf16[32,8192]{1,0:T(8,128)(2,1)} %param.7) | copy-start | bytes 1572868
  44.8 13.5 %copy-start.3 = (f32[32,32]{1,0:T(8,128)S(1)}, f32[32,32]{1,0:T(8,128)}, u32[]{:S(2)}) copy-start(f32[32,32]{1,0:T(8,128)} %shard_map.67) | copy-start | bytes 12292
  45.9 47.1 %all-to-all-start = ((bf16[32,16,576]{2,0,1:T(8,128)(2,1)}), bf16[32,16,576]{2,0,1:T(8,128)(2,1)S(1)}, u32[]{:S(2)}, u32[]{:S(2)}) async-start(bf16[32,16,576]{2,0,1:T(8,128)(2,1)} %pad_maximum_fusion.5), calls=%async_computation | async-start | bytes 1310720 | tf_op jit(solution)/shard_map/all_to_all | solution.py:56
  129.5 1.9 copy-start.4
  129.5 1.9 copy-start.5
  165.6 5.9 %copy-start.2 = (f32[32,32]{1,0:T(8,128)S(1)}, f32[32,32]{1,0:T(8,128)}, u32[]{:S(2)}) copy-start(f32[32,32]{1,0:T(8,128)} %shard_map.68) | copy-start | bytes 12292
  166.8 39.5 %all-to-all-start.1 = ((bf16[32,16,576]{2,0,1:T(8,128)(2,1)}), bf16[32,16,576]{2,0,1:T(8,128)(2,1)S(1)}, u32[]{:S(2)}, u32[]{:S(2)}) async-start(bf16[32,16,576]{2,0,1:T(8,128)(2,1)} %pad_maximum_fusion.6), calls=%async_computation.1 | async-start | bytes 1310720 | tf_op jit(solution)/shard_map/all_to_all | solution.py:56

commit v10 on v9

--- a/solution.py
+++ b/solution.py
@@ -132,7 +132,7 @@
         summed = pair_sum(jnp.concatenate(
             [gram_part / npair_all, weighted_part / npair_all, cross_part], axis=0))
         inverse = inverse_factor(summed[:k])
-        basis_now = split_product(inverse, wide_trial)
+        basis_now = product(inverse, wide_trial)
         projected = lax.dot_general(
             summed[2 * k:], inverse, (((1,), (1,)), ((), ())),
             precision=HIGHEST_PRECISION, preferred_element_type=jnp.float32,

time: 245 us -> 249 us (1.016)
    dot_general x4 -> x6, matrix products: 1.33 us -> 6.78 us  [product(): jnp.dot(first_mat, second_mat, precision=HIGHEST_PRECISION, preferred_ele...]
    dot_general x4 -> x2, matrix products: 12.3 us -> 7.05 us  [split_product(): jnp.dot(jnp.concatenate([first_high, first_low, first_high], axis=1), jnp...]
  transfers between devices with their start and end apart: 2 -> 2, of which waited for: 2 -> 2; matrix products, arithmetic and copies ran while one was open for 3% -> 2% of each run, Pallas kernels for 0% -> 0%
where the time goes in v10:
time: 249 us; the launch traced here: 248 us
  blocking collectives  123 us (49%)
  waiting for transfers between devices  63.6 us (26%)
  matrix products  22.3 us (9%)
  starting transfers between devices  17.2 us (7%)
  Pallas kernels  9.79 us (4%)
  other arithmetic  8.18 us (3%)
  local copies, waits for them, and re-layouts  3.69 us (1%)
    all_gather x2, blocking collectives, aux_sum(): lax.all_gather(mine, 'aux', axis=1, tiled=True).astype(jnp.float32)  67.2 us
    all_to_all x2, waiting for transfers between devices, aux_sum(): pieces = lax.all_to_all(pieces, 'aux', 1, 1, tiled=True)  63.6 us
    all_gather x2, blocking collectives, pair_sum(): return lax.all_gather(matrices, 'pair').sum(0)  55.5 us
    all_to_all x2, starting transfers between devices, aux_sum(): pieces = lax.all_to_all(pieces, 'aux', 1, 1, tiled=True)  17.2 us
    pallas_call x2, Pallas kernels, inverse_factor(): pl.pallas_call(_inverse_factor_kernel, out_shape=jax.ShapeDtypeStruct((k,...  9.79 us
    dot_general x2, matrix products, split_product(): jnp.dot(jnp.concatenate([first_high, first_low, first_high], axis=1), jnp...  7.05 us
    dot_general x6, matrix products, product(): jnp.dot(first_mat, second_mat, precision=HIGHEST_PRECISION, preferred_ele...  6.78 us
  transfers between devices with their start and end apart: 2, of which 2 were waited for; matrix products, arithmetic and copies ran while one was open for 2% of the time, Pallas kernels for 0%

profile of v10, /device:TPU:2, one launch (start us, length us, event | category | flops | bytes accessed | tf_op | source)
XLA Modules:
  0.0 248.4 jit_solution(18333368898559439942)
XLA Ops:
  2.4 2.0 fusion.58
  5.4 30.0 %all-gather.2 = f32[32,224,32]{1,2,0:T(8,128)} all-gather(f32[1,224,32]{1,2,0:T(8,128)S(1)} %maximum_bitcast_fusion), channel_id=2, replica_groups=mesh['aux'=16,'pair'=32] {'pair'}, dimensions={0}, use_global_device_ids=true | all-gather | bytes 946176 | tf_op jit(solution)/shard_map/all_gather | solution.py:43
  35.4 1.3 reduce_sum.60
  37.4 4.9 %shard_map.67 = f32[32,32]{1,0:T(8,128)} custom-call(f32[32,32]{1,0:T(8,128)} %copy.21.gram_ref), custom_call_target="tpu_custom_call" | custom-call | tf_op jit(solution)/shard_map/pallas_call | solution.py:88
  42.3 0.9 fusion.31
  43.4 1.3 convolution_convert_fusion.1
  44.8 1.1 copy.30
  46.9 12.4 %all-to-all-start = ((bf16[32,16,576]{2,0,1:T(8,128)(2,1)}), bf16[32,16,576]{2,0,1:T(8,128)(2,1)}, u32[]{:S(2)}, u32[]{:S(2)}) async-start(bf16[32,16,576]{2,0,1:T(8,128)(2,1)} %pad_maximum_fusion.3), calls=%async_computation | async-start | bytes 1310720 | tf_op jit(solution)/shard_map/all_to_all | solution.py:56
  59.6 1.9 subtract_convert_fusion.3
  61.5 32.6 %all-to-all-done = bf16[32,16,576]{2,0,1:T(8,128)(2,1)} async-done(((bf16[32,16,576]{2,0,1:T(8,128)(2,1)}), bf16[32,16,576]{2,0,1:T(8,128)(2,1)}, u32[]{:S(2)}, u32[]{:S(2)}) %all-to-all-start) | async-done | bytes 589856 | tf_op jit(solution)/shard_map/all_to_all | solution.py:56
  95.2 1.1 slice_reduce_fusion.1
  96.3 33.6 %all_gather.20 = bf16[32,8192]{1,0:T(8,128)(2,1)S(1)} all-gather(bf16[32,512]{1,0:T(8,128)(2,1)S(1)} %slice_reduce_fusion.1), channel_id=1, replica_groups=mesh['aux'=16,'pair'=32] {'aux'}, dimensions={1}, use_global_device_ids=true | all-gather | bytes 557056 | tf_op jit(solution)/shard_map/all_gather | solution.py:61
  130.1 3.5 %multiply_convert_fusion = (bf16[32,8192]{1,0:T(8,128)(2,1)S(1)}, bf16[32,8192]{1,0:T(8,128)(2,1)S(1)}, bf16[32,8192]{1,0:T(8,128)(2,1)S(1)}, bf16[32,8192]{1,0:T(8,128)(2,1)S(1)}, f32[32,8192]{1,0:T(8,128)}) fusion(f32[8192]{0:T(1024)S(1)} %bitcast.46, f32[32,8192]{1,0:T(8,128)} %get-tuple-element.29, bf16[32,8192]{1,0:T(8,128)(2,1)} %get-tuple-element.11, ...), kind=kOutput, calls=%fused_computation.44 | convolution fusion | flops 59000832 | bytes 5804032 | tf_op jit(solution)/shard_map/dot_general | solution.py:35
  133.6 1.0 convolution_bitcast_fusion
  135.6 25.5 %all-gather.3 = f32[32,224,32]{1,2,0:T(8,128)} all-gather(f32[1,224,32]{1,2,0:T(8,128)S(1)} %maximum_bitcast_fusion.1), channel_id=3, replica_groups=mesh['aux'=16,'pair'=32] {'pair'}, dimensions={0}, use_global_device_ids=true | all-gather | bytes 946176 | tf_op jit(solution)/shard_map/all_gather | solution.py:43
  161.1 1.3 reduce_sum.63
  163.1 4.9 %shard_map.68 = f32[32,32]{1,0:T(8,128)} custom-call(f32[32,32]{1,0:T(8,128)} %copy.22.gram_ref), custom_call_target="tpu_custom_call" | custom-call | tf_op jit(solution)/shard_map/pallas_call | solution.py:88
  168.0 0.9 fusion.29
  169.8 0.9 pad_maximum_fusion.4
  170.8 4.8 %all-to-all-start.1 = ((bf16[32,16,576]{2,0,1:T(8,128)(2,1)}), bf16[32,16,576]{2,0,1:T(8,128)(2,1)S(1)}, u32[]{:S(2)}, u32[]{:S(2)}) async-start(bf16[32,16,576]{2,0,1:T(8,128)(2,1)} %pad_maximum_fusion.4), calls=%async_computation.1 | async-start | bytes 1310720 | tf_op jit(solution)/shard_map/all_to_all | solution.py:56
  175.8 3.5 %subtract_convert_fusion = (bf16[32,8192]{1,0:T(8,128)(2,1)}, bf16[32,8192]{1,0:T(8,128)(2,1)}, f32[32,8192]{1,0:T(8,128)}) fusion(f32[32,32]{1,0:T(8,128)S(1)} %copy-done.2, f32[32,8192]{1,0:T(8,128)} %get-tuple-element.31), kind=kOutput, calls=%fused_computation.37 | convolution fusion | flops 101711872 | bytes 3149824 | tf_op jit(solution)/shard_map/dot_general | solution.py:25
  179.4 30.9 %all-to-all-done.1 = bf16[32,16,576]{2,0,1:T(8,128)(2,1)S(1)} async-done(((bf16[32,16,576]{2,0,1:T(8,128)(2,1)}), bf16[32,16,576]{2,0,1:T(8,128)(2,1)S(1)}, u32[]{:S(2)}, u32[]{:S(2)}) %all-to-all-start.1) | async-done | bytes 589856 | tf_op jit(solution)/shard_map/all_to_all | solution.py:56
  210.5 33.6 %all_gather.23 = bf16[32,8192]{1,0:T(8,128)(2,1)S(1)} all-gather(bf16[32,512]{1,0:T(8,128)(2,1)S(1)} %slice_reduce_fusion), channel_id=1, replica_groups=mesh['aux'=16,'pair'=32] {'aux'}, dimensions={1}, use_global_device_ids=true | all-gather | bytes 557056 | tf_op jit(solution)/shard_map/all_gather | solution.py:61
  244.9 3.5 %fusion.57 = (bf16[32,8192]{1,0:T(8,128)(2,1)}, f32[32,8192]{1,0:T(8,128)}) fusion(f32[32,8192]{1,0:T(8,128)} %get-tuple-element.32, f32[8192]{0:T(1024)S(1)} %bitcast.47, bf16[32,8192]{1,0:T(8,128)(2,1)} %get-tuple-element.5, bf16[32,8192]{1,0:T(8,128)(2,1)} %get-tuple-element.6, bf16[32,32]{1,0:T(8,128)(2,1)S(1)} %get-tuple-element.24, ...), kind=kOutput, calls=%fused_computation.102 | convolution fusion | flops 56903680 | bytes 4231168 | tf_op jit(solution)/shard_map/dot_general | solution.py:35
  (43 shorter events, 9.8 us)
Async XLA Ops:
  0.6 1.8 copy-start
  0.6 3.7 %copy-start.1 = (bf16[32,8192]{1,0:T(8,128)(2,1)S(1)}, bf16[32,8192]{1,0:T(8,128)(2,1)}, u32[]{:S(2)}) copy-start(bf16[32,8192]{1,0:T(8,128)(2,1)} %param.7) | copy-start | bytes 1572868
  44.7 14.6 %copy-start.3 = (f32[32,32]{1,0:T(8,128)S(1)}, f32[32,32]{1,0:T(8,128)}, u32[]{:S(2)}) copy-start(f32[32,32]{1,0:T(8,128)} %shard_map.67) | copy-start | bytes 12292
  46.9 47.2 %all-to-all-start = ((bf16[32,16,576]{2,0,1:T(8,128)(2,1)}), bf16[32,16,576]{2,0,1:T(8,128)(2,1)}, u32[]{:S(2)}, u32[]{:S(2)}) async-start(bf16[32,16,576]{2,0,1:T(8,128)(2,1)} %pad_maximum_fusion.3), calls=%async_computation | async-start | bytes 1310720 | tf_op jit(solution)/shard_map/all_to_all | solution.py:56
  169.6 6.0 %copy-start.2 = (f32[32,32]{1,0:T(8,128)S(1)}, f32[32,32]{1,0:T(8,128)}, u32[]{:S(2)}) copy-start(f32[32,32]{1,0:T(8,128)} %shard_map.68) | copy-start | bytes 12292
  170.8 39.5 %all-to-all-start.1 = ((bf16[32,16,576]{2,0,1:T(8,128)(2,1)}), bf16[32,16,576]{2,0,1:T(8,128)(2,1)S(1)}, u32[]{:S(2)}, u32[]{:S(2)}) async-start(bf16[32,16,576]{2,0,1:T(8,128)(2,1)} %pad_maximum_fusion.4), calls=%async_computation.1 | async-start | bytes 1310720 | tf_op jit(solution)/shard_map/all_to_all | solution.py:56

commit v11 on v9

--- a/solution.py
+++ b/solution.py
@@ -27,11 +27,14 @@
     )
 
 
+def split_bf16(values):
+    high_wide = lax.reduce_precision(values, exponent_bits=8, mantissa_bits=7)
+    return high_wide.astype(jnp.bfloat16), (values - high_wide).astype(jnp.bfloat16)
+
+
 def split_product(first_mat, second_mat):
-    first_high = first_mat.astype(jnp.bfloat16)
-    first_low = (first_mat - first_high.astype(jnp.float32)).astype(jnp.bfloat16)
-    second_high = second_mat.astype(jnp.bfloat16)
-    second_low = (second_mat - second_high.astype(jnp.float32)).astype(jnp.bfloat16)
+    first_high, first_low = split_bf16(first_mat)
+    second_high, second_low = split_bf16(second_mat)
     return jnp.dot(
         jnp.concatenate([first_high, first_low, first_high], axis=1),
         jnp.concatenate([second_high, second_high, second_low], axis=0),
@@ -46,8 +49,7 @@
 def aux_sum(terms, small):
     n_aux = lax.axis_size("aux")
     rows, cols = terms.shape
-    high = small.astype(jnp.bfloat16)
-    low = (small - high.astype(jnp.float32)).astype(jnp.bfloat16)
+    high, low = split_bf16(small)
     extra = jnp.concatenate([high, low], axis=1)
     pieces = jnp.concatenate([
         terms.reshape(rows, n_aux, cols // n_aux),
@@ -111,8 +113,7 @@
     for iteration in range(ITERS):
         wide_trial = trial_now.astype(jnp.float32)
         weighted = wide_trial * diag_row
-        weighted_high = weighted.astype(jnp.bfloat16)
-        weighted_low = (weighted - weighted_high.astype(jnp.float32)).astype(jnp.bfloat16)
+        weighted_high, weighted_low = split_bf16(weighted)
         if iteration == 0:
             both = correlation_of(
                 jnp.concatenate([trial_now, weighted_high, weighted_low], axis=0), trial_now, None)
@@ -120,8 +121,7 @@
             weighted_part = both[k:2 * k] + both[2 * k:]
             cross_part = correlation_of(b_tensor, trial_now, None)
         else:
-            high = trial_now.astype(jnp.bfloat16)
-            low = (trial_now - high.astype(jnp.float32)).astype(jnp.bfloat16)
+            high, low = split_bf16(trial_now)
             split = jnp.concatenate([high, low], axis=0)
             both = correlation_of(
                 jnp.concatenate([high, low, weighted_high, weighted_low], axis=0), split, None)

time: 245 us -> 246 us (level)
  no operation moved by 1% of the time
where the time goes in v11:
time: 246 us; the launch traced here: 245 us
  blocking collectives  123 us (50%)
  waiting for transfers between devices  62.7 us (25%)
  matrix products  21.4 us (9%)
  starting transfers between devices  17.2 us (7%)
  Pallas kernels  9.79 us (4%)
  other arithmetic  7.25 us (3%)
  local copies, waits for them, and re-layouts  2.66 us (1%)
    all_gather x2, blocking collectives, aux_sum(): lax.all_gather(mine, 'aux', axis=1, tiled=True).astype(jnp.float32)  67.2 us
    all_to_all x2, waiting for transfers between devices, aux_sum(): pieces = lax.all_to_all(pieces, 'aux', 1, 1, tiled=True)  62.7 us
    all_gather x2, blocking collectives, pair_sum(): return lax.all_gather(matrices, 'pair').sum(0)  55.5 us
    all_to_all x2, starting transfers between devices, aux_sum(): pieces = lax.all_to_all(pieces, 'aux', 1, 1, tiled=True)  17.2 us
    dot_general x4, matrix products, split_product(): jnp.dot(jnp.concatenate([first_high, first_low, first_high], axis=1), jnp...  12.4 us
    pallas_call x2, Pallas kernels, inverse_factor(): pl.pallas_call(_inverse_factor_kernel, out_shape=jax.ShapeDtypeStruct((k,...  9.79 us
  transfers between devices with their start and end apart: 2, of which 2 were waited for; matrix products, arithmetic and copies ran while one was open for 3% of the time, Pallas kernels for 0%

profile of v11, /device:TPU:2, one launch (start us, length us, event | category | flops | bytes accessed | tf_op | source)
XLA Modules:
  0.0 244.7 jit_solution(16440013450139218912)
XLA Ops:
  0.7 0.9 dynamic_slice.3
  2.4 2.0 fusion.94
  4.4 1.2 reduce-precision_convert_fusion.4
  6.4 30.0 %all-gather.2 = f32[32,224,32]{1,2,0:T(8,128)} all-gather(f32[1,224,32]{1,2,0:T(8,128)S(1)} %maximum_bitcast_fusion), channel_id=2, replica_groups=mesh['aux'=16,'pair'=32] {'pair'}, dimensions={0}, use_global_device_ids=true | all-gather | bytes 946176 | tf_op jit(solution)/shard_map/all_gather | solution.py:46
  36.4 1.3 reduce_sum.60
  38.4 4.9 %shard_map.67 = f32[32,32]{1,0:T(8,128)} custom-call(f32[32,32]{1,0:T(8,128)} %copy.21.gram_ref), custom_call_target="tpu_custom_call" | custom-call | tf_op jit(solution)/shard_map/pallas_call | solution.py:90
  43.3 0.9 fusion.49
  45.2 0.9 pad_maximum_fusion.3
  46.1 12.4 %all-to-all-start = ((bf16[32,16,576]{2,0,1:T(8,128)(2,1)}), bf16[32,16,576]{2,0,1:T(8,128)(2,1)S(1)}, u32[]{:S(2)}, u32[]{:S(2)}) async-start(bf16[32,16,576]{2,0,1:T(8,128)(2,1)} %pad_maximum_fusion.3), calls=%async_computation | async-start | bytes 1310720 | tf_op jit(solution)/shard_map/all_to_all | solution.py:58
  58.5 3.1 %reduce-precision_convert_fusion.3 = (bf16[32,8192]{1,0:T(8,128)(2,1)}, bf16[32,8192]{1,0:T(8,128)(2,1)}, f32[32,8192]{1,0:T(8,128)}) fusion(bf16[32,8192]{1,0:T(8,128)(2,1)} %get-tuple-element.16, bf16[32,8192]{1,0:T(8,128)(2,1)} %get-tuple-element.15, bf16[32,32]{1,0:T(8,128)(2,1)S(1)} %get-tuple-element.30, bf16[32,32]{1,0:T(8,128)(2,1)S(1)} %get-tuple-element.29), kind=kOutput, calls=%fused_computation.53 | convolution fusion | flops 56117248 | bytes 3149824 | tf_op jit(solution)/shard_map/dot_general | solution.py:38
  61.8 31.3 %all-to-all-done = bf16[32,16,576]{2,0,1:T(8,128)(2,1)S(1)} async-done(((bf16[32,16,576]{2,0,1:T(8,128)(2,1)}), bf16[32,16,576]{2,0,1:T(8,128)(2,1)S(1)}, u32[]{:S(2)}, u32[]{:S(2)}) %all-to-all-start) | async-done | bytes 589856 | tf_op jit(solution)/shard_map/all_to_all | solution.py:58
  93.4 33.6 %all_gather.20 = bf16[32,8192]{1,0:T(8,128)(2,1)S(1)} all-gather(bf16[32,512]{1,0:T(8,128)(2,1)S(1)} %slice_reduce_fusion.1), channel_id=1, replica_groups=mesh['aux'=16,'pair'=32] {'aux'}, dimensions={1}, use_global_device_ids=true | all-gather | bytes 557056 | tf_op jit(solution)/shard_map/all_gather | solution.py:63
  127.2 2.6 %reduce-precision_convert_fusion.1 = (bf16[32,8192]{1,0:T(8,128)(2,1)S(1)}, bf16[32,8192]{1,0:T(8,128)(2,1)S(1)}, bf16[32,8192]{1,0:T(8,128)(2,1)S(1)}, bf16[32,8192]{1,0:T(8,128)(2,1)S(1)}) fusion(f32[8192]{0:T(1024)S(1)} %bitcast.42, f32[32,8192]{1,0:T(8,128)} %get-tuple-element.33, bf16[32,8192]{1,0:T(8,128)(2,1)} %get-tuple-element.12, ...), kind=kOutput, calls=%fused_computation.49 | convolution fusion | flops 59000832 | bytes 4755456 | tf_op jit(solution)/shard_map/dot_general | solution.py:38
  129.8 1.0 convolution_bitcast_fusion
  131.9 25.5 %all-gather.3 = f32[32,224,32]{1,2,0:T(8,128)} all-gather(f32[1,224,32]{1,2,0:T(8,128)S(1)} %maximum_bitcast_fusion.1), channel_id=3, replica_groups=mesh['aux'=16,'pair'=32] {'pair'}, dimensions={0}, use_global_device_ids=true | all-gather | bytes 946176 | tf_op jit(solution)/shard_map/all_gather | solution.py:46
  157.4 1.3 reduce_sum.63
  159.4 4.9 %shard_map.68 = f32[32,32]{1,0:T(8,128)} custom-call(f32[32,32]{1,0:T(8,128)} %copy.22.gram_ref), custom_call_target="tpu_custom_call" | custom-call | tf_op jit(solution)/shard_map/pallas_call | solution.py:90
  164.2 0.9 fusion.47
  166.1 0.9 pad_maximum_fusion.4
  167.0 4.8 %all-to-all-start.1 = ((bf16[32,16,576]{2,0,1:T(8,128)(2,1)}), bf16[32,16,576]{2,0,1:T(8,128)(2,1)S(1)}, u32[]{:S(2)}, u32[]{:S(2)}) async-start(bf16[32,16,576]{2,0,1:T(8,128)(2,1)} %pad_maximum_fusion.4), calls=%async_computation.1 | async-start | bytes 1310720 | tf_op jit(solution)/shard_map/all_to_all | solution.py:58
  171.9 3.1 %reduce-precision_convert_fusion = (bf16[32,8192]{1,0:T(8,128)(2,1)}, bf16[32,8192]{1,0:T(8,128)(2,1)}, f32[32,8192]{1,0:T(8,128)}) fusion(bf16[32,8192]{1,0:T(8,128)(2,1)} %copy-done.4, bf16[32,8192]{1,0:T(8,128)(2,1)} %copy-done.5, bf16[32,32]{1,0:T(8,128)(2,1)S(1)} %get-tuple-element.24, bf16[32,32]{1,0:T(8,128)(2,1)S(1)} %get-tuple-element.23), kind=kOutput, calls=%fused_computation.47 | convolution fusion | flops 56117248 | bytes 3149824 | tf_op jit(solution)/shard_map/dot_general | solution.py:38
  175.2 31.3 %all-to-all-done.1 = bf16[32,16,576]{2,0,1:T(8,128)(2,1)S(1)} async-done(((bf16[32,16,576]{2,0,1:T(8,128)(2,1)}), bf16[32,16,576]{2,0,1:T(8,128)(2,1)S(1)}, u32[]{:S(2)}, u32[]{:S(2)}) %all-to-all-start.1) | async-done | bytes 589856 | tf_op jit(solution)/shard_map/all_to_all | solution.py:58
  206.8 33.6 %all_gather.23 = bf16[32,8192]{1,0:T(8,128)(2,1)S(1)} all-gather(bf16[32,512]{1,0:T(8,128)(2,1)S(1)} %slice_reduce_fusion), channel_id=1, replica_groups=mesh['aux'=16,'pair'=32] {'aux'}, dimensions={1}, use_global_device_ids=true | all-gather | bytes 557056 | tf_op jit(solution)/shard_map/all_gather | solution.py:63
  241.2 3.6 %fusion.93 = (bf16[32,8192]{1,0:T(8,128)(2,1)}, f32[32,8192]{1,0:T(8,128)}) fusion(f32[32,8192]{1,0:T(8,128)} %get-tuple-element.34, f32[8192]{0:T(1024)S(1)} %bitcast.43, bf16[32,8192]{1,0:T(8,128)(2,1)} %get-tuple-element.8, bf16[32,8192]{1,0:T(8,128)(2,1)} %get-tuple-element.7, bf16[32,32]{1,0:T(8,128)(2,1)S(1)} %get-tuple-element.20, ...), kind=kOutput, calls=%fused_computation.152 | convolution fusion | flops 56903680 | bytes 4231168 | tf_op jit(solution)/shard_map/dot_general | solution.py:38
  (49 shorter events, 7.6 us)
Async XLA Ops:
  0.6 1.8 copy-start
  0.6 3.7 %copy-start.1 = (bf16[32,8192]{1,0:T(8,128)(2,1)S(1)}, bf16[32,8192]{1,0:T(8,128)(2,1)}, u32[]{:S(2)}) copy-start(bf16[32,8192]{1,0:T(8,128)(2,1)} %param.7) | copy-start | bytes 1572868
  45.0 13.5 %copy-start.3 = (f32[32,32]{1,0:T(8,128)S(1)}, f32[32,32]{1,0:T(8,128)}, u32[]{:S(2)}) copy-start(f32[32,32]{1,0:T(8,128)} %shard_map.67) | copy-start | bytes 12292
  46.1 47.1 %all-to-all-start = ((bf16[32,16,576]{2,0,1:T(8,128)(2,1)}), bf16[32,16,576]{2,0,1:T(8,128)(2,1)S(1)}, u32[]{:S(2)}, u32[]{:S(2)}) async-start(bf16[32,16,576]{2,0,1:T(8,128)(2,1)} %pad_maximum_fusion.3), calls=%async_computation | async-start | bytes 1310720 | tf_op jit(solution)/shard_map/all_to_all | solution.py:58
  129.8 1.9 copy-start.4
  129.8 1.9 copy-start.5
  165.9 5.9 %copy-start.2 = (f32[32,32]{1,0:T(8,128)S(1)}, f32[32,32]{1,0:T(8,128)}, u32[]{:S(2)}) copy-start(f32[32,32]{1,0:T(8,128)} %shard_map.68) | copy-start | bytes 12292
  167.0 39.5 %all-to-all-start.1 = ((bf16[32,16,576]{2,0,1:T(8,128)(2,1)}), bf16[32,16,576]{2,0,1:T(8,128)(2,1)S(1)}, u32[]{:S(2)}, u32[]{:S(2)}) async-start(bf16[32,16,576]{2,0,1:T(8,128)(2,1)} %pad_maximum_fusion.4), calls=%async_computation.1 | async-start | bytes 1310720 | tf_op jit(solution)/shard_map/all_to_all | solution.py:58

commit v12 on v11

--- a/solution.py
+++ b/solution.py
@@ -69,14 +69,13 @@
     rows = lax.broadcasted_iota(jnp.int32, (k, k), 0)
     lanes = lax.broadcasted_iota(jnp.int32, (k, k), 1)
     row_ids = lax.broadcasted_iota(jnp.int32, (k, 1), 0)
-    lane_ids = lax.broadcasted_iota(jnp.int32, (1, k), 1)
     inverse = (rows == lanes).astype(jnp.float32)
     for j in range(k):
         pick = rows == j
         column = jnp.sum(jnp.where(lanes == j, work, 0.0), axis=1, keepdims=True)
         work_row = jnp.sum(jnp.where(pick, work, 0.0), axis=0, keepdims=True)
         inverse_row = jnp.sum(jnp.where(pick, inverse, 0.0), axis=0, keepdims=True)
-        pivot = jnp.sum(jnp.where(lane_ids == j, work_row, 0.0), axis=1, keepdims=True)
+        pivot = jnp.sum(jnp.where(row_ids == j, column, 0.0), axis=0, keepdims=True)
         scale = 1.0 / jnp.sqrt(pivot)
         work_row = work_row * scale
         inverse_row = inverse_row * scale

time: 246 us -> 245 us (level)
  no operation moved by 1% of the time
where the time goes in v12:
time: 245 us
  blocking collectives  123 us (50%)
  waiting for transfers between devices  62.7 us (26%)
  matrix products  21.4 us (9%)
  starting transfers between devices  17.2 us (7%)
  Pallas kernels  9.72 us (4%)
  other arithmetic  7.25 us (3%)
  local copies, waits for them, and re-layouts  2.66 us (1%)
    all_gather x2, blocking collectives, aux_sum(): lax.all_gather(mine, 'aux', axis=1, tiled=True).astype(jnp.float32)  67.2 us
    all_to_all x2, waiting for transfers between devices, aux_sum(): pieces = lax.all_to_all(pieces, 'aux', 1, 1, tiled=True)  62.7 us
    all_gather x2, blocking collectives, pair_sum(): return lax.all_gather(matrices, 'pair').sum(0)  55.5 us
    all_to_all x2, starting transfers between devices, aux_sum(): pieces = lax.all_to_all(pieces, 'aux', 1, 1, tiled=True)  17.2 us
    dot_general x4, matrix products, split_product(): jnp.dot(jnp.concatenate([first_high, first_low, first_high], axis=1), jnp...  12.4 us
    pallas_call x2, Pallas kernels, inverse_factor(): pl.pallas_call(_inverse_factor_kernel, out_shape=jax.ShapeDtypeStruct((k,...  9.72 us
  transfers between devices with their start and end apart: 2, of which 2 were waited for; matrix products, arithmetic and copies ran while one was open for 3% of the time, Pallas kernels for 0%

profile of v12, /device:TPU:2, one launch (start us, length us, event | category | flops | bytes accessed | tf_op | source)
XLA Modules:
  0.0 244.6 jit_solution(17939910417946868622)
XLA Ops:
  0.7 0.9 dynamic_slice.3
  2.4 2.0 fusion.94
  4.4 1.2 reduce-precision_convert_fusion.4
  6.4 30.0 %all-gather.2 = f32[32,224,32]{1,2,0:T(8,128)} all-gather(f32[1,224,32]{1,2,0:T(8,128)S(1)} %maximum_bitcast_fusion), channel_id=2, replica_groups=mesh['aux'=16,'pair'=32] {'pair'}, dimensions={0}, use_global_device_ids=true | all-gather | bytes 946176 | tf_op jit(solution)/shard_map/all_gather | solution.py:46
  36.4 1.3 reduce_sum.60
  38.4 4.9 %shard_map.67 = f32[32,32]{1,0:T(8,128)} custom-call(f32[32,32]{1,0:T(8,128)} %copy.21.gram_ref), custom_call_target="tpu_custom_call" | custom-call | tf_op jit(solution)/shard_map/pallas_call | solution.py:89
  43.3 0.9 fusion.49
  45.1 0.9 pad_maximum_fusion.3
  46.1 12.4 %all-to-all-start = ((bf16[32,16,576]{2,0,1:T(8,128)(2,1)}), bf16[32,16,576]{2,0,1:T(8,128)(2,1)S(1)}, u32[]{:S(2)}, u32[]{:S(2)}) async-start(bf16[32,16,576]{2,0,1:T(8,128)(2,1)} %pad_maximum_fusion.3), calls=%async_computation | async-start | bytes 1310720 | tf_op jit(solution)/shard_map/all_to_all | solution.py:58
  58.5 3.1 %reduce-precision_convert_fusion.3 = (bf16[32,8192]{1,0:T(8,128)(2,1)}, bf16[32,8192]{1,0:T(8,128)(2,1)}, f32[32,8192]{1,0:T(8,128)}) fusion(bf16[32,8192]{1,0:T(8,128)(2,1)} %get-tuple-element.16, bf16[32,8192]{1,0:T(8,128)(2,1)} %get-tuple-element.15, bf16[32,32]{1,0:T(8,128)(2,1)S(1)} %get-tuple-element.30, bf16[32,32]{1,0:T(8,128)(2,1)S(1)} %get-tuple-element.29), kind=kOutput, calls=%fused_computation.53 | convolution fusion | flops 56117248 | bytes 3149824 | tf_op jit(solution)/shard_map/dot_general | solution.py:38
  61.8 31.3 %all-to-all-done = bf16[32,16,576]{2,0,1:T(8,128)(2,1)S(1)} async-done(((bf16[32,16,576]{2,0,1:T(8,128)(2,1)}), bf16[32,16,576]{2,0,1:T(8,128)(2,1)S(1)}, u32[]{:S(2)}, u32[]{:S(2)}) %all-to-all-start) | async-done | bytes 589856 | tf_op jit(solution)/shard_map/all_to_all | solution.py:58
  93.4 33.6 %all_gather.20 = bf16[32,8192]{1,0:T(8,128)(2,1)S(1)} all-gather(bf16[32,512]{1,0:T(8,128)(2,1)S(1)} %slice_reduce_fusion.1), channel_id=1, replica_groups=mesh['aux'=16,'pair'=32] {'aux'}, dimensions={1}, use_global_device_ids=true | all-gather | bytes 557056 | tf_op jit(solution)/shard_map/all_gather | solution.py:63
  127.2 2.6 %reduce-precision_convert_fusion.1 = (bf16[32,8192]{1,0:T(8,128)(2,1)S(1)}, bf16[32,8192]{1,0:T(8,128)(2,1)S(1)}, bf16[32,8192]{1,0:T(8,128)(2,1)S(1)}, bf16[32,8192]{1,0:T(8,128)(2,1)S(1)}) fusion(f32[8192]{0:T(1024)S(1)} %bitcast.42, f32[32,8192]{1,0:T(8,128)} %get-tuple-element.33, bf16[32,8192]{1,0:T(8,128)(2,1)} %get-tuple-element.12, ...), kind=kOutput, calls=%fused_computation.49 | convolution fusion | flops 59000832 | bytes 4755456 | tf_op jit(solution)/shard_map/dot_general | solution.py:38
  129.8 1.0 convolution_bitcast_fusion
  131.8 25.5 %all-gather.3 = f32[32,224,32]{1,2,0:T(8,128)} all-gather(f32[1,224,32]{1,2,0:T(8,128)S(1)} %maximum_bitcast_fusion.1), channel_id=3, replica_groups=mesh['aux'=16,'pair'=32] {'pair'}, dimensions={0}, use_global_device_ids=true | all-gather | bytes 946176 | tf_op jit(solution)/shard_map/all_gather | solution.py:46
  157.3 1.3 reduce_sum.63
  159.3 4.9 %shard_map.68 = f32[32,32]{1,0:T(8,128)} custom-call(f32[32,32]{1,0:T(8,128)} %copy.22.gram_ref), custom_call_target="tpu_custom_call" | custom-call | tf_op jit(solution)/shard_map/pallas_call | solution.py:89
  164.2 0.9 fusion.47
  166.0 0.9 pad_maximum_fusion.4
  167.0 4.8 %all-to-all-start.1 = ((bf16[32,16,576]{2,0,1:T(8,128)(2,1)}), bf16[32,16,576]{2,0,1:T(8,128)(2,1)S(1)}, u32[]{:S(2)}, u32[]{:S(2)}) async-start(bf16[32,16,576]{2,0,1:T(8,128)(2,1)} %pad_maximum_fusion.4), calls=%async_computation.1 | async-start | bytes 1310720 | tf_op jit(solution)/shard_map/all_to_all | solution.py:58
  171.8 3.1 %reduce-precision_convert_fusion = (bf16[32,8192]{1,0:T(8,128)(2,1)}, bf16[32,8192]{1,0:T(8,128)(2,1)}, f32[32,8192]{1,0:T(8,128)}) fusion(bf16[32,8192]{1,0:T(8,128)(2,1)} %copy-done.4, bf16[32,8192]{1,0:T(8,128)(2,1)} %copy-done.5, bf16[32,32]{1,0:T(8,128)(2,1)S(1)} %get-tuple-element.24, bf16[32,32]{1,0:T(8,128)(2,1)S(1)} %get-tuple-element.23), kind=kOutput, calls=%fused_computation.47 | convolution fusion | flops 56117248 | bytes 3149824 | tf_op jit(solution)/shard_map/dot_general | solution.py:38
  175.1 31.4 %all-to-all-done.1 = bf16[32,16,576]{2,0,1:T(8,128)(2,1)S(1)} async-done(((bf16[32,16,576]{2,0,1:T(8,128)(2,1)}), bf16[32,16,576]{2,0,1:T(8,128)(2,1)S(1)}, u32[]{:S(2)}, u32[]{:S(2)}) %all-to-all-start.1) | async-done | bytes 589856 | tf_op jit(solution)/shard_map/all_to_all | solution.py:58
  206.7 33.6 %all_gather.23 = bf16[32,8192]{1,0:T(8,128)(2,1)S(1)} all-gather(bf16[32,512]{1,0:T(8,128)(2,1)S(1)} %slice_reduce_fusion), channel_id=1, replica_groups=mesh['aux'=16,'pair'=32] {'aux'}, dimensions={1}, use_global_device_ids=true | all-gather | bytes 557056 | tf_op jit(solution)/shard_map/all_gather | solution.py:63
  241.1 3.6 %fusion.93 = (bf16[32,8192]{1,0:T(8,128)(2,1)}, f32[32,8192]{1,0:T(8,128)}) fusion(f32[32,8192]{1,0:T(8,128)} %get-tuple-element.34, f32[8192]{0:T(1024)S(1)} %bitcast.43, bf16[32,8192]{1,0:T(8,128)(2,1)} %get-tuple-element.8, bf16[32,8192]{1,0:T(8,128)(2,1)} %get-tuple-element.7, bf16[32,32]{1,0:T(8,128)(2,1)S(1)} %get-tuple-element.20, ...), kind=kOutput, calls=%fused_computation.152 | convolution fusion | flops 56903680 | bytes 4231168 | tf_op jit(solution)/shard_map/dot_general | solution.py:38
  (49 shorter events, 7.6 us)
Async XLA Ops:
  0.6 1.8 copy-start
  0.6 3.7 %copy-start.1 = (bf16[32,8192]{1,0:T(8,128)(2,1)S(1)}, bf16[32,8192]{1,0:T(8,128)(2,1)}, u32[]{:S(2)}) copy-start(bf16[32,8192]{1,0:T(8,128)(2,1)} %param.7) | copy-start | bytes 1572868
  44.9 13.5 %copy-start.3 = (f32[32,32]{1,0:T(8,128)S(1)}, f32[32,32]{1,0:T(8,128)}, u32[]{:S(2)}) copy-start(f32[32,32]{1,0:T(8,128)} %shard_map.67) | copy-start | bytes 12292
  46.1 47.1 %all-to-all-start = ((bf16[32,16,576]{2,0,1:T(8,128)(2,1)}), bf16[32,16,576]{2,0,1:T(8,128)(2,1)S(1)}, u32[]{:S(2)}, u32[]{:S(2)}) async-start(bf16[32,16,576]{2,0,1:T(8,128)(2,1)} %pad_maximum_fusion.3), calls=%async_computation | async-start | bytes 1310720 | tf_op jit(solution)/shard_map/all_to_all | solution.py:58
  129.8 1.9 copy-start.4
  129.8 1.9 copy-start.5
  165.8 5.9 %copy-start.2 = (f32[32,32]{1,0:T(8,128)S(1)}, f32[32,32]{1,0:T(8,128)}, u32[]{:S(2)}) copy-start(f32[32,32]{1,0:T(8,128)} %shard_map.68) | copy-start | bytes 12292
  167.0 39.5 %all-to-all-start.1 = ((bf16[32,16,576]{2,0,1:T(8,128)(2,1)}), bf16[32,16,576]{2,0,1:T(8,128)(2,1)S(1)}, u32[]{:S(2)}, u32[]{:S(2)}) async-start(bf16[32,16,576]{2,0,1:T(8,128)(2,1)} %pad_maximum_fusion.4), calls=%async_computation.1 | async-start | bytes 1310720 | tf_op jit(solution)/shard_map/all_to_all | solution.py:58

commit v13 on v12

--- a/solution.py
+++ b/solution.py
@@ -108,6 +108,7 @@
         diagonal = lax.dynamic_slice_in_dim(
             everything, lax.axis_index("pair") * block_cols, block_cols)
     diag_row = diagonal[None, :]
+    inverse_diag = (1.0 / diagonal)[None, :]
     trial_now = trial
     for iteration in range(ITERS):
         wide_trial = trial_now.astype(jnp.float32)
@@ -149,7 +150,7 @@
         subspace = group_sum + diag_part
         image_now = coupling + diag_row * basis_now
         residual = image_now - split_product(subspace, basis_now)
-        trial_now = basis_now - residual / diag_row
+        trial_now = basis_now - residual * inverse_diag
     return (trial_now, residual.astype(jnp.bfloat16), subspace)
 
 

time: 245 us -> 245 us (level)
  no operation moved by 1% of the time
where the time goes in v13:
time: 245 us
  blocking collectives  123 us (50%)
  waiting for transfers between devices  62.7 us (26%)
  matrix products  21.4 us (9%)
  starting transfers between devices  17.2 us (7%)
  Pallas kernels  9.72 us (4%)
  other arithmetic  7.27 us (3%)
  local copies, waits for them, and re-layouts  2.66 us (1%)
    all_gather x2, blocking collectives, aux_sum(): lax.all_gather(mine, 'aux', axis=1, tiled=True).astype(jnp.float32)  67.2 us
    all_to_all x2, waiting for transfers between devices, aux_sum(): pieces = lax.all_to_all(pieces, 'aux', 1, 1, tiled=True)  62.7 us
    all_gather x2, blocking collectives, pair_sum(): return lax.all_gather(matrices, 'pair').sum(0)  55.5 us
    all_to_all x2, starting transfers between devices, aux_sum(): pieces = lax.all_to_all(pieces, 'aux', 1, 1, tiled=True)  17.2 us
    dot_general x4, matrix products, split_product(): jnp.dot(jnp.concatenate([first_high, first_low, first_high], axis=1), jnp...  12.3 us
    pallas_call x2, Pallas kernels, inverse_factor(): pl.pallas_call(_inverse_factor_kernel, out_shape=jax.ShapeDtypeStruct((k,...  9.72 us
  transfers between devices with their start and end apart: 2, of which 2 were waited for; matrix products, arithmetic and copies ran while one was open for 3% of the time, Pallas kernels for 0%

profile of v13, /device:TPU:2, one launch (start us, length us, event | category | flops | bytes accessed | tf_op | source)
XLA Modules:
  0.0 244.6 jit_solution(4355926048657135774)
XLA Ops:
  0.7 0.9 dynamic_slice.3
  2.4 2.0 fusion.94
  4.4 1.2 reduce-precision_convert_fusion.4
  6.4 30.0 %all-gather.2 = f32[32,224,32]{1,2,0:T(8,128)} all-gather(f32[1,224,32]{1,2,0:T(8,128)S(1)} %maximum_bitcast_fusion), channel_id=2, replica_groups=mesh['aux'=16,'pair'=32] {'pair'}, dimensions={0}, use_global_device_ids=true | all-gather | bytes 946176 | tf_op jit(solution)/shard_map/all_gather | solution.py:46
  36.4 1.3 reduce_sum.60
  38.4 4.9 %shard_map.67 = f32[32,32]{1,0:T(8,128)} custom-call(f32[32,32]{1,0:T(8,128)} %copy.21.gram_ref), custom_call_target="tpu_custom_call" | custom-call | tf_op jit(solution)/shard_map/pallas_call | solution.py:89
  43.3 0.9 fusion.49
  45.1 0.9 pad_maximum_fusion.3
  46.1 12.4 %all-to-all-start = ((bf16[32,16,576]{2,0,1:T(8,128)(2,1)}), bf16[32,16,576]{2,0,1:T(8,128)(2,1)S(1)}, u32[]{:S(2)}, u32[]{:S(2)}) async-start(bf16[32,16,576]{2,0,1:T(8,128)(2,1)} %pad_maximum_fusion.3), calls=%async_computation | async-start | bytes 1310720 | tf_op jit(solution)/shard_map/all_to_all | solution.py:58
  58.5 3.1 %reduce-precision_convert_fusion.3 = (bf16[32,8192]{1,0:T(8,128)(2,1)}, bf16[32,8192]{1,0:T(8,128)(2,1)}, f32[32,8192]{1,0:T(8,128)}) fusion(bf16[32,8192]{1,0:T(8,128)(2,1)} %get-tuple-element.16, bf16[32,8192]{1,0:T(8,128)(2,1)} %get-tuple-element.15, bf16[32,32]{1,0:T(8,128)(2,1)S(1)} %get-tuple-element.30, bf16[32,32]{1,0:T(8,128)(2,1)S(1)} %get-tuple-element.29), kind=kOutput, calls=%fused_computation.53 | convolution fusion | flops 56117248 | bytes 3149824 | tf_op jit(solution)/shard_map/dot_general | solution.py:38
  61.8 31.3 %all-to-all-done = bf16[32,16,576]{2,0,1:T(8,128)(2,1)S(1)} async-done(((bf16[32,16,576]{2,0,1:T(8,128)(2,1)}), bf16[32,16,576]{2,0,1:T(8,128)(2,1)S(1)}, u32[]{:S(2)}, u32[]{:S(2)}) %all-to-all-start) | async-done | bytes 589856 | tf_op jit(solution)/shard_map/all_to_all | solution.py:58
  93.4 33.6 %all_gather.20 = bf16[32,8192]{1,0:T(8,128)(2,1)S(1)} all-gather(bf16[32,512]{1,0:T(8,128)(2,1)S(1)} %slice_reduce_fusion.1), channel_id=1, replica_groups=mesh['aux'=16,'pair'=32] {'aux'}, dimensions={1}, use_global_device_ids=true | all-gather | bytes 557056 | tf_op jit(solution)/shard_map/all_gather | solution.py:63
  127.2 2.6 %reduce-precision_convert_fusion.1 = (bf16[32,8192]{1,0:T(8,128)(2,1)S(1)}, bf16[32,8192]{1,0:T(8,128)(2,1)S(1)}, bf16[32,8192]{1,0:T(8,128)(2,1)S(1)}, bf16[32,8192]{1,0:T(8,128)(2,1)S(1)}) fusion(f32[8192]{0:T(1024)S(1)} %bitcast.44, f32[32,8192]{1,0:T(8,128)} %get-tuple-element.33, f32[8192]{0:T(1024)S(1)} %broadcast_divide_fusion, ...), kind=kOutput, calls=%fused_computation.49 | convolution fusion | flops 59000832 | bytes 4788224 | tf_op jit(solution)/shard_map/dot_general | solution.py:38
  129.8 1.0 convolution_bitcast_fusion
  131.8 25.5 %all-gather.3 = f32[32,224,32]{1,2,0:T(8,128)} all-gather(f32[1,224,32]{1,2,0:T(8,128)S(1)} %maximum_bitcast_fusion.1), channel_id=3, replica_groups=mesh['aux'=16,'pair'=32] {'pair'}, dimensions={0}, use_global_device_ids=true | all-gather | bytes 946176 | tf_op jit(solution)/shard_map/all_gather | solution.py:46
  157.3 1.3 reduce_sum.63
  159.3 4.9 %shard_map.68 = f32[32,32]{1,0:T(8,128)} custom-call(f32[32,32]{1,0:T(8,128)} %copy.22.gram_ref), custom_call_target="tpu_custom_call" | custom-call | tf_op jit(solution)/shard_map/pallas_call | solution.py:89
  164.2 0.9 fusion.47
  166.0 0.9 pad_maximum_fusion.4
  166.9 4.8 %all-to-all-start.1 = ((bf16[32,16,576]{2,0,1:T(8,128)(2,1)}), bf16[32,16,576]{2,0,1:T(8,128)(2,1)S(1)}, u32[]{:S(2)}, u32[]{:S(2)}) async-start(bf16[32,16,576]{2,0,1:T(8,128)(2,1)} %pad_maximum_fusion.4), calls=%async_computation.1 | async-start | bytes 1310720 | tf_op jit(solution)/shard_map/all_to_all | solution.py:58
  171.8 3.1 %reduce-precision_convert_fusion = (bf16[32,8192]{1,0:T(8,128)(2,1)}, bf16[32,8192]{1,0:T(8,128)(2,1)}, f32[32,8192]{1,0:T(8,128)}) fusion(bf16[32,8192]{1,0:T(8,128)(2,1)} %copy-done.4, bf16[32,8192]{1,0:T(8,128)(2,1)} %copy-done.5, bf16[32,32]{1,0:T(8,128)(2,1)S(1)} %get-tuple-element.24, bf16[32,32]{1,0:T(8,128)(2,1)S(1)} %get-tuple-element.23), kind=kOutput, calls=%fused_computation.47 | convolution fusion | flops 56117248 | bytes 3149824 | tf_op jit(solution)/shard_map/dot_general | solution.py:38
  175.1 31.3 %all-to-all-done.1 = bf16[32,16,576]{2,0,1:T(8,128)(2,1)S(1)} async-done(((bf16[32,16,576]{2,0,1:T(8,128)(2,1)}), bf16[32,16,576]{2,0,1:T(8,128)(2,1)S(1)}, u32[]{:S(2)}, u32[]{:S(2)}) %all-to-all-start.1) | async-done | bytes 589856 | tf_op jit(solution)/shard_map/all_to_all | solution.py:58
  206.7 33.6 %all_gather.23 = bf16[32,8192]{1,0:T(8,128)(2,1)S(1)} all-gather(bf16[32,512]{1,0:T(8,128)(2,1)S(1)} %slice_reduce_fusion), channel_id=1, replica_groups=mesh['aux'=16,'pair'=32] {'aux'}, dimensions={1}, use_global_device_ids=true | all-gather | bytes 557056 | tf_op jit(solution)/shard_map/all_gather | solution.py:63
  241.1 3.6 %fusion.93 = (bf16[32,8192]{1,0:T(8,128)(2,1)}, f32[32,8192]{1,0:T(8,128)}) fusion(f32[32,8192]{1,0:T(8,128)} %get-tuple-element.34, f32[8192]{0:T(1024)S(1)} %broadcast_divide_fusion, bf16[32,8192]{1,0:T(8,128)(2,1)} %get-tuple-element.8, bf16[32,8192]{1,0:T(8,128)(2,1)} %get-tuple-element.7, bf16[32,32]{1,0:T(8,128)(2,1)S(1)} %get-tuple-element.20, ...), kind=kOutput, calls=%fused_computation.153 | convolution fusion | flops 56903680 | bytes 4263936 | tf_op jit(solution)/shard_map/dot_general | solution.py:38
  (50 shorter events, 7.6 us)
Async XLA Ops:
  0.6 1.8 copy-start
  0.6 3.7 %copy-start.1 = (bf16[32,8192]{1,0:T(8,128)(2,1)S(1)}, bf16[32,8192]{1,0:T(8,128)(2,1)}, u32[]{:S(2)}) copy-start(bf16[32,8192]{1,0:T(8,128)(2,1)} %param.7) | copy-start | bytes 1572868
  44.9 13.5 %copy-start.3 = (f32[32,32]{1,0:T(8,128)S(1)}, f32[32,32]{1,0:T(8,128)}, u32[]{:S(2)}) copy-start(f32[32,32]{1,0:T(8,128)} %shard_map.67) | copy-start | bytes 12292
  46.1 47.1 %all-to-all-start = ((bf16[32,16,576]{2,0,1:T(8,128)(2,1)}), bf16[32,16,576]{2,0,1:T(8,128)(2,1)S(1)}, u32[]{:S(2)}, u32[]{:S(2)}) async-start(bf16[32,16,576]{2,0,1:T(8,128)(2,1)} %pad_maximum_fusion.3), calls=%async_computation | async-start | bytes 1310720 | tf_op jit(solution)/shard_map/all_to_all | solution.py:58
  129.7 1.9 copy-start.4
  129.7 1.9 copy-start.5
  165.8 5.9 %copy-start.2 = (f32[32,32]{1,0:T(8,128)S(1)}, f32[32,32]{1,0:T(8,128)}, u32[]{:S(2)}) copy-start(f32[32,32]{1,0:T(8,128)} %shard_map.68) | copy-start | bytes 12292
  166.9 39.5 %all-to-all-start.1 = ((bf16[32,16,576]{2,0,1:T(8,128)(2,1)}), bf16[32,16,576]{2,0,1:T(8,128)(2,1)S(1)}, u32[]{:S(2)}, u32[]{:S(2)}) async-start(bf16[32,16,576]{2,0,1:T(8,128)(2,1)} %pad_maximum_fusion.4), calls=%async_computation.1 | async-start | bytes 1310720 | tf_op jit(solution)/shard_map/all_to_all | solution.py:58

commit v14 on v12

--- a/solution.py
+++ b/solution.py
@@ -130,7 +130,7 @@
             cross_part = cross[:, :k] + cross[:, k:]
         summed = pair_sum(jnp.concatenate(
             [gram_part / npair_all, weighted_part / npair_all, cross_part], axis=0))
-        inverse = inverse_factor(summed[:k])
+        inverse = inverse_factor(summed[:k].T)
         basis_now = split_product(inverse, wide_trial)
         projected = lax.dot_general(
             summed[2 * k:], inverse, (((1,), (1,)), ((), ())),

time: 245 us -> 245 us (level)
  no operation moved by 1% of the time
where the time goes in v14:
time: 245 us; the launch traced here: 244 us
  blocking collectives  123 us (50%)
  waiting for transfers between devices  62.7 us (26%)
  matrix products  21.4 us (9%)
  starting transfers between devices  17.2 us (7%)
  Pallas kernels  9.72 us (4%)
  other arithmetic  7.25 us (3%)
  local copies, waits for them, and re-layouts  2.51 us (1%)
    all_gather x2, blocking collectives, aux_sum(): lax.all_gather(mine, 'aux', axis=1, tiled=True).astype(jnp.float32)  67.2 us
    all_to_all x2, waiting for transfers between devices, aux_sum(): pieces = lax.all_to_all(pieces, 'aux', 1, 1, tiled=True)  62.7 us
    all_gather x2, blocking collectives, pair_sum(): return lax.all_gather(matrices, 'pair').sum(0)  55.5 us
    all_to_all x2, starting transfers between devices, aux_sum(): pieces = lax.all_to_all(pieces, 'aux', 1, 1, tiled=True)  17.2 us
    dot_general x4, matrix products, split_product(): jnp.dot(jnp.concatenate([first_high, first_low, first_high], axis=1), jnp...  12.4 us
    pallas_call x2, Pallas kernels, inverse_factor(): pl.pallas_call(_inverse_factor_kernel, out_shape=jax.ShapeDtypeStruct((k,...  9.72 us
  transfers between devices with their start and end apart: 2, of which 2 were waited for; matrix products, arithmetic and copies ran while one was open for 3% of the time, Pallas kernels for 0%

profile of v14, /device:TPU:2, one launch (start us, length us, event | category | flops | bytes accessed | tf_op | source)
XLA Modules:
  0.0 244.5 jit_solution(3965979380424006667)
XLA Ops:
  0.7 0.9 dynamic_slice.3
  2.4 2.0 fusion.94
  4.4 1.2 reduce-precision_convert_fusion.4
  6.4 30.0 %all-gather.2 = f32[32,224,32]{1,2,0:T(8,128)} all-gather(f32[1,224,32]{1,2,0:T(8,128)S(1)} %maximum_bitcast_fusion), channel_id=2, replica_groups=mesh['aux'=16,'pair'=32] {'pair'}, dimensions={0}, use_global_device_ids=true | all-gather | bytes 946176 | tf_op jit(solution)/shard_map/all_gather | solution.py:46
  36.4 1.3 reduce_sum.60
  38.3 4.9 %shard_map.67 = f32[32,32]{1,0:T(8,128)} custom-call(f32[32,32]{1,0:T(8,128)} %slice_bitcast_fusion.1.gram_ref), custom_call_target="tpu_custom_call" | custom-call | tf_op jit(solution)/shard_map/pallas_call | solution.py:89
  43.2 0.9 fusion.49
  45.1 0.9 pad_maximum_fusion.3
  46.0 12.4 %all-to-all-start = ((bf16[32,16,576]{2,0,1:T(8,128)(2,1)}), bf16[32,16,576]{2,0,1:T(8,128)(2,1)S(1)}, u32[]{:S(2)}, u32[]{:S(2)}) async-start(bf16[32,16,576]{2,0,1:T(8,128)(2,1)} %pad_maximum_fusion.3), calls=%async_computation | async-start | bytes 1310720 | tf_op jit(solution)/shard_map/all_to_all | solution.py:58
  58.4 3.1 %reduce-precision_convert_fusion.3 = (bf16[32,8192]{1,0:T(8,128)(2,1)}, bf16[32,8192]{1,0:T(8,128)(2,1)}, f32[32,8192]{1,0:T(8,128)}) fusion(bf16[32,8192]{1,0:T(8,128)(2,1)} %get-tuple-element.16, bf16[32,8192]{1,0:T(8,128)(2,1)} %get-tuple-element.15, bf16[32,32]{1,0:T(8,128)(2,1)S(1)} %get-tuple-element.30, bf16[32,32]{1,0:T(8,128)(2,1)S(1)} %get-tuple-element.29), kind=kOutput, calls=%fused_computation.53 | convolution fusion | flops 56117248 | bytes 3149824 | tf_op jit(solution)/shard_map/dot_general | solution.py:38
  61.7 31.3 %all-to-all-done = bf16[32,16,576]{2,0,1:T(8,128)(2,1)S(1)} async-done(((bf16[32,16,576]{2,0,1:T(8,128)(2,1)}), bf16[32,16,576]{2,0,1:T(8,128)(2,1)S(1)}, u32[]{:S(2)}, u32[]{:S(2)}) %all-to-all-start) | async-done | bytes 589856 | tf_op jit(solution)/shard_map/all_to_all | solution.py:58
  93.3 33.6 %all_gather.20 = bf16[32,8192]{1,0:T(8,128)(2,1)S(1)} all-gather(bf16[32,512]{1,0:T(8,128)(2,1)S(1)} %slice_reduce_fusion.1), channel_id=1, replica_groups=mesh['aux'=16,'pair'=32] {'aux'}, dimensions={1}, use_global_device_ids=true | all-gather | bytes 557056 | tf_op jit(solution)/shard_map/all_gather | solution.py:63
  127.1 2.6 %reduce-precision_convert_fusion.1 = (bf16[32,8192]{1,0:T(8,128)(2,1)S(1)}, bf16[32,8192]{1,0:T(8,128)(2,1)S(1)}, bf16[32,8192]{1,0:T(8,128)(2,1)S(1)}, bf16[32,8192]{1,0:T(8,128)(2,1)S(1)}) fusion(f32[8192]{0:T(1024)S(1)} %bitcast.46, f32[32,8192]{1,0:T(8,128)} %get-tuple-element.33, bf16[32,8192]{1,0:T(8,128)(2,1)} %get-tuple-element.12, ...), kind=kOutput, calls=%fused_computation.49 | convolution fusion | flops 59000832 | bytes 4755456 | tf_op jit(solution)/shard_map/dot_general | solution.py:38
  129.7 1.0 convolution_bitcast_fusion
  131.7 25.5 %all-gather.3 = f32[32,224,32]{1,2,0:T(8,128)} all-gather(f32[1,224,32]{1,2,0:T(8,128)S(1)} %maximum_bitcast_fusion.1), channel_id=3, replica_groups=mesh['aux'=16,'pair'=32] {'pair'}, dimensions={0}, use_global_device_ids=true | all-gather | bytes 946176 | tf_op jit(solution)/shard_map/all_gather | solution.py:46
  157.2 1.3 reduce_sum.63
  159.1 4.9 %shard_map.68 = f32[32,32]{1,0:T(8,128)} custom-call(f32[32,32]{1,0:T(8,128)} %slice_bitcast_fusion.gram_ref), custom_call_target="tpu_custom_call" | custom-call | tf_op jit(solution)/shard_map/pallas_call | solution.py:89
  164.0 0.9 fusion.47
  165.9 0.9 pad_maximum_fusion.4
  166.8 4.8 %all-to-all-start.1 = ((bf16[32,16,576]{2,0,1:T(8,128)(2,1)}), bf16[32,16,576]{2,0,1:T(8,128)(2,1)S(1)}, u32[]{:S(2)}, u32[]{:S(2)}) async-start(bf16[32,16,576]{2,0,1:T(8,128)(2,1)} %pad_maximum_fusion.4), calls=%async_computation.1 | async-start | bytes 1310720 | tf_op jit(solution)/shard_map/all_to_all | solution.py:58
  171.6 3.1 %reduce-precision_convert_fusion = (bf16[32,8192]{1,0:T(8,128)(2,1)}, bf16[32,8192]{1,0:T(8,128)(2,1)}, f32[32,8192]{1,0:T(8,128)}) fusion(bf16[32,8192]{1,0:T(8,128)(2,1)} %copy-done.4, bf16[32,8192]{1,0:T(8,128)(2,1)} %copy-done.5, bf16[32,32]{1,0:T(8,128)(2,1)S(1)} %get-tuple-element.24, bf16[32,32]{1,0:T(8,128)(2,1)S(1)} %get-tuple-element.23), kind=kOutput, calls=%fused_computation.47 | convolution fusion | flops 56117248 | bytes 3149824 | tf_op jit(solution)/shard_map/dot_general | solution.py:38
  174.9 31.3 %all-to-all-done.1 = bf16[32,16,576]{2,0,1:T(8,128)(2,1)S(1)} async-done(((bf16[32,16,576]{2,0,1:T(8,128)(2,1)}), bf16[32,16,576]{2,0,1:T(8,128)(2,1)S(1)}, u32[]{:S(2)}, u32[]{:S(2)}) %all-to-all-start.1) | async-done | bytes 589856 | tf_op jit(solution)/shard_map/all_to_all | solution.py:58
  206.5 33.6 %all_gather.23 = bf16[32,8192]{1,0:T(8,128)(2,1)S(1)} all-gather(bf16[32,512]{1,0:T(8,128)(2,1)S(1)} %slice_reduce_fusion), channel_id=1, replica_groups=mesh['aux'=16,'pair'=32] {'aux'}, dimensions={1}, use_global_device_ids=true | all-gather | bytes 557056 | tf_op jit(solution)/shard_map/all_gather | solution.py:63
  240.9 3.6 %fusion.93 = (bf16[32,8192]{1,0:T(8,128)(2,1)}, f32[32,8192]{1,0:T(8,128)}) fusion(f32[32,8192]{1,0:T(8,128)} %get-tuple-element.34, f32[8192]{0:T(1024)S(1)} %bitcast.47, bf16[32,8192]{1,0:T(8,128)(2,1)} %get-tuple-element.8, bf16[32,8192]{1,0:T(8,128)(2,1)} %get-tuple-element.7, bf16[32,32]{1,0:T(8,128)(2,1)S(1)} %get-tuple-element.20, ...), kind=kOutput, calls=%fused_computation.154 | convolution fusion | flops 56903680 | bytes 4231168 | tf_op jit(solution)/shard_map/dot_general | solution.py:38
  (47 shorter events, 7.4 us)
Async XLA Ops:
  0.6 1.8 copy-start
  0.6 3.7 %copy-start.1 = (bf16[32,8192]{1,0:T(8,128)(2,1)S(1)}, bf16[32,8192]{1,0:T(8,128)(2,1)}, u32[]{:S(2)}) copy-start(bf16[32,8192]{1,0:T(8,128)(2,1)} %param.7) | copy-start | bytes 1572868
  44.9 13.5 %copy-start.3 = (f32[32,32]{1,0:T(8,128)S(1)}, f32[32,32]{1,0:T(8,128)}, u32[]{:S(2)}) copy-start(f32[32,32]{1,0:T(8,128)} %shard_map.67) | copy-start | bytes 12292
  46.0 47.1 %all-to-all-start = ((bf16[32,16,576]{2,0,1:T(8,128)(2,1)}), bf16[32,16,576]{2,0,1:T(8,128)(2,1)S(1)}, u32[]{:S(2)}, u32[]{:S(2)}) async-start(bf16[32,16,576]{2,0,1:T(8,128)(2,1)} %pad_maximum_fusion.3), calls=%async_computation | async-start | bytes 1310720 | tf_op jit(solution)/shard_map/all_to_all | solution.py:58
  129.7 1.9 copy-start.4
  129.7 1.9 copy-start.5
  165.7 5.9 %copy-start.2 = (f32[32,32]{1,0:T(8,128)S(1)}, f32[32,32]{1,0:T(8,128)}, u32[]{:S(2)}) copy-start(f32[32,32]{1,0:T(8,128)} %shard_map.68) | copy-start | bytes 12292
  166.8 39.5 %all-to-all-start.1 = ((bf16[32,16,576]{2,0,1:T(8,128)(2,1)}), bf16[32,16,576]{2,0,1:T(8,128)(2,1)S(1)}, u32[]{:S(2)}, u32[]{:S(2)}) async-start(bf16[32,16,576]{2,0,1:T(8,128)(2,1)} %pad_maximum_fusion.4), calls=%async_computation.1 | async-start | bytes 1310720 | tf_op jit(solution)/shard_map/all_to_all | solution.py:58

commit v15 on v11

--- a/solution.py
+++ b/solution.py
@@ -102,7 +102,9 @@
     nvir = eps_vir.shape[0]
     if block_cols % nvir == 0:
         occ_rows = block_cols // nvir
-        occ_block = lax.dynamic_slice_in_dim(eps_occ, lax.axis_index("pair") * occ_rows, occ_rows)
+        n_blocks = eps_occ.shape[0] // occ_rows
+        mine = lax.broadcasted_iota(jnp.int32, (n_blocks, 1), 0) == lax.axis_index("pair")
+        occ_block = jnp.sum(jnp.where(mine, eps_occ.reshape(n_blocks, occ_rows), 0.0), axis=0)
         diagonal = (eps_vir[None, :] - occ_block[:, None]).reshape(block_cols)
     else:
         everything = (eps_vir[None, :] - eps_occ[:, None]).reshape(npair_all)

time: 246 us -> 246 us (level)
  no operation moved by 1% of the time
where the time goes in v15:
time: 246 us; the launch traced here: 245 us
  blocking collectives  123 us (50%)
  waiting for transfers between devices  62.7 us (25%)
  matrix products  21.4 us (9%)
  starting transfers between devices  17.2 us (7%)
  Pallas kernels  9.79 us (4%)
  other arithmetic  7.31 us (3%)
  local copies, waits for them, and re-layouts  2.64 us (1%)
    all_gather x2, blocking collectives, aux_sum(): lax.all_gather(mine, 'aux', axis=1, tiled=True).astype(jnp.float32)  67.2 us
    all_to_all x2, waiting for transfers between devices, aux_sum(): pieces = lax.all_to_all(pieces, 'aux', 1, 1, tiled=True)  62.7 us
    all_gather x2, blocking collectives, pair_sum(): return lax.all_gather(matrices, 'pair').sum(0)  55.5 us
    all_to_all x2, starting transfers between devices, aux_sum(): pieces = lax.all_to_all(pieces, 'aux', 1, 1, tiled=True)  17.2 us
    dot_general x4, matrix products, split_product(): jnp.dot(jnp.concatenate([first_high, first_low, first_high], axis=1), jnp...  12.3 us
    pallas_call x2, Pallas kernels, inverse_factor(): pl.pallas_call(_inverse_factor_kernel, out_shape=jax.ShapeDtypeStruct((k,...  9.79 us
  transfers between devices with their start and end apart: 2, of which 2 were waited for; matrix products, arithmetic and copies ran while one was open for 3% of the time, Pallas kernels for 0%

profile of v15, /device:TPU:2, one launch (start us, length us, event | category | flops | bytes accessed | tf_op | source)
XLA Modules:
  0.0 244.7 jit_solution(10443553139352881670)
XLA Ops:
  0.7 0.9 reshape.38
  2.5 2.0 fusion.94
  4.5 1.2 reduce-precision_convert_fusion.4
  6.5 30.0 %all-gather.2 = f32[32,224,32]{1,2,0:T(8,128)} all-gather(f32[1,224,32]{1,2,0:T(8,128)S(1)} %maximum_bitcast_fusion), channel_id=2, replica_groups=mesh['aux'=16,'pair'=32] {'pair'}, dimensions={0}, use_global_device_ids=true | all-gather | bytes 946176 | tf_op jit(solution)/shard_map/all_gather | solution.py:46
  36.5 1.3 reduce_sum.70
  38.5 4.9 %shard_map.67 = f32[32,32]{1,0:T(8,128)} custom-call(f32[32,32]{1,0:T(8,128)} %copy.25.gram_ref), custom_call_target="tpu_custom_call" | custom-call | tf_op jit(solution)/shard_map/pallas_call | solution.py:90
  43.4 0.9 fusion.49
  45.3 0.9 pad_maximum_fusion.3
  46.2 12.4 %all-to-all-start = ((bf16[32,16,576]{2,0,1:T(8,128)(2,1)}), bf16[32,16,576]{2,0,1:T(8,128)(2,1)S(1)}, u32[]{:S(2)}, u32[]{:S(2)}) async-start(bf16[32,16,576]{2,0,1:T(8,128)(2,1)} %pad_maximum_fusion.3), calls=%async_computation | async-start | bytes 1310720 | tf_op jit(solution)/shard_map/all_to_all | solution.py:58
  58.6 3.1 %reduce-precision_convert_fusion.3 = (bf16[32,8192]{1,0:T(8,128)(2,1)}, bf16[32,8192]{1,0:T(8,128)(2,1)}, f32[32,8192]{1,0:T(8,128)}) fusion(bf16[32,8192]{1,0:T(8,128)(2,1)} %get-tuple-element.16, bf16[32,8192]{1,0:T(8,128)(2,1)} %get-tuple-element.15, bf16[32,32]{1,0:T(8,128)(2,1)S(1)} %get-tuple-element.30, bf16[32,32]{1,0:T(8,128)(2,1)S(1)} %get-tuple-element.29), kind=kOutput, calls=%fused_computation.53 | convolution fusion | flops 56117248 | bytes 3149824 | tf_op jit(solution)/shard_map/dot_general | solution.py:38
  61.9 31.4 %all-to-all-done = bf16[32,16,576]{2,0,1:T(8,128)(2,1)S(1)} async-done(((bf16[32,16,576]{2,0,1:T(8,128)(2,1)}), bf16[32,16,576]{2,0,1:T(8,128)(2,1)S(1)}, u32[]{:S(2)}, u32[]{:S(2)}) %all-to-all-start) | async-done | bytes 589856 | tf_op jit(solution)/shard_map/all_to_all | solution.py:58
  93.5 33.6 %all_gather.20 = bf16[32,8192]{1,0:T(8,128)(2,1)S(1)} all-gather(bf16[32,512]{1,0:T(8,128)(2,1)S(1)} %slice_reduce_fusion.1), channel_id=1, replica_groups=mesh['aux'=16,'pair'=32] {'aux'}, dimensions={1}, use_global_device_ids=true | all-gather | bytes 557056 | tf_op jit(solution)/shard_map/all_gather | solution.py:63
  127.3 2.6 %reduce-precision_convert_fusion.1 = (bf16[32,8192]{1,0:T(8,128)(2,1)S(1)}, bf16[32,8192]{1,0:T(8,128)(2,1)S(1)}, bf16[32,8192]{1,0:T(8,128)(2,1)S(1)}, bf16[32,8192]{1,0:T(8,128)(2,1)S(1)}) fusion(f32[8192]{0:T(1024)S(1)} %bitcast.42, f32[32,8192]{1,0:T(8,128)} %get-tuple-element.33, bf16[32,8192]{1,0:T(8,128)(2,1)} %get-tuple-element.12, ...), kind=kOutput, calls=%fused_computation.49 | convolution fusion | flops 59000832 | bytes 4755456 | tf_op jit(solution)/shard_map/dot_general | solution.py:38
  129.9 1.0 convolution_bitcast_fusion
  131.9 25.5 %all-gather.3 = f32[32,224,32]{1,2,0:T(8,128)} all-gather(f32[1,224,32]{1,2,0:T(8,128)S(1)} %maximum_bitcast_fusion.1), channel_id=3, replica_groups=mesh['aux'=16,'pair'=32] {'pair'}, dimensions={0}, use_global_device_ids=true | all-gather | bytes 946176 | tf_op jit(solution)/shard_map/all_gather | solution.py:46
  157.4 1.3 reduce_sum.73
  159.4 4.9 %shard_map.68 = f32[32,32]{1,0:T(8,128)} custom-call(f32[32,32]{1,0:T(8,128)} %copy.26.gram_ref), custom_call_target="tpu_custom_call" | custom-call | tf_op jit(solution)/shard_map/pallas_call | solution.py:90
  164.3 0.9 fusion.47
  166.2 0.9 pad_maximum_fusion.4
  167.1 4.8 %all-to-all-start.1 = ((bf16[32,16,576]{2,0,1:T(8,128)(2,1)}), bf16[32,16,576]{2,0,1:T(8,128)(2,1)S(1)}, u32[]{:S(2)}, u32[]{:S(2)}) async-start(bf16[32,16,576]{2,0,1:T(8,128)(2,1)} %pad_maximum_fusion.4), calls=%async_computation.1 | async-start | bytes 1310720 | tf_op jit(solution)/shard_map/all_to_all | solution.py:58
  171.9 3.1 %reduce-precision_convert_fusion = (bf16[32,8192]{1,0:T(8,128)(2,1)}, bf16[32,8192]{1,0:T(8,128)(2,1)}, f32[32,8192]{1,0:T(8,128)}) fusion(bf16[32,8192]{1,0:T(8,128)(2,1)} %copy-done.4, bf16[32,8192]{1,0:T(8,128)(2,1)} %copy-done.5, bf16[32,32]{1,0:T(8,128)(2,1)S(1)} %get-tuple-element.24, bf16[32,32]{1,0:T(8,128)(2,1)S(1)} %get-tuple-element.23), kind=kOutput, calls=%fused_computation.47 | convolution fusion | flops 56117248 | bytes 3149824 | tf_op jit(solution)/shard_map/dot_general | solution.py:38
  175.2 31.4 %all-to-all-done.1 = bf16[32,16,576]{2,0,1:T(8,128)(2,1)S(1)} async-done(((bf16[32,16,576]{2,0,1:T(8,128)(2,1)}), bf16[32,16,576]{2,0,1:T(8,128)(2,1)S(1)}, u32[]{:S(2)}, u32[]{:S(2)}) %all-to-all-start.1) | async-done | bytes 589856 | tf_op jit(solution)/shard_map/all_to_all | solution.py:58
  206.8 33.6 %all_gather.23 = bf16[32,8192]{1,0:T(8,128)(2,1)S(1)} all-gather(bf16[32,512]{1,0:T(8,128)(2,1)S(1)} %slice_reduce_fusion), channel_id=1, replica_groups=mesh['aux'=16,'pair'=32] {'aux'}, dimensions={1}, use_global_device_ids=true | all-gather | bytes 557056 | tf_op jit(solution)/shard_map/all_gather | solution.py:63
  241.2 3.6 %fusion.93 = (bf16[32,8192]{1,0:T(8,128)(2,1)}, f32[32,8192]{1,0:T(8,128)}) fusion(f32[32,8192]{1,0:T(8,128)} %get-tuple-element.34, f32[8192]{0:T(1024)S(1)} %bitcast.43, bf16[32,8192]{1,0:T(8,128)(2,1)} %get-tuple-element.8, bf16[32,8192]{1,0:T(8,128)(2,1)} %get-tuple-element.7, bf16[32,32]{1,0:T(8,128)(2,1)S(1)} %get-tuple-element.20, ...), kind=kOutput, calls=%fused_computation.154 | convolution fusion | flops 56903680 | bytes 4231168 | tf_op jit(solution)/shard_map/dot_general | solution.py:38
  (51 shorter events, 7.7 us)
Async XLA Ops:
  0.6 1.8 copy-start
  0.6 3.8 %copy-start.1 = (bf16[32,8192]{1,0:T(8,128)(2,1)S(1)}, bf16[32,8192]{1,0:T(8,128)(2,1)}, u32[]{:S(2)}) copy-start(bf16[32,8192]{1,0:T(8,128)(2,1)} %param.7) | copy-start | bytes 1572868
  45.1 13.5 %copy-start.3 = (f32[32,32]{1,0:T(8,128)S(1)}, f32[32,32]{1,0:T(8,128)}, u32[]{:S(2)}) copy-start(f32[32,32]{1,0:T(8,128)} %shard_map.67) | copy-start | bytes 12292
  46.2 47.1 %all-to-all-start = ((bf16[32,16,576]{2,0,1:T(8,128)(2,1)}), bf16[32,16,576]{2,0,1:T(8,128)(2,1)S(1)}, u32[]{:S(2)}, u32[]{:S(2)}) async-start(bf16[32,16,576]{2,0,1:T(8,128)(2,1)} %pad_maximum_fusion.3), calls=%async_computation | async-start | bytes 1310720 | tf_op jit(solution)/shard_map/all_to_all | solution.py:58
  129.8 1.9 copy-start.4
  129.9 1.9 copy-start.5
  165.9 5.9 %copy-start.2 = (f32[32,32]{1,0:T(8,128)S(1)}, f32[32,32]{1,0:T(8,128)}, u32[]{:S(2)}) copy-start(f32[32,32]{1,0:T(8,128)} %shard_map.68) | copy-start | bytes 12292
  167.1 39.5 %all-to-all-start.1 = ((bf16[32,16,576]{2,0,1:T(8,128)(2,1)}), bf16[32,16,576]{2,0,1:T(8,128)(2,1)S(1)}, u32[]{:S(2)}, u32[]{:S(2)}) async-start(bf16[32,16,576]{2,0,1:T(8,128)(2,1)} %pad_maximum_fusion.4), calls=%async_computation.1 | async-start | bytes 1310720 | tf_op jit(solution)/shard_map/all_to_all | solution.py:58

commit v16 on v11

--- a/solution.py
+++ b/solution.py
@@ -115,11 +115,13 @@
         weighted = wide_trial * diag_row
         weighted_high, weighted_low = split_bf16(weighted)
         if iteration == 0:
-            both = correlation_of(
-                jnp.concatenate([trial_now, weighted_high, weighted_low], axis=0), trial_now, None)
-            gram_part = both[:k]
-            weighted_part = both[k:2 * k] + both[2 * k:]
-            cross_part = correlation_of(b_tensor, trial_now, None)
+            rows = b_tensor.shape[0]
+            summed = pair_sum(correlation_of(
+                jnp.concatenate([b_tensor, trial_now, weighted_high, weighted_low], axis=0),
+                trial_now, None))
+            cross_sum = summed[:rows]
+            gram_sum = summed[rows:rows + k] / npair_all
+            weighted_sum = (summed[rows + k:rows + 2 * k] + summed[rows + 2 * k:]) / npair_all
         else:
             high, low = split_bf16(trial_now)
             split = jnp.concatenate([high, low], axis=0)
@@ -129,19 +131,22 @@
             weighted_part = both[2 * k:3 * k, :k] + both[2 * k:3 * k, k:] + both[3 * k:, :k]
             cross = correlation_of(b_tensor, split, None)
             cross_part = cross[:, :k] + cross[:, k:]
-        summed = pair_sum(jnp.concatenate(
-            [gram_part / npair_all, weighted_part / npair_all, cross_part], axis=0))
-        inverse = inverse_factor(summed[:k])
+            summed = pair_sum(jnp.concatenate(
+                [gram_part / npair_all, weighted_part / npair_all, cross_part], axis=0))
+            gram_sum = summed[:k]
+            weighted_sum = summed[k:2 * k]
+            cross_sum = summed[2 * k:]
+        inverse = inverse_factor(gram_sum)
         basis_now = split_product(inverse, wide_trial)
         projected = lax.dot_general(
-            summed[2 * k:], inverse, (((1,), (1,)), ((), ())),
+            cross_sum, inverse, (((1,), (1,)), ((), ())),
             precision=HIGHEST_PRECISION, preferred_element_type=jnp.float32,
         )
         group_part = lax.dot_general(
             projected, projected, (((0,), (0,)), ((), ())),
             precision=HIGHEST_PRECISION, preferred_element_type=jnp.float32,
         )
-        diag_part = product(product(inverse, summed[k:2 * k]), inverse.T)
+        diag_part = product(product(inverse, weighted_sum), inverse.T)
         projected_low = projected.astype(jnp.bfloat16)
         term = lax.dot_general(
             projected_low, b_tensor, (((0,), (0,)), ((), ())), preferred_element_type=jnp.float32

time: 246 us -> 293 us (1.19)
  waiting for transfers between devices: 62.7 us -> 127 us
  blocking collectives: 123 us -> 92.6 us
  between operations: 0.98 us -> 14.3 us
    all_gather x0 -> x1, waiting for transfers between devices: none -> 62.6 us  [pair_sum(): return lax.all_gather(matrices, 'pair').sum(0)]
    all_gather x2 -> x1, blocking collectives: 55.5 us -> 25.5 us  [pair_sum(): return lax.all_gather(matrices, 'pair').sum(0)]
  transfers between devices with their start and end apart: 2 -> 3, of which waited for: 2 -> 3; matrix products, arithmetic and copies ran while one was open for 3% -> 2% of each run, Pallas kernels for 0% -> 0%
where the time goes in v16:
time: 293 us; the launch traced here: 292 us
  waiting for transfers between devices  127 us (43%)
  blocking collectives  92.6 us (32%)
  matrix products  19.6 us (7%)
  starting transfers between devices  17.5 us (6%)
  between operations  14.3 us (5%)
  Pallas kernels  9.78 us (3%)
  other arithmetic  7.68 us (3%)
  local copies, waits for them, and re-layouts  3.75 us (1%)
    all_gather x2, blocking collectives, aux_sum(): lax.all_gather(mine, 'aux', axis=1, tiled=True).astype(jnp.float32)  67.1 us
    all_to_all x2, waiting for transfers between devices, aux_sum(): pieces = lax.all_to_all(pieces, 'aux', 1, 1, tiled=True)  64 us
    all_gather x1, waiting for transfers between devices, pair_sum(): return lax.all_gather(matrices, 'pair').sum(0)  62.6 us
    all_gather x1, blocking collectives, pair_sum(): return lax.all_gather(matrices, 'pair').sum(0)  25.5 us
    all_to_all x2, starting transfers between devices, aux_sum(): pieces = lax.all_to_all(pieces, 'aux', 1, 1, tiled=True)  17.4 us
    dot_general x4, matrix products, split_product(): jnp.dot(jnp.concatenate([first_high, first_low, first_high], axis=1), jnp...  10.3 us
    pallas_call x2, Pallas kernels, inverse_factor(): pl.pallas_call(_inverse_factor_kernel, out_shape=jax.ShapeDtypeStruct((k,...  9.78 us
  transfers between devices with their start and end apart: 3, of which 3 were waited for; matrix products, arithmetic and copies ran while one was open for 2% of the time, Pallas kernels for 0%

profile of v16, /device:TPU:2, one launch (start us, length us, event | category | flops | bytes accessed | tf_op | source)
XLA Modules:
  0.0 291.8 jit_solution(1992879527102725594)
XLA Ops:
  7.2 0.9 dynamic_slice.3
  8.9 2.3 reduce-precision_convert_fusion.4
  11.2 3.2 %fusion.2 = f32[256,32]{0,1:T(8,128)} fusion(bf16[32,8192]{1,0:T(8,128)(2,1)} %param.7, bf16[32,8192]{1,0:T(8,128)(2,1)S(1)} %get-tuple-element.14, bf16[32,8192]{1,0:T(8,128)(2,1)S(1)} %get-tuple-element.13, bf16[160,8192]{1,0:T(8,128)(2,1)S(1)} %copy-done), kind=kOutput, calls=%fused_computation.6 | convolution fusion | flops 150994944 | bytes 4227072 | tf_op jit(solution)/shard_map/dot_general | solution.py:15
  14.4 62.6 %all-gather.5.cloned.1.call-done = f32[8192,32]{0,1:T(8,128)} async-done(((f32[256,32]{0,1:T(8,128)}), f32[8192,32]{0,1:T(8,128)}) %all-gather.5.cloned.1.call-update) | async-done | bytes 1048592 | tf_op jit(solution)/shard_map/all_gather | solution.py:46
  77.0 1.5 copy.37
  79.4 4.9 %shard_map.67 = f32[32,32]{1,0:T(8,128)} custom-call(f32[32,32]{1,0:T(8,128)} %broadcast_multiply_fusion.gram_ref), custom_call_target="tpu_custom_call" | custom-call | tf_op jit(solution)/shard_map/pallas_call | solution.py:90
  84.3 0.9 fusion.51
  86.0 0.9 pad_maximum_fusion.3
  87.0 12.3 %all-to-all-start = ((bf16[32,16,576]{2,0,1:T(8,128)(2,1)}), bf16[32,16,576]{2,0,1:T(8,128)(2,1)S(1)}, u32[]{:S(2)}, u32[]{:S(2)}) async-start(bf16[32,16,576]{2,0,1:T(8,128)(2,1)} %pad_maximum_fusion.3), calls=%async_computation | async-start | bytes 1310720 | tf_op jit(solution)/shard_map/all_to_all | solution.py:58
  99.4 3.1 %reduce-precision_convert_fusion.3 = (bf16[32,8192]{1,0:T(8,128)(2,1)}, bf16[32,8192]{1,0:T(8,128)(2,1)}, f32[32,8192]{1,0:T(8,128)}) fusion(bf16[32,8192]{1,0:T(8,128)(2,1)} %get-tuple-element.16, bf16[32,8192]{1,0:T(8,128)(2,1)} %get-tuple-element.15, bf16[32,32]{1,0:T(8,128)(2,1)S(1)} %get-tuple-element.33, bf16[32,32]{1,0:T(8,128)(2,1)S(1)} %get-tuple-element.32), kind=kOutput, calls=%fused_computation.55 | convolution fusion | flops 56117248 | bytes 3149824 | tf_op jit(solution)/shard_map/dot_general | solution.py:38
  102.7 31.0 %all-to-all-done = bf16[32,16,576]{2,0,1:T(8,128)(2,1)S(1)} async-done(((bf16[32,16,576]{2,0,1:T(8,128)(2,1)}), bf16[32,16,576]{2,0,1:T(8,128)(2,1)S(1)}, u32[]{:S(2)}, u32[]{:S(2)}) %all-to-all-start) | async-done | bytes 589856 | tf_op jit(solution)/shard_map/all_to_all | solution.py:58
  133.9 33.5 %all_gather.20 = bf16[32,8192]{1,0:T(8,128)(2,1)S(1)} all-gather(bf16[32,512]{1,0:T(8,128)(2,1)S(1)} %slice_reduce_fusion.1), channel_id=1, replica_groups=mesh['aux'=16,'pair'=32] {'aux'}, dimensions={1}, use_global_device_ids=true | all-gather | bytes 557056 | tf_op jit(solution)/shard_map/all_gather | solution.py:63
  167.5 2.6 reduce-precision_convert_fusion.1
  170.1 1.0 convolution_bitcast_fusion
  172.2 25.5 %all-gather.2 = f32[32,224,32]{1,2,0:T(8,128)} all-gather(f32[1,224,32]{1,2,0:T(8,128)S(1)} %maximum_bitcast_fusion), channel_id=3, replica_groups=mesh['aux'=16,'pair'=32] {'pair'}, dimensions={0}, use_global_device_ids=true | all-gather | bytes 946176 | tf_op jit(solution)/shard_map/all_gather | solution.py:46
  197.7 1.3 reduce_sum.63
  199.7 4.9 %shard_map.68 = f32[32,32]{1,0:T(8,128)} custom-call(f32[32,32]{1,0:T(8,128)} %copy.33.gram_ref), custom_call_target="tpu_custom_call" | custom-call | tf_op jit(solution)/shard_map/pallas_call | solution.py:90
  204.6 0.9 fusion.49
  206.4 0.9 pad_maximum_fusion.4
  207.4 5.1 %all-to-all-start.1 = ((bf16[32,16,576]{2,0,1:T(8,128)(2,1)}), bf16[32,16,576]{2,0,1:T(8,128)(2,1)S(1)}, u32[]{:S(2)}, u32[]{:S(2)}) async-start(bf16[32,16,576]{2,0,1:T(8,128)(2,1)} %pad_maximum_fusion.4), calls=%async_computation.1 | async-start | bytes 1310720 | tf_op jit(solution)/shard_map/all_to_all | solution.py:58
  212.5 1.4 reduce-precision_convert_fusion
  214.1 33.1 %all-to-all-done.1 = bf16[32,16,576]{2,0,1:T(8,128)(2,1)S(1)} async-done(((bf16[32,16,576]{2,0,1:T(8,128)(2,1)}), bf16[32,16,576]{2,0,1:T(8,128)(2,1)S(1)}, u32[]{:S(2)}, u32[]{:S(2)}) %all-to-all-start.1) | async-done | bytes 589856 | tf_op jit(solution)/shard_map/all_to_all | solution.py:58
  247.4 33.6 %all_gather.23 = bf16[32,8192]{1,0:T(8,128)(2,1)S(1)} all-gather(bf16[32,512]{1,0:T(8,128)(2,1)S(1)} %slice_reduce_fusion), channel_id=1, replica_groups=mesh['aux'=16,'pair'=32] {'aux'}, dimensions={1}, use_global_device_ids=true | all-gather | bytes 557056 | tf_op jit(solution)/shard_map/all_gather | solution.py:63
  281.8 3.2 %fusion.97 = (bf16[32,8192]{1,0:T(8,128)(2,1)}, f32[32,8192]{1,0:T(8,128)}) fusion(f32[32,8192]{1,0:T(8,128)S(1)} %get-tuple-element.35, f32[8192]{0:T(1024)S(1)} %bitcast.45, bf16[32,8192]{1,0:T(8,128)(2,1)} %get-tuple-element.8, bf16[32,8192]{1,0:T(8,128)(2,1)} %get-tuple-element.7, bf16[32,32]{1,0:T(8,128)(2,1)S(1)} %get-tuple-element.23, ...), kind=kOutput, calls=%fused_computation.155 | convolution fusion | flops 56903680 | bytes 4231168 | tf_op jit(solution)/shard_map/dot_general | solution.py:38
  (50 shorter events, 7.0 us)
Async XLA Ops:
  7.2 4.0 %copy-start = (bf16[160,8192]{1,0:T(8,128)(2,1)S(1)}, bf16[160,8192]{1,0:T(8,128)(2,1)}, u32[]{:S(2)}) copy-start(bf16[160,8192]{1,0:T(8,128)(2,1)} %param.4) | copy-start | bytes 7864324
  7.2 69.8 %all-gather.5.cloned.1.call-start = ((), (), s32[]{:S(2)}) async-start(), calls=%async_computation.2 | async-start | bytes 1081344 | tf_op jit(solution)/shard_map/all_gather | solution.py:46
  85.9 13.6 %copy-start.2 = (f32[32,32]{1,0:T(8,128)S(1)}, f32[32,32]{1,0:T(8,128)}, u32[]{:S(2)}) copy-start(f32[32,32]{1,0:T(8,128)} %shard_map.67) | copy-start | bytes 12292
  87.0 46.7 %all-to-all-start = ((bf16[32,16,576]{2,0,1:T(8,128)(2,1)}), bf16[32,16,576]{2,0,1:T(8,128)(2,1)S(1)}, u32[]{:S(2)}, u32[]{:S(2)}) async-start(bf16[32,16,576]{2,0,1:T(8,128)(2,1)} %pad_maximum_fusion.3), calls=%async_computation | async-start | bytes 1310720 | tf_op jit(solution)/shard_map/all_to_all | solution.py:58
  170.1 1.7 copy-start.3
  206.3 6.2 %copy-start.1 = (f32[32,32]{1,0:T(8,128)S(1)}, f32[32,32]{1,0:T(8,128)}, u32[]{:S(2)}) copy-start(f32[32,32]{1,0:T(8,128)} %shard_map.68) | copy-start | bytes 12292
  206.3 6.2 %copy-start.4 = (bf16[32,8192]{1,0:T(8,128)(2,1)S(1)}, bf16[32,8192]{1,0:T(8,128)(2,1)}, u32[]{:S(2)}) copy-start(bf16[32,8192]{1,0:T(8,128)(2,1)} %copy-done.3) | copy-start | bytes 1572868
  207.4 39.8 %all-to-all-start.1 = ((bf16[32,16,576]{2,0,1:T(8,128)(2,1)}), bf16[32,16,576]{2,0,1:T(8,128)(2,1)S(1)}, u32[]{:S(2)}, u32[]{:S(2)}) async-start(bf16[32,16,576]{2,0,1:T(8,128)(2,1)} %pad_maximum_fusion.4), calls=%async_computation.1 | async-start | bytes 1310720 | tf_op jit(solution)/shard_map/all_to_all | solution.py:58
Sparse Core Ops, SparseCore 0:
  14.5 62.4 all-gather.4
